TPU v7x, 256 devices: a whole 4x4x8 slice. The times are simulated.
256 devices in a mesh: dp: 8 (over z), ctx: 32 (over y, x, core).
Axes of the slice: x: 4, y: 4, z: 8, core: 2. Of those that a mesh axis runs over, the one named last changes fastest.
Arguments:
- queries: bfloat16 [32768, 4096], P(('dp', 'ctx')), parts along dimension 0, may hold values from -0.6640625 to 0.6640625
- key_vectors: bfloat16 [32768, 4096], P(('dp', 'ctx')), parts along dimension 0, may hold values from -0.6640625 to 0.6640625
- values: bfloat16 [32768, 4096], P(('dp', 'ctx')), parts along dimension 0, may hold values from -0.6640625 to 0.6640625
- out_grad: bfloat16 [32768, 4096], P(('dp', 'ctx')), parts along dimension 0, may hold values from -0.6640625 to 0.6640625
- log_decay: bfloat16 [32768, 32], P(('dp', 'ctx')), parts along dimension 0, may hold values from -2.2 to 0
Outputs:
- attended: bfloat16 [32768, 4096], P(('dp', 'ctx')), parts along dimension 0
- query_grad: bfloat16 [32768, 4096], P(('dp', 'ctx')), parts along dimension 0
- key_grad: bfloat16 [32768, 4096], P(('dp', 'ctx')), parts along dimension 0
- value_grad: bfloat16 [32768, 4096], P(('dp', 'ctx')), parts along dimension 0
There are 8 independent parts, one for each index of `dp`. A program takes and returns all parts, laid end to end along the dimension named above; each array names one. Nothing has to cross between parts.
All inputs are finite; a program needn't handle non-finite values.
Results may differ from a plain program's by a relative error of at most 0.001.
Values may be sent and summed in bfloat16 or wider, within the bound.
No kernel may reach another device: no remote copies, remote signals or barrier semaphores. Data moves between devices by JAX's collectives and lax.ppermute only.
A program may use at most 320 MiB of HBM per device.

v0:
```python
import jax
import jax.numpy as jnp
from jax import lax
from jax.sharding import PartitionSpec as P
from jax.experimental import pallas as pl
from jax.experimental.pallas import tpu as pltpu

SPAN = 64


def combine(earlier, latter):
    return (earlier[0] + latter[0], jnp.exp(latter[0])[..., None, None] * earlier[1] + latter[1])


def prepare(queries, key_vectors, values, out_grad, log_decay):
    highest = lax.Precision.HIGHEST
    length = queries.shape[0]
    heads = log_decay.shape[1]
    q_rows = queries.reshape(length, heads, -1).astype(jnp.float32)
    k_rows = key_vectors.reshape(length, heads, -1).astype(jnp.float32)
    v_rows = values.reshape(length, heads, -1).astype(jnp.float32)
    g_rows = out_grad.reshape(length, heads, -1).astype(jnp.float32)
    cumul = jnp.cumsum(log_decay.astype(jnp.float32), axis=0)
    total = cumul[-1]
    query_decay = jnp.exp(cumul)
    key_decay = jnp.exp(total[None, :] - cumul)
    state = jnp.einsum("she,shf->hef", k_rows * key_decay[..., None], v_rows, precision=highest)
    grad_state = jnp.einsum("the,thf->hef", q_rows * query_decay[..., None], g_rows, precision=highest)
    cumul_heads = jnp.transpose(cumul)
    pieces = (cumul_heads[:, None, :], cumul_heads[:, :, None], jnp.transpose(query_decay)[:, :, None],
              jnp.transpose(key_decay)[:, :, None])
    return total, state, grad_state, pieces


def head_kernel(q_ref, k_ref, v_ref, g_ref, row_ref, col_ref, qd_ref, kd_ref, s_ref, gs_ref,
                att_ref, qg_ref, kg_ref, vg_ref):
    highest = lax.Precision.HIGHEST
    f32 = jnp.float32
    q = q_ref[...].astype(f32)
    k = k_ref[...].astype(f32)
    v = v_ref[...].astype(f32)
    g = g_ref[...].astype(f32)
    size = q.shape[0]
    later = lax.broadcasted_iota(jnp.int32, (size, size), 0) >= lax.broadcasted_iota(jnp.int32, (size, size), 1)
    spread = col_ref[0] - row_ref[0]
    weights = jnp.where(later, jnp.exp(jnp.where(later, spread, 0.0)), 0.0)
    nt = (((1,), (1,)), ((), ()))
    scores = lax.dot_general(q, k, nt, precision=highest, preferred_element_type=f32) * weights
    grad_scores = lax.dot_general(g, v, nt, precision=highest, preferred_element_type=f32) * weights
    qd = qd_ref[0]
    kd = kd_ref[0]
    state = s_ref[0]
    grad_in = gs_ref[0]
    dot = lambda a, b: jnp.dot(a, b, precision=highest, preferred_element_type=f32)
    att_ref[...] = (dot(scores, v) + dot(q * qd, state)).astype(att_ref.dtype)
    qg_ref[...] = (dot(grad_scores, k) + lax.dot_general(g * qd, state, nt, precision=highest,
                                                         preferred_element_type=f32)).astype(qg_ref.dtype)
    kg_ref[...] = (dot(grad_scores.T, q) + lax.dot_general(v * kd, grad_in, nt, precision=highest,
                                                           preferred_element_type=f32)).astype(kg_ref.dtype)
    vg_ref[...] = (dot(scores.T, g) + dot(k * kd, grad_in)).astype(vg_ref.dtype)


def finish(inputs, pieces, state_in, grad_in):
    queries = inputs[0]
    length, width = queries.shape
    heads = state_in.shape[0]
    dk = width // heads
    rows, cols, qd, kd = pieces
    tile = pl.BlockSpec((length, dk), lambda h: (0, h))
    per_head = lambda a: pl.BlockSpec((1,) + a.shape[1:], lambda h: (h, 0, 0))
    out = jax.ShapeDtypeStruct((length, width), jnp.bfloat16)
    return pl.pallas_call(
        head_kernel,
        grid=(heads,),
        in_specs=[tile] * 4 + [per_head(a) for a in (rows, cols, qd, kd, state_in, grad_in)],
        out_specs=[tile] * 4,
        out_shape=[out] * 4,
        compiler_params=pltpu.CompilerParams(dimension_semantics=("arbitrary",)),
    )(*inputs, rows, cols, qd, kd, state_in, grad_in)


def gather_rows(row, axis):
    count = lax.axis_size(axis)
    me = lax.axis_index(axis)
    known = row[None]
    step = 1
    while step < count:
        pairs = [(i, (i + step) % count) for i in range(count)]
        known = jnp.concatenate([known, lax.ppermute(known, axis, pairs)], 0)
        step *= 2
    return known[(me - jnp.arange(count)) % count]


def window_sum(ordered, place, first, last):
    total = jnp.zeros_like(ordered[0])
    for back in range(first, last + 1):
        index = place - back
        picked = lax.dynamic_index_in_dim(ordered, jnp.maximum(index, 0), 0, False)
        total = total + jnp.where(index >= 0, picked, jnp.zeros_like(picked))
    return total


def chip_scan(chip_totals, state, axis, chip, chips, reverse, steps):
    direction = -1 if reverse else 1
    ordered = chip_totals[::-1] if reverse else chip_totals
    place = chips - 1 - chip if reverse else chip
    sent = state
    carried = jnp.zeros_like(state)
    for count, step in enumerate(steps):
        pairs = []
        for c in range(chips):
            target = c + direction * step
            if 0 <= target < chips:
                for core in range(2):
                    pairs.append((2 * c + core, 2 * target + core))
        received = lax.ppermute(sent, axis, pairs)
        to_start = jnp.exp(window_sum(ordered, place, 1, step - 1))[:, None, None]
        carried = carried + to_start * received
        if count + 1 < len(steps):
            to_end = jnp.exp(window_sum(ordered, place, 0, step - 1))[:, None, None]
            sent = sent + to_end * received
    return carried


def shards(queries, key_vectors, values, out_grad, log_decay):
    axis = "ctx"
    total, state, grad_state, pieces = prepare(queries, key_vectors, values, out_grad, log_decay)
    heads = total.shape[0]
    half = heads // 2
    chips = lax.axis_size(axis) // 2
    core = lax.axis_index(axis) % 2
    partner = [(2 * c + k, 2 * c + 1 - k) for c in range(chips) for k in range(2)]

    def other_half(a):
        return lax.dynamic_slice_in_dim(a, (1 - core) * half, half, 0)

    def own_half(a):
        return lax.dynamic_slice_in_dim(a, core * half, half, 0)

    sent = (total, other_half(state), other_half(grad_state))
    other_total, other_state, other_grad = lax.ppermute(sent, axis, partner)
    first = core == 0
    mine_state = own_half(state)
    mine_grad = own_half(grad_state)
    own_total_half = own_half(total)
    other_total_half = own_half(other_total)
    one = jnp.ones_like(own_total_half)
    fwd_a = jnp.where(first, jnp.exp(other_total_half), one)[:, None, None]
    fwd_b = jnp.where(first, one, jnp.exp(own_total_half))[:, None, None]
    chip_state = fwd_a * mine_state + fwd_b * other_state
    bwd_a = jnp.where(first, one, jnp.exp(other_total_half))[:, None, None]
    bwd_b = jnp.where(first, jnp.exp(own_total_half), one)[:, None, None]
    chip_grad = bwd_a * mine_grad + bwd_b * other_grad
    every_total = gather_rows(total, axis)
    chip_totals = every_total[0::2] + every_total[1::2]
    chip = lax.axis_index(axis) // 2
    steps = []
    step = 1
    while step < chips:
        steps.append(step)
        step *= 2
    turn = len(steps) // 2
    orders = (steps, steps[turn:] + steps[:turn])
    group = half // 2
    scans = []
    for chip_sum, reverse in ((chip_state, False), (chip_grad, True)):
        parts = []
        for g, order in enumerate(orders):
            group_totals = lax.dynamic_slice_in_dim(chip_totals, core * half + g * group, group, 1)
            parts.append(
                chip_scan(group_totals, chip_sum[g * group:(g + 1) * group], axis, chip, chips, reverse, order)
            )
        scans.append(jnp.concatenate(parts, 0))
    before, after = scans
    total_c0 = jnp.where(first, own_total_half, other_total_half)
    total_c1 = jnp.where(first, other_total_half, own_total_half)
    state_c0 = jnp.where(first, mine_state, other_state)
    grad_c1 = jnp.where(first, other_grad, mine_grad)
    fwd_core0 = before
    fwd_core1 = jnp.exp(total_c0)[:, None, None] * before + state_c0
    bwd_core0 = jnp.exp(total_c1)[:, None, None] * after + grad_c1
    bwd_core1 = after
    keep_fwd = jnp.where(first, fwd_core0, fwd_core1)
    keep_bwd = jnp.where(first, bwd_core0, bwd_core1)
    give_fwd = jnp.where(first, fwd_core1, fwd_core0)
    give_bwd = jnp.where(first, bwd_core1, bwd_core0)
    got_fwd, got_bwd = lax.ppermute((give_fwd, give_bwd), axis, partner)

    def assemble(keep, got):
        return jnp.where(first, jnp.concatenate([keep, got], 0), jnp.concatenate([got, keep], 0))

    inputs = (queries, key_vectors, values, out_grad)
    return tuple(finish(inputs, pieces, assemble(keep_fwd, got_fwd), assemble(keep_bwd, got_bwd)))


def solution(mesh):
    return jax.shard_map(
        shards,
        mesh=mesh,
        in_specs=(
            P(("dp", "ctx"), None),
            P(("dp", "ctx"), None),
            P(("dp", "ctx"), None),
            P(("dp", "ctx"), None),
            P(("dp", "ctx"), None),
        ),
        out_specs=(
            P(("dp", "ctx"), None),
            P(("dp", "ctx"), None),
            P(("dp", "ctx"), None),
            P(("dp", "ctx"), None),
        ),
        check_vma=False,
    )
```

profile of v0, /device:TPU:1, one launch (start us, length us, event | category | flops | bytes accessed | tf_op | source)
XLA Modules:
  0.0 204.1 jit_solution(801476941017047303)
XLA Ops:
  0.6 0.9 copy.42
  1.7 2.7 %collective-permute-start.3 = (f32[1,32]{1,0:T(1,128)S(1)}, f32[1,32]{1,0:T(1,128)S(1)}, u32[]{:S(2)}, u32[]{:S(2)}) collective-permute-start(f32[1,32]{1,0:T(1,128)S(1)} %get-tuple-element.54), channel_id=1, source_target_pairs={{0,1},{1,2},{2,3},{3,4},{4,5},{5,6},{6,7},{7,8},{8,9},{9,10},{10,1... | collective-permute-start | bytes 392 | tf_op jit(solution)/shard_map/ppermute | solution.py:89
  4.4 0.7 collective-permute-start
  5.2 2.6 %copy.54 = f32[128,4096]{0,1:T(8,128)} copy(bf16[128,4096]{1,0:T(8,128)(2,1)} %q_ref.1) | data formatting | bytes 3145728 | tf_op jit(solution)/shard_map/convert_element_type | solution.py:19
  7.8 2.8 %fusion = f32[32,128,128]{2,1,0:T(8,128)S(1)} fusion(f32[128,32,128]{0,2,1:T(8,128)} %bitcast.184, f32[128,32]{0,1:T(8,128)S(1)} %copy.47, bf16[128,4096]{1,0:T(8,128)(2,1)S(1)} %copy-done.3), kind=kOutput, calls=%fused_computation.3 | convolution fusion | flops 805830656 | bytes 5259264 | tf_op jit(solution)/shard_map/the,thf->hef/dot_general | solution.py:28
  10.6 1.1 constant_dynamic-slice_fusion.18
  11.8 0.8 copy-done.2
  12.6 1.6 copy.53
  14.2 3.0 %fusion.2 = f32[32,128,128]{2,1,0:T(8,128)S(1)} fusion(f32[128,32,128]{0,2,1:T(8,128)} %bitcast.185, f32[128,32]{0,1:T(8,128)S(1)} %copy.44, bf16[128,4096]{1,0:T(8,128)(2,1)} %v_ref.1), kind=kOutput, calls=%fused_computation.5 | convolution fusion | flops 805830656 | bytes 5259264 | tf_op jit(solution)/shard_map/she,shf->hef/dot_general | solution.py:27
  17.3 1.1 constant_dynamic-slice_fusion.19
  18.5 1.0 collective-permute-start.4
  19.6 5.1 %collective-permute-done.4 = f32[2,32]{1,0:T(2,128)S(1)} collective-permute-done((f32[2,32]{1,0:T(2,128)S(1)}, f32[2,32]{1,0:T(2,128)S(1)}, u32[]{:S(2)}, u32[]{:S(2)}) %collective-permute-start.4) | collective-permute-done | bytes 288 | tf_op jit(solution)/shard_map/ppermute | solution.py:89
  24.8 6.0 %collective-permute-done.5 = f32[4,32]{1,0:T(4,128)S(1)} collective-permute-done((f32[4,32]{1,0:T(4,128)S(1)}, f32[4,32]{1,0:T(4,128)S(1)}, u32[]{:S(2)}, u32[]{:S(2)}) %collective-permute-start.5) | collective-permute-done | bytes 544 | tf_op jit(solution)/shard_map/ppermute | solution.py:89
  31.0 3.6 %collective-permute-done.6 = f32[8,32]{1,0:T(8,128)S(1)} collective-permute-done((f32[8,32]{1,0:T(8,128)S(1)}, f32[8,32]{1,0:T(8,128)S(1)}, u32[]{:S(2)}, u32[]{:S(2)}) %collective-permute-start.6) | collective-permute-done | bytes 1056 | tf_op jit(solution)/shard_map/ppermute | solution.py:89
  34.7 4.0 %collective-permute-done.7 = f32[16,32]{1,0:T(8,128)S(1)} collective-permute-done((f32[16,32]{1,0:T(8,128)S(1)}, f32[16,32]{1,0:T(8,128)S(1)}, u32[]{:S(2)}, u32[]{:S(2)}) %collective-permute-start.7) | collective-permute-done | bytes 2080 | tf_op jit(solution)/shard_map/ppermute | solution.py:89
  39.7 1.7 multiply_add_fusion
  41.5 1.3 collective-permute-start.17
  42.8 1.3 collective-permute-start.21
  45.1 4.0 %collective-permute-start.11 = (f32[8,128,128]{2,1,0:T(8,128)S(1)}, f32[8,128,128]{2,1,0:T(8,128)S(1)}, u32[]{:S(2)}, u32[]{:S(2)}) collective-permute-start(f32[8,128,128]{2,1,0:T(8,128)S(1)} %get-tuple-element.51), channel_id=1, source_target_pairs={{0,8},{1,9},{2,10},{3,11},{4,12},{5,13},{6,14},{7,15},{8,16},{9,17... | collective-permute-start | bytes 1572872 | tf_op jit(solution)/shard_map/ppermute | solution.py:116
  49.1 4.0 %collective-permute-start.2 = (f32[8,128,128]{2,1,0:T(8,128)S(1)}, f32[8,128,128]{2,1,0:T(8,128)S(1)}, u32[]{:S(2)}, u32[]{:S(2)}) collective-permute-start(f32[8,128,128]{2,1,0:T(8,128)S(1)} %get-tuple-element.50), channel_id=1, source_target_pairs={{0,2},{1,3},{2,4},{3,5},{4,6},{5,7},{6,8},{7,9},{8,10},{9,11},{10,... | collective-permute-start | bytes 1572872 | tf_op jit(solution)/shard_map/ppermute | solution.py:116
  53.5 1.3 collective-permute-start.18
  55.0 1.3 collective-permute-start.22
  56.3 7.8 %collective-permute-done.11 = f32[8,128,128]{2,1,0:T(8,128)S(1)} collective-permute-done((f32[8,128,128]{2,1,0:T(8,128)S(1)}, f32[8,128,128]{2,1,0:T(8,128)S(1)}, u32[]{:S(2)}, u32[]{:S(2)}) %collective-permute-start.11) | collective-permute-done | bytes 524320 | tf_op jit(solution)/shard_map/ppermute | solution.py:116
  64.3 1.3 collective-permute-start.8
  65.6 5.7 %collective-permute-start.12 = (f32[8,128,128]{2,1,0:T(8,128)S(1)}, f32[8,128,128]{2,1,0:T(8,128)S(1)}, u32[]{:S(2)}, u32[]{:S(2)}) collective-permute-start(f32[8,128,128]{2,1,0:T(8,128)S(1)} %get-tuple-element.49), channel_id=1, source_target_pairs={{0,16},{1,17},{2,18},{3,19},{4,20},{5,21},{6,22},{7,23},{8,24},{9,... | collective-permute-start | bytes 1572872 | tf_op jit(solution)/shard_map/ppermute | solution.py:116
  71.4 1.3 collective-permute-start.19
  72.7 14.0 %collective-permute-done.22 = f32[8,128,128]{2,1,0:T(8,128)S(1)} collective-permute-done((f32[8,128,128]{2,1,0:T(8,128)S(1)}, f32[8,128,128]{2,1,0:T(8,128)S(1)}, u32[]{:S(2)}, u32[]{:S(2)}) %collective-permute-start.22) | collective-permute-done | bytes 524320 | tf_op jit(solution)/shard_map/ppermute | solution.py:116
  86.9 1.3 collective-permute-start.23
  88.3 4.1 %collective-permute-start.9 = (f32[8,128,128]{2,1,0:T(8,128)S(1)}, f32[8,128,128]{2,1,0:T(8,128)S(1)}, u32[]{:S(2)}, u32[]{:S(2)}) collective-permute-start(f32[8,128,128]{2,1,0:T(8,128)S(1)} %multiply_add_fusion.16), channel_id=1, source_target_pairs={{0,8},{1,9},{2,10},{3,11},{4,12},{5,13},{6,14},{7,15},{8,16},{9,17... | collective-permute-start | bytes 1572872 | tf_op jit(solution)/shard_map/ppermute | solution.py:116
  92.6 10.7 %collective-permute-start.13 = (f32[8,128,128]{2,1,0:T(8,128)S(1)}, f32[8,128,128]{2,1,0:T(8,128)S(1)}, u32[]{:S(2)}, u32[]{:S(2)}) collective-permute-start(f32[8,128,128]{2,1,0:T(8,128)S(1)} %multiply_add_fusion.12), channel_id=1, source_target_pairs={{0,2},{1,3},{2,4},{3,5},{4,6},{5,7},{6,8},{7,9},{8,10},{9,11},{10,... | collective-permute-start | bytes 1572872 | tf_op jit(solution)/shard_map/ppermute | solution.py:116
  103.4 1.3 collective-permute-start.20
  104.7 1.4 collective-permute-done.23
  106.2 1.5 collective-permute-start.24
  107.8 23.9 %collective-permute-start.10 = (f32[8,128,128]{2,1,0:T(8,128)S(1)}, f32[8,128,128]{2,1,0:T(8,128)S(1)}, u32[]{:S(2)}, u32[]{:S(2)}) collective-permute-start(f32[8,128,128]{2,1,0:T(8,128)S(1)} %multiply_add_fusion.15), channel_id=1, source_target_pairs={{0,16},{1,17},{2,18},{3,19},{4,20},{5,21},{6,22},{7,23},{8,24},{9,... | collective-permute-start | bytes 1572872 | tf_op jit(solution)/shard_map/ppermute | solution.py:116
  131.8 1.3 collective-permute-start.14
  133.2 16.4 %collective-permute-done.20 = f32[8,128,128]{2,1,0:T(8,128)S(1)} collective-permute-done((f32[8,128,128]{2,1,0:T(8,128)S(1)}, f32[8,128,128]{2,1,0:T(8,128)S(1)}, u32[]{:S(2)}, u32[]{:S(2)}) %collective-permute-start.20) | collective-permute-done | bytes 524320 | tf_op jit(solution)/shard_map/ppermute | solution.py:116
  150.0 1.1 copy-done.1
  151.1 1.3 fusion.13
  152.4 1.7 collective-permute-start.25
  154.6 0.8 copy-done.6
  155.4 1.7 fusion.11
  157.0 1.4 collective-permute-start.15
  158.6 2.0 copy.51.qd_ref
  160.6 2.0 copy.52.kd_ref
  162.6 2.0 copy.50.col_ref
  164.6 3.3 %maximum_select_fusion.1.gs_ref = f32[32,128,128]{2,1,0:T(8,128)} fusion(f32[16,128,128]{2,1,0:T(8,128)} %collective-permute-done.25, f32[16,128,128]{2,1,0:T(8,128)S(1)} %get-tuple-element.40, pred[]{:T(512)S(6)} %eq.7), kind=kLoop, calls=%fused_computation.2 | loop fusion | flops 1572864 | bytes 4194305 | tf_op jit(solution)/shard_map/jit(_where)/select_n | solution.py:190
  167.9 1.6 maximum_select_fusion.s_ref
  169.5 34.5 %shard_map.84 = (bf16[128,4096]{1,0:T(8,128)(2,1)}, bf16[128,4096]{1,0:T(8,128)(2,1)}, bf16[128,4096]{1,0:T(8,128)(2,1)}, bf16[128,4096]{1,0:T(8,128)(2,1)}) custom-call(bf16[128,4096]{1,0:T(8,128)(2,1)} %q_ref.1, bf16[128,4096]{1,0:T(8,128)(2,1)} %k_ref.1, bf16[128,4096]{1,0:T(8,128)(2,1)} %v_ref.1, bf16[128,4096]{1,0:T(8,128)(2,1)} %g_ref.1, ...), custom_call_target="tpu_custom_call" | custom-call | tf_op jit(solution)/shard_map/pallas_call | solution.py:72
  (87 shorter events, 5.6 us)
Async XLA Ops:
  0.6 7.2 %copy-start.3 = (bf16[128,4096]{1,0:T(8,128)(2,1)S(1)}, bf16[128,4096]{1,0:T(8,128)(2,1)}, u32[]{:S(2)}) copy-start(bf16[128,4096]{1,0:T(8,128)(2,1)} %g_ref.1) | copy-start | bytes 3145732
  1.7 16.8 %collective-permute-start.3 = (f32[1,32]{1,0:T(1,128)S(1)}, f32[1,32]{1,0:T(1,128)S(1)}, u32[]{:S(2)}, u32[]{:S(2)}) collective-permute-start(f32[1,32]{1,0:T(1,128)S(1)} %get-tuple-element.54), channel_id=1, source_target_pairs={{0,1},{1,2},{2,3},{3,4},{4,5},{5,6},{6,7},{7,8},{8,9},{9,10},{10,1... | collective-permute-start | bytes 392 | tf_op jit(solution)/shard_map/ppermute | solution.py:89
  4.4 26.5 %collective-permute-start = (f32[32]{0:T(128)S(1)}, f32[32]{0:T(128)S(1)}, u32[]{:S(2)}, u32[]{:S(2)}) collective-permute-start(f32[32]{0:T(128)S(1)} %get-tuple-element.55), channel_id=1, source_target_pairs={{0,1},{1,0},{2,3},{3,2},{4,5},{5,4},{6,7},{7,6},{8,9},{9,8},{10,11... | collective-permute-start | bytes 392 | tf_op jit(solution)/shard_map/ppermute | solution.py:141
  10.6 3.6 %copy-start = (f32[32,128,128]{2,1,0:T(8,128)}, f32[32,128,128]{2,1,0:T(8,128)S(1)}, u32[]{:S(2)}) copy-start(f32[32,128,128]{2,1,0:T(8,128)S(1)} %fusion) | copy-start | bytes 6291460
  10.6 2.0 copy-start.2
  11.7 28.0 %collective-permute-start.16 = (f32[16,128,128]{2,1,0:T(8,128)}, f32[16,128,128]{2,1,0:T(8,128)}, u32[]{:S(2)}, u32[]{:S(2)}) collective-permute-start(f32[16,128,128]{2,1,0:T(8,128)} %constant_dynamic-slice_fusion.18), channel_id=1, source_target_pairs={{0,1},{1,0},{2,3},{3,2},{4,5},{5,4},{6,7},{7,6},{8,9},{9,8},{10,11... | collective-permute-start | bytes 3145736 | tf_op jit(solution)/shard_map/ppermute | solution.py:141
  18.3 25.8 %collective-permute-start.1 = (f32[16,128,128]{2,1,0:T(8,128)}, f32[16,128,128]{2,1,0:T(8,128)S(1)}, u32[]{:S(2)}, u32[]{:S(2)}) collective-permute-start(f32[16,128,128]{2,1,0:T(8,128)} %constant_dynamic-slice_fusion.19), channel_id=1, source_target_pairs={{0,1},{1,0},{2,3},{3,2},{4,5},{5,4},{6,7},{7,6},{8,9},{9,8},{10,11... | collective-permute-start | bytes 3145736 | tf_op jit(solution)/shard_map/ppermute | solution.py:141
  18.5 6.1 %collective-permute-start.4 = (f32[2,32]{1,0:T(2,128)S(1)}, f32[2,32]{1,0:T(2,128)S(1)}, u32[]{:S(2)}, u32[]{:S(2)}) collective-permute-start(f32[2,32]{1,0:T(2,128)S(1)} %pad_maximum_fusion.4), channel_id=1, source_target_pairs={{0,2},{1,3},{2,4},{3,5},{4,6},{5,7},{6,8},{7,9},{8,10},{9,11},{10,... | collective-permute-start | bytes 776 | tf_op jit(solution)/shard_map/ppermute | solution.py:89
  24.6 6.1 %collective-permute-start.5 = (f32[4,32]{1,0:T(4,128)S(1)}, f32[4,32]{1,0:T(4,128)S(1)}, u32[]{:S(2)}, u32[]{:S(2)}) collective-permute-start(f32[4,32]{1,0:T(4,128)S(1)} %pad_maximum_fusion.3), channel_id=1, source_target_pairs={{0,4},{1,5},{2,6},{3,7},{4,8},{5,9},{6,10},{7,11},{8,12},{9,13},{1... | collective-permute-start | bytes 1544 | tf_op jit(solution)/shard_map/ppermute | solution.py:89
  30.8 3.7 %collective-permute-start.6 = (f32[8,32]{1,0:T(8,128)S(1)}, f32[8,32]{1,0:T(8,128)S(1)}, u32[]{:S(2)}, u32[]{:S(2)}) collective-permute-start(f32[8,32]{1,0:T(8,128)S(1)} %pad_maximum_fusion.2), channel_id=1, source_target_pairs={{0,8},{1,9},{2,10},{3,11},{4,12},{5,13},{6,14},{7,15},{8,16},{9,17... | collective-permute-start | bytes 3080 | tf_op jit(solution)/shard_map/ppermute | solution.py:89
  34.6 4.1 %collective-permute-start.7 = (f32[16,32]{1,0:T(8,128)S(1)}, f32[16,32]{1,0:T(8,128)S(1)}, u32[]{:S(2)}, u32[]{:S(2)}) collective-permute-start(f32[16,32]{1,0:T(8,128)S(1)} %concatenate.40), channel_id=1, source_target_pairs={{0,16},{1,17},{2,18},{3,19},{4,20},{5,21},{6,22},{7,23},{8,24},{9,... | collective-permute-start | bytes 6152 | tf_op jit(solution)/shard_map/ppermute | solution.py:89
  41.5 11.6 %collective-permute-start.17 = (f32[8,128,128]{2,1,0:T(8,128)S(1)}, f32[8,128,128]{2,1,0:T(8,128)S(1)}, u32[]{:S(2)}, u32[]{:S(2)}) collective-permute-start(f32[8,128,128]{2,1,0:T(8,128)S(1)} %get-tuple-element.46), channel_id=1, source_target_pairs={{2,0},{3,1},{4,2},{5,3},{6,4},{7,5},{8,6},{9,7},{10,8},{11,9},{12,... | collective-permute-start | bytes 1572872 | tf_op jit(solution)/shard_map/ppermute | solution.py:116
  42.8 10.5 %collective-permute-start.21 = (f32[8,128,128]{2,1,0:T(8,128)S(1)}, f32[8,128,128]{2,1,0:T(8,128)S(1)}, u32[]{:S(2)}, u32[]{:S(2)}) collective-permute-start(f32[8,128,128]{2,1,0:T(8,128)S(1)} %get-tuple-element.47), channel_id=1, source_target_pairs={{8,0},{9,1},{10,2},{11,3},{12,4},{13,5},{14,6},{15,7},{16,8},{17,9... | collective-permute-start | bytes 1572872 | tf_op jit(solution)/shard_map/ppermute | solution.py:116
  44.1 1.0 copy-start.5
  45.1 18.9 %collective-permute-start.11 = (f32[8,128,128]{2,1,0:T(8,128)S(1)}, f32[8,128,128]{2,1,0:T(8,128)S(1)}, u32[]{:S(2)}, u32[]{:S(2)}) collective-permute-start(f32[8,128,128]{2,1,0:T(8,128)S(1)} %get-tuple-element.51), channel_id=1, source_target_pairs={{0,8},{1,9},{2,10},{3,11},{4,12},{5,13},{6,14},{7,15},{8,16},{9,17... | collective-permute-start | bytes 1572872 | tf_op jit(solution)/shard_map/ppermute | solution.py:116
  49.1 14.9 %collective-permute-start.2 = (f32[8,128,128]{2,1,0:T(8,128)S(1)}, f32[8,128,128]{2,1,0:T(8,128)S(1)}, u32[]{:S(2)}, u32[]{:S(2)}) collective-permute-start(f32[8,128,128]{2,1,0:T(8,128)S(1)} %get-tuple-element.50), channel_id=1, source_target_pairs={{0,2},{1,3},{2,4},{3,5},{4,6},{5,7},{6,8},{7,9},{8,10},{9,11},{10,... | collective-permute-start | bytes 1572872 | tf_op jit(solution)/shard_map/ppermute | solution.py:116
  53.5 17.8 %collective-permute-start.18 = (f32[8,128,128]{2,1,0:T(8,128)S(1)}, f32[8,128,128]{2,1,0:T(8,128)S(1)}, u32[]{:S(2)}, u32[]{:S(2)}) collective-permute-start(f32[8,128,128]{2,1,0:T(8,128)S(1)} %get-tuple-element.44), channel_id=1, source_target_pairs={{4,0},{5,1},{6,2},{7,3},{8,4},{9,5},{10,6},{11,7},{12,8},{13,9},{1... | collective-permute-start | bytes 1572872 | tf_op jit(solution)/shard_map/ppermute | solution.py:116
  55.0 31.8 %collective-permute-start.22 = (f32[8,128,128]{2,1,0:T(8,128)S(1)}, f32[8,128,128]{2,1,0:T(8,128)S(1)}, u32[]{:S(2)}, u32[]{:S(2)}) collective-permute-start(f32[8,128,128]{2,1,0:T(8,128)S(1)} %get-tuple-element.45), channel_id=1, source_target_pairs={{16,0},{17,1},{18,2},{19,3},{20,4},{21,5},{22,6},{23,7},{24,8},{25... | collective-permute-start | bytes 1572872 | tf_op jit(solution)/shard_map/ppermute | solution.py:116
  64.3 23.9 %collective-permute-start.8 = (f32[8,128,128]{2,1,0:T(8,128)S(1)}, f32[8,128,128]{2,1,0:T(8,128)S(1)}, u32[]{:S(2)}, u32[]{:S(2)}) collective-permute-start(f32[8,128,128]{2,1,0:T(8,128)S(1)} %get-tuple-element.48), channel_id=1, source_target_pairs={{0,4},{1,5},{2,6},{3,7},{4,8},{5,9},{6,10},{7,11},{8,12},{9,13},{1... | collective-permute-start | bytes 1572872 | tf_op jit(solution)/shard_map/ppermute | solution.py:116
  65.6 26.9 %collective-permute-start.12 = (f32[8,128,128]{2,1,0:T(8,128)S(1)}, f32[8,128,128]{2,1,0:T(8,128)S(1)}, u32[]{:S(2)}, u32[]{:S(2)}) collective-permute-start(f32[8,128,128]{2,1,0:T(8,128)S(1)} %get-tuple-element.49), channel_id=1, source_target_pairs={{0,16},{1,17},{2,18},{3,19},{4,20},{5,21},{6,22},{7,23},{8,24},{9,... | collective-permute-start | bytes 1572872 | tf_op jit(solution)/shard_map/ppermute | solution.py:116
  71.4 31.8 %collective-permute-start.19 = (f32[8,128,128]{2,1,0:T(8,128)S(1)}, f32[8,128,128]{2,1,0:T(8,128)S(1)}, u32[]{:S(2)}, u32[]{:S(2)}) collective-permute-start(f32[8,128,128]{2,1,0:T(8,128)S(1)} %multiply_add_fusion.8), channel_id=1, source_target_pairs={{8,0},{9,1},{10,2},{11,3},{12,4},{13,5},{14,6},{15,7},{16,8},{17,9... | collective-permute-start | bytes 1572872 | tf_op jit(solution)/shard_map/ppermute | solution.py:116
  86.9 19.2 %collective-permute-start.23 = (f32[8,128,128]{2,1,0:T(8,128)S(1)}, f32[8,128,128]{2,1,0:T(8,128)S(1)}, u32[]{:S(2)}, u32[]{:S(2)}) collective-permute-start(f32[8,128,128]{2,1,0:T(8,128)S(1)} %multiply_add_fusion.4), channel_id=1, source_target_pairs={{2,0},{3,1},{4,2},{5,3},{6,4},{7,5},{8,6},{9,7},{10,8},{11,9},{12,... | collective-permute-start | bytes 1572872 | tf_op jit(solution)/shard_map/ppermute | solution.py:116
  88.3 19.4 %collective-permute-start.9 = (f32[8,128,128]{2,1,0:T(8,128)S(1)}, f32[8,128,128]{2,1,0:T(8,128)S(1)}, u32[]{:S(2)}, u32[]{:S(2)}) collective-permute-start(f32[8,128,128]{2,1,0:T(8,128)S(1)} %multiply_add_fusion.16), channel_id=1, source_target_pairs={{0,8},{1,9},{2,10},{3,11},{4,12},{5,13},{6,14},{7,15},{8,16},{9,17... | collective-permute-start | bytes 1572872 | tf_op jit(solution)/shard_map/ppermute | solution.py:116
  92.6 39.1 %collective-permute-start.13 = (f32[8,128,128]{2,1,0:T(8,128)S(1)}, f32[8,128,128]{2,1,0:T(8,128)S(1)}, u32[]{:S(2)}, u32[]{:S(2)}) collective-permute-start(f32[8,128,128]{2,1,0:T(8,128)S(1)} %multiply_add_fusion.12), channel_id=1, source_target_pairs={{0,2},{1,3},{2,4},{3,5},{4,6},{5,7},{6,8},{7,9},{8,10},{9,11},{10,... | collective-permute-start | bytes 1572872 | tf_op jit(solution)/shard_map/ppermute | solution.py:116
  103.4 46.1 %collective-permute-start.20 = (f32[8,128,128]{2,1,0:T(8,128)S(1)}, f32[8,128,128]{2,1,0:T(8,128)S(1)}, u32[]{:S(2)}, u32[]{:S(2)}) collective-permute-start(f32[8,128,128]{2,1,0:T(8,128)S(1)} %multiply_add_fusion.7), channel_id=1, source_target_pairs={{16,0},{17,1},{18,2},{19,3},{20,4},{21,5},{22,6},{23,7},{24,8},{25... | collective-permute-start | bytes 1572872 | tf_op jit(solution)/shard_map/ppermute | solution.py:116
  106.2 43.6 %collective-permute-start.24 = (f32[8,128,128]{2,1,0:T(8,128)S(1)}, f32[8,128,128]{2,1,0:T(8,128)S(1)}, u32[]{:S(2)}, u32[]{:S(2)}) collective-permute-start(f32[8,128,128]{2,1,0:T(8,128)S(1)} %multiply_add_fusion.3), channel_id=1, source_target_pairs={{4,0},{5,1},{6,2},{7,3},{8,4},{9,5},{10,6},{11,7},{12,8},{13,9},{1... | collective-permute-start | bytes 1572872 | tf_op jit(solution)/shard_map/ppermute | solution.py:116
  107.8 46.3 %collective-permute-start.10 = (f32[8,128,128]{2,1,0:T(8,128)S(1)}, f32[8,128,128]{2,1,0:T(8,128)S(1)}, u32[]{:S(2)}, u32[]{:S(2)}) collective-permute-start(f32[8,128,128]{2,1,0:T(8,128)S(1)} %multiply_add_fusion.15), channel_id=1, source_target_pairs={{0,16},{1,17},{2,18},{3,19},{4,20},{5,21},{6,22},{7,23},{8,24},{9,... | collective-permute-start | bytes 1572872 | tf_op jit(solution)/shard_map/ppermute | solution.py:116
  131.8 22.5 %collective-permute-start.14 = (f32[8,128,128]{2,1,0:T(8,128)S(1)}, f32[8,128,128]{2,1,0:T(8,128)S(1)}, u32[]{:S(2)}, u32[]{:S(2)}) collective-permute-start(f32[8,128,128]{2,1,0:T(8,128)S(1)} %multiply_add_fusion.11), channel_id=1, source_target_pairs={{0,4},{1,5},{2,6},{3,7},{4,8},{5,9},{6,10},{7,11},{8,12},{9,13},{1... | collective-permute-start | bytes 1572872 | tf_op jit(solution)/shard_map/ppermute | solution.py:116
  149.5 1.6 copy-start.1
  152.4 12.1 %collective-permute-start.25 = (f32[16,128,128]{2,1,0:T(8,128)}, f32[16,128,128]{2,1,0:T(8,128)}, u32[]{:S(2)}, u32[]{:S(2)}) collective-permute-start(f32[16,128,128]{2,1,0:T(8,128)} %get-tuple-element.41), channel_id=1, source_target_pairs={{0,1},{1,0},{2,3},{3,2},{4,5},{5,4},{6,7},{7,6},{8,9},{9,8},{10,11... | collective-permute-start | bytes 3145736 | tf_op jit(solution)/shard_map/ppermute | solution.py:187
  154.2 1.2 copy-start.6
  157.0 10.9 %collective-permute-start.15 = (f32[16,128,128]{2,1,0:T(8,128)}, f32[16,128,128]{2,1,0:T(8,128)S(1)}, u32[]{:S(2)}, u32[]{:S(2)}) collective-permute-start(f32[16,128,128]{2,1,0:T(8,128)} %get-tuple-element.43), channel_id=1, source_target_pairs={{0,1},{1,0},{2,3},{3,2},{4,5},{5,4},{6,7},{7,6},{8,9},{9,8},{10,11... | collective-permute-start | bytes 3145736 | tf_op jit(solution)/shard_map/ppermute | solution.py:187
  158.5 4.1 %copy-start.7 = (f32[128,32]{0,1:T(8,128)}, f32[128,32]{0,1:T(8,128)S(1)}, u32[]{:S(2)}) copy-start(f32[128,32]{0,1:T(8,128)S(1)} %copy.43) | copy-start | bytes 49156
  164.6 3.3 %copy-start.4 = (f32[16,128,128]{2,1,0:T(8,128)S(1)}, f32[16,128,128]{2,1,0:T(8,128)}, u32[]{:S(2)}) copy-start(f32[16,128,128]{2,1,0:T(8,128)} %get-tuple-element.42) | copy-start | bytes 3145732
where the time goes:
time: 207 us; the launch traced here: 204 us
  starting transfers between devices  73.4 us (35%)
  waiting for transfers between devices  58.3 us (28%)
  Pallas kernels  34.5 us (17%)
  local copies, waits for them, and re-layouts  17.8 us (9%)
  other arithmetic  12.8 us (6%)
  matrix products  5.77 us (3%)
    ppermute x16, starting transfers between devices, chip_scan(): received = lax.ppermute(sent, axis, pairs)  65.6 us
    ppermute x16, waiting for transfers between devices, chip_scan(): received = lax.ppermute(sent, axis, pairs)  39.7 us
    pallas_call x1, Pallas kernels, finish(): pl.pallas_call(head_kernel, grid=(heads,), in_specs=[tile] * 4 + [per_hea...  34.5 us
    ppermute x5, waiting for transfers between devices, gather_rows(): known = jnp.concatenate([known, lax.ppermute(known, axis, pairs)], 0)  18.6 us
    select_n x2, other arithmetic, assemble(): jnp.where(first, jnp.concatenate([keep, got], 0), jnp.concatenate([got, k...  4.9 us
  transfers between devices with their start and end apart: 26, of which 9 were waited for; matrix products, arithmetic and copies ran while one was open for 15% of the time, Pallas kernels for 0%

commit v1 on v0

--- a/solution.py
+++ b/solution.py
@@ -26,57 +26,78 @@
     key_decay = jnp.exp(total[None, :] - cumul)
     state = jnp.einsum("she,shf->hef", k_rows * key_decay[..., None], v_rows, precision=highest)
     grad_state = jnp.einsum("the,thf->hef", q_rows * query_decay[..., None], g_rows, precision=highest)
-    cumul_heads = jnp.transpose(cumul)
-    pieces = (cumul_heads[:, None, :], cumul_heads[:, :, None], jnp.transpose(query_decay)[:, :, None],
-              jnp.transpose(key_decay)[:, :, None])
+    pieces = jnp.transpose(cumul)
+    total = jnp.sum(log_decay.astype(jnp.float32), axis=0)
     return total, state, grad_state, pieces
 
 
-def head_kernel(q_ref, k_ref, v_ref, g_ref, row_ref, col_ref, qd_ref, kd_ref, s_ref, gs_ref,
-                att_ref, qg_ref, kg_ref, vg_ref):
-    highest = lax.Precision.HIGHEST
+def split(x):
+    high = x.astype(jnp.bfloat16)
+    return high, (x - high.astype(jnp.float32)).astype(jnp.bfloat16)
+
+
+def head_kernel(q_ref, k_ref, v_ref, g_ref, cum_ref, s_ref, gs_ref, att_ref, qg_ref, kg_ref, vg_ref):
     f32 = jnp.float32
-    q = q_ref[...].astype(f32)
-    k = k_ref[...].astype(f32)
-    v = v_ref[...].astype(f32)
-    g = g_ref[...].astype(f32)
-    size = q.shape[0]
+    nn = (((1,), (0,)), ((), ()))
+    nt = (((1,), (1,)), ((), ()))
+
+    def mm(a, b, dims):
+        return lax.dot_general(a, b, dims, preferred_element_type=f32)
+
+    def mm_right(a, b, dims):
+        high, low = split(b)
+        return mm(a, high, dims) + mm(a, low, dims)
+
+    def mm_left(a, b, dims):
+        high, low = split(a)
+        return mm(high, b, dims) + mm(low, b, dims)
+
+    size = q_ref.shape[0]
+    block = cum_ref.shape[0]
+    dk = q_ref.shape[1] // block
     later = lax.broadcasted_iota(jnp.int32, (size, size), 0) >= lax.broadcasted_iota(jnp.int32, (size, size), 1)
-    spread = col_ref[0] - row_ref[0]
-    weights = jnp.where(later, jnp.exp(jnp.where(later, spread, 0.0)), 0.0)
-    nt = (((1,), (1,)), ((), ()))
-    scores = lax.dot_general(q, k, nt, precision=highest, preferred_element_type=f32) * weights
-    grad_scores = lax.dot_general(g, v, nt, precision=highest, preferred_element_type=f32) * weights
-    qd = qd_ref[0]
-    kd = kd_ref[0]
-    state = s_ref[0]
-    grad_in = gs_ref[0]
-    dot = lambda a, b: jnp.dot(a, b, precision=highest, preferred_element_type=f32)
-    att_ref[...] = (dot(scores, v) + dot(q * qd, state)).astype(att_ref.dtype)
-    qg_ref[...] = (dot(grad_scores, k) + lax.dot_general(g * qd, state, nt, precision=highest,
-                                                         preferred_element_type=f32)).astype(qg_ref.dtype)
-    kg_ref[...] = (dot(grad_scores.T, q) + lax.dot_general(v * kd, grad_in, nt, precision=highest,
-                                                           preferred_element_type=f32)).astype(kg_ref.dtype)
-    vg_ref[...] = (dot(scores.T, g) + dot(k * kd, grad_in)).astype(vg_ref.dtype)
-
-
-def finish(inputs, pieces, state_in, grad_in):
+    for j in range(block):
+        cols = slice(j * dk, (j + 1) * dk)
+        q = q_ref[:, cols]
+        k = k_ref[:, cols]
+        v = v_ref[:, cols]
+        g = g_ref[:, cols]
+        row = cum_ref[j:j + 1, :]
+        grid_row = jnp.broadcast_to(row, (size, size))
+        col = jnp.sum(jnp.where(later & (~(lax.broadcasted_iota(jnp.int32, (size, size), 0) >
+                                           lax.broadcasted_iota(jnp.int32, (size, size), 1))), grid_row, 0.0),
+                      axis=1, keepdims=True)
+        last = row[:, size - 1:size]
+        weights = jnp.where(later, jnp.exp(jnp.where(later, col - row, 0.0)), 0.0)
+        scores = mm(q, k, nt) * weights
+        grad_scores = mm(g, v, nt) * weights
+        qd = jnp.exp(col)
+        kd = jnp.exp(last - col)
+        state = s_ref[j]
+        grad_in = gs_ref[j]
+        att_ref[:, cols] = (mm_left(scores, v, nn) + qd * mm_right(q, state, nn)).astype(att_ref.dtype)
+        qg_ref[:, cols] = (mm_left(grad_scores, k, nn) + qd * mm_right(g, state, nt)).astype(qg_ref.dtype)
+        kg_ref[:, cols] = (mm_left(grad_scores.T, q, nn) + kd * mm_right(v, grad_in, nt)).astype(kg_ref.dtype)
+        vg_ref[:, cols] = (mm_left(scores.T, g, nn) + kd * mm_right(k, grad_in, nn)).astype(vg_ref.dtype)
+
+
+def finish(inputs, cumul_heads, state_in, grad_in):
     queries = inputs[0]
     length, width = queries.shape
     heads = state_in.shape[0]
     dk = width // heads
-    rows, cols, qd, kd = pieces
-    tile = pl.BlockSpec((length, dk), lambda h: (0, h))
-    per_head = lambda a: pl.BlockSpec((1,) + a.shape[1:], lambda h: (h, 0, 0))
+    block = 8
+    tile = pl.BlockSpec((length, block * dk), lambda h: (0, h))
+    states = pl.BlockSpec((block, dk, dk), lambda h: (h, 0, 0))
     out = jax.ShapeDtypeStruct((length, width), jnp.bfloat16)
     return pl.pallas_call(
         head_kernel,
-        grid=(heads,),
-        in_specs=[tile] * 4 + [per_head(a) for a in (rows, cols, qd, kd, state_in, grad_in)],
+        grid=(heads // block,),
+        in_specs=[tile] * 4 + [pl.BlockSpec((block, length), lambda h: (h, 0)), states, states],
         out_specs=[tile] * 4,
         out_shape=[out] * 4,
         compiler_params=pltpu.CompilerParams(dimension_semantics=("arbitrary",)),
-    )(*inputs, rows, cols, qd, kd, state_in, grad_in)
+    )(*inputs, cumul_heads, state_in, grad_in)
 
 
 def gather_rows(row, axis):

time: 207 us -> 178 us (0.86)
  starting transfers between devices: 73.4 us -> 45.7 us
  waiting for transfers between devices: 58.3 us -> 84.8 us
  Pallas kernels: 34.5 us -> 13.7 us
  local copies, waits for them, and re-layouts: 17.8 us -> 11.9 us
    ppermute x16, starting transfers between devices: 65.6 us -> 39.2 us  [chip_scan(): received = lax.ppermute(sent, axis, pairs)]
    ppermute x16, waiting for transfers between devices: 39.7 us -> 65.7 us  [chip_scan(): received = lax.ppermute(sent, axis, pairs)]
    pallas_call x1, Pallas kernels: 34.5 us -> 13.7 us  [finish(): pl.pallas_call(head_kernel, grid=(heads // block,), in_specs=[tile] * 4 +...]
    broadcast_in_dim x3 -> x0, local copies, waits for them, and re-layouts: 6 us -> none  [the longest x1 2.01 us: prepare(): jnp.transpose(key_decay)[:, :, None]]
    ppermute x3, starting transfers between devices: 0.8 us -> 4.34 us  [shards(): other_total, other_state, other_grad = lax.ppermute(sent, axis, partner)]
    ppermute x5, starting transfers between devices: 3.96 us -> 0.49 us  [gather_rows(): known = jnp.concatenate([known, lax.ppermute(known, axis, pairs)], 0)]
  transfers between devices with their start and end apart: 26 -> 26, of which waited for: 9 -> 10; matrix products, arithmetic and copies ran while one was open for 15% -> 15% of each run, Pallas kernels for 0% -> 0%
where the time goes in v1:
time: 178 us; the launch traced here: 177 us
  waiting for transfers between devices  84.8 us (48%)
  starting transfers between devices  45.7 us (26%)
  Pallas kernels  13.7 us (8%)
  other arithmetic  13.6 us (8%)
  local copies, waits for them, and re-layouts  11.9 us (7%)
  matrix products  5.77 us (3%)
    ppermute x16, waiting for transfers between devices, chip_scan(): received = lax.ppermute(sent, axis, pairs)  65.7 us
    ppermute x16, starting transfers between devices, chip_scan(): received = lax.ppermute(sent, axis, pairs)  39.2 us
    ppermute x5, waiting for transfers between devices, gather_rows(): known = jnp.concatenate([known, lax.ppermute(known, axis, pairs)], 0)  19.1 us
    pallas_call x1, Pallas kernels, finish(): pl.pallas_call(head_kernel, grid=(heads // block,), in_specs=[tile] * 4 +...  13.7 us
    select_n x2, other arithmetic, assemble(): jnp.where(first, jnp.concatenate([keep, got], 0), jnp.concatenate([got, k...  4.87 us
    ppermute x3, starting transfers between devices, shards(): other_total, other_state, other_grad = lax.ppermute(sent, axis, partner)  4.34 us
  transfers between devices with their start and end apart: 26, of which 10 were waited for; matrix products, arithmetic and copies ran while one was open for 15% of the time, Pallas kernels for 0%

profile of v1, /device:TPU:1, one launch (start us, length us, event | category | flops | bytes accessed | tf_op | source)
XLA Modules:
  0.0 176.8 jit_solution(4949150700784395140)
XLA Ops:
  0.6 0.9 convert_reduce_fusion
  1.5 3.3 %collective-permute-start = (f32[32]{0:T(128)S(1)}, f32[32]{0:T(128)S(1)}, u32[]{:S(2)}, u32[]{:S(2)}) collective-permute-start(f32[32]{0:T(128)S(1)} %convert_reduce_fusion), channel_id=1, source_target_pairs={{0,1},{1,0},{2,3},{3,2},{4,5},{5,4},{6,7},{7,6},{8,9},{9,8},{10,11... | collective-permute-start | bytes 392 | tf_op jit(solution)/shard_map/ppermute | solution.py:162
  4.9 0.8 copy.9
  5.9 2.6 %copy.18 = f32[128,4096]{0,1:T(8,128)} copy(bf16[128,4096]{1,0:T(8,128)(2,1)} %q_ref.1) | data formatting | bytes 3145728 | tf_op jit(solution)/shard_map/convert_element_type | solution.py:19
  8.6 2.8 %fusion = f32[32,128,128]{2,1,0:T(8,128)S(1)} fusion(f32[128,32,128]{0,2,1:T(8,128)} %bitcast.166, f32[128,32]{0,1:T(8,128)S(1)} %copy.14, bf16[128,4096]{1,0:T(8,128)(2,1)S(1)} %copy-done.6), kind=kOutput, calls=%fused_computation.3 | convolution fusion | flops 805830656 | bytes 5259264 | tf_op jit(solution)/shard_map/the,thf->hef/dot_general | solution.py:28
  11.3 1.1 constant_dynamic-slice_fusion.18
  12.4 0.5 collective-permute-start.16
  13.3 1.6 copy.17
  15.0 3.0 %fusion.2 = f32[32,128,128]{2,1,0:T(8,128)S(1)} fusion(f32[128,32,128]{0,2,1:T(8,128)} %bitcast.167, f32[128,32]{0,1:T(8,128)S(1)} %copy.11, bf16[128,4096]{1,0:T(8,128)(2,1)} %v_ref.1), kind=kOutput, calls=%fused_computation.5 | convolution fusion | flops 805830656 | bytes 5259264 | tf_op jit(solution)/shard_map/she,shf->hef/dot_general | solution.py:27
  18.0 1.1 constant_dynamic-slice_fusion.19
  19.1 0.5 collective-permute-start.1
  19.9 5.6 %collective-permute-done.4 = f32[2,32]{1,0:T(2,128)S(1)} collective-permute-done((f32[2,32]{1,0:T(2,128)S(1)}, f32[2,32]{1,0:T(2,128)S(1)}, u32[]{:S(2)}, u32[]{:S(2)}) %collective-permute-start.4) | collective-permute-done | bytes 288 | tf_op jit(solution)/shard_map/ppermute | solution.py:110
  25.6 6.0 %collective-permute-done.5 = f32[4,32]{1,0:T(4,128)S(1)} collective-permute-done((f32[4,32]{1,0:T(4,128)S(1)}, f32[4,32]{1,0:T(4,128)S(1)}, u32[]{:S(2)}, u32[]{:S(2)}) %collective-permute-start.5) | collective-permute-done | bytes 544 | tf_op jit(solution)/shard_map/ppermute | solution.py:110
  31.8 3.6 %collective-permute-done.6 = f32[8,32]{1,0:T(8,128)S(1)} collective-permute-done((f32[8,32]{1,0:T(8,128)S(1)}, f32[8,32]{1,0:T(8,128)S(1)}, u32[]{:S(2)}, u32[]{:S(2)}) %collective-permute-start.6) | collective-permute-done | bytes 1056 | tf_op jit(solution)/shard_map/ppermute | solution.py:110
  35.5 4.0 %collective-permute-done.7 = f32[16,32]{1,0:T(8,128)S(1)} collective-permute-done((f32[16,32]{1,0:T(8,128)S(1)}, f32[16,32]{1,0:T(8,128)S(1)}, u32[]{:S(2)}, u32[]{:S(2)}) %collective-permute-start.7) | collective-permute-done | bytes 2080 | tf_op jit(solution)/shard_map/ppermute | solution.py:110
  39.5 0.6 gather_fusion
  40.5 1.7 multiply_add_fusion
  42.4 1.3 collective-permute-start.17
  43.7 1.3 collective-permute-start.21
  45.3 0.7 copy-done.3
  45.9 4.0 %collective-permute-start.2 = (f32[8,128,128]{2,1,0:T(8,128)S(1)}, f32[8,128,128]{2,1,0:T(8,128)S(1)}, u32[]{:S(2)}, u32[]{:S(2)}) collective-permute-start(f32[8,128,128]{2,1,0:T(8,128)S(1)} %get-tuple-element.50), channel_id=1, source_target_pairs={{0,2},{1,3},{2,4},{3,5},{4,6},{5,7},{6,8},{7,9},{8,10},{9,11},{10,... | collective-permute-start | bytes 1572872 | tf_op jit(solution)/shard_map/ppermute | solution.py:137
  50.0 4.0 %collective-permute-start.11 = (f32[8,128,128]{2,1,0:T(8,128)S(1)}, f32[8,128,128]{2,1,0:T(8,128)S(1)}, u32[]{:S(2)}, u32[]{:S(2)}) collective-permute-start(f32[8,128,128]{2,1,0:T(8,128)S(1)} %get-tuple-element.51), channel_id=1, source_target_pairs={{0,8},{1,9},{2,10},{3,11},{4,12},{5,13},{6,14},{7,15},{8,16},{9,17... | collective-permute-start | bytes 1572872 | tf_op jit(solution)/shard_map/ppermute | solution.py:137
  54.5 1.3 collective-permute-start.18
  56.0 1.3 collective-permute-start.22
  57.3 13.2 %collective-permute-done.11 = f32[8,128,128]{2,1,0:T(8,128)S(1)} collective-permute-done((f32[8,128,128]{2,1,0:T(8,128)S(1)}, f32[8,128,128]{2,1,0:T(8,128)S(1)}, u32[]{:S(2)}, u32[]{:S(2)}) %collective-permute-start.11) | collective-permute-done | bytes 524320 | tf_op jit(solution)/shard_map/ppermute | solution.py:137
  70.7 1.3 collective-permute-start.8
  72.0 6.8 %collective-permute-start.12 = (f32[8,128,128]{2,1,0:T(8,128)S(1)}, f32[8,128,128]{2,1,0:T(8,128)S(1)}, u32[]{:S(2)}, u32[]{:S(2)}) collective-permute-start(f32[8,128,128]{2,1,0:T(8,128)S(1)} %get-tuple-element.49), channel_id=1, source_target_pairs={{0,16},{1,17},{2,18},{3,19},{4,20},{5,21},{6,22},{7,23},{8,24},{9,... | collective-permute-start | bytes 1572872 | tf_op jit(solution)/shard_map/ppermute | solution.py:137
  78.9 1.3 collective-permute-start.19
  80.2 18.5 %collective-permute-done.22 = f32[8,128,128]{2,1,0:T(8,128)S(1)} collective-permute-done((f32[8,128,128]{2,1,0:T(8,128)S(1)}, f32[8,128,128]{2,1,0:T(8,128)S(1)}, u32[]{:S(2)}, u32[]{:S(2)}) %collective-permute-start.22) | collective-permute-done | bytes 524320 | tf_op jit(solution)/shard_map/ppermute | solution.py:137
  98.9 1.3 collective-permute-start.23
  100.3 1.3 collective-permute-start.9
  101.8 4.0 %collective-permute-start.13 = (f32[8,128,128]{2,1,0:T(8,128)S(1)}, f32[8,128,128]{2,1,0:T(8,128)S(1)}, u32[]{:S(2)}, u32[]{:S(2)}) collective-permute-start(f32[8,128,128]{2,1,0:T(8,128)S(1)} %multiply_add_fusion.12), channel_id=1, source_target_pairs={{0,2},{1,3},{2,4},{3,5},{4,6},{5,7},{6,8},{7,9},{8,10},{9,11},{10,... | collective-permute-start | bytes 1572872 | tf_op jit(solution)/shard_map/ppermute | solution.py:137
  106.0 1.3 collective-permute-start.20
  107.3 6.5 %collective-permute-done.23 = f32[8,128,128]{2,1,0:T(8,128)S(1)} collective-permute-done((f32[8,128,128]{2,1,0:T(8,128)S(1)}, f32[8,128,128]{2,1,0:T(8,128)S(1)}, u32[]{:S(2)}, u32[]{:S(2)}) %collective-permute-start.23) | collective-permute-done | bytes 524320 | tf_op jit(solution)/shard_map/ppermute | solution.py:137
  113.9 1.5 collective-permute-start.24
  115.4 7.4 %collective-permute-done.9 = f32[8,128,128]{2,1,0:T(8,128)S(1)} collective-permute-done((f32[8,128,128]{2,1,0:T(8,128)S(1)}, f32[8,128,128]{2,1,0:T(8,128)S(1)}, u32[]{:S(2)}, u32[]{:S(2)}) %collective-permute-start.9) | collective-permute-done | bytes 524320 | tf_op jit(solution)/shard_map/ppermute | solution.py:137
  122.9 5.9 %collective-permute-start.10 = (f32[8,128,128]{2,1,0:T(8,128)S(1)}, f32[8,128,128]{2,1,0:T(8,128)S(1)}, u32[]{:S(2)}, u32[]{:S(2)}) collective-permute-start(f32[8,128,128]{2,1,0:T(8,128)S(1)} %multiply_add_fusion.15), channel_id=1, source_target_pairs={{0,16},{1,17},{2,18},{3,19},{4,20},{5,21},{6,22},{7,23},{8,24},{9,... | collective-permute-start | bytes 1572872 | tf_op jit(solution)/shard_map/ppermute | solution.py:137
  129.0 1.3 collective-permute-start.14
  130.3 19.6 %collective-permute-done.20 = f32[8,128,128]{2,1,0:T(8,128)S(1)} collective-permute-done((f32[8,128,128]{2,1,0:T(8,128)S(1)}, f32[8,128,128]{2,1,0:T(8,128)S(1)}, u32[]{:S(2)}, u32[]{:S(2)}) %collective-permute-start.20) | collective-permute-done | bytes 524320 | tf_op jit(solution)/shard_map/ppermute | solution.py:137
  150.4 1.1 copy-done.1
  151.6 1.3 fusion.13
  152.9 1.7 collective-permute-start.25
  155.0 0.8 copy-done.4
  155.8 1.7 fusion.11
  157.5 0.7 copy.10
  158.2 3.3 %maximum_select_fusion.1.gs_ref = f32[32,128,128]{2,1,0:T(8,128)} fusion(f32[16,128,128]{2,1,0:T(8,128)} %collective-permute-done.25, f32[16,128,128]{2,1,0:T(8,128)S(1)} %get-tuple-element.40, pred[]{:T(512)S(6)} %eq.7), kind=kLoop, calls=%fused_computation.2 | loop fusion | flops 1572864 | bytes 4194305 | tf_op jit(solution)/shard_map/jit(_where)/select_n | solution.py:211
  161.4 1.6 maximum_select_fusion.s_ref
  163.0 13.7 %shard_map.84 = (bf16[128,4096]{1,0:T(8,128)(2,1)}, bf16[128,4096]{1,0:T(8,128)(2,1)}, bf16[128,4096]{1,0:T(8,128)(2,1)}, bf16[128,4096]{1,0:T(8,128)(2,1)}) custom-call(bf16[128,4096]{1,0:T(8,128)(2,1)} %q_ref.1, bf16[128,4096]{1,0:T(8,128)(2,1)} %k_ref.1, bf16[128,4096]{1,0:T(8,128)(2,1)} %v_ref.1, bf16[128,4096]{1,0:T(8,128)(2,1)} %g_ref.1, ...), custom_call_target="tpu_custom_call" | custom-call | tf_op jit(solution)/shard_map/pallas_call | solution.py:93
  (82 shorter events, 4.9 us)
Async XLA Ops:
  0.6 7.9 %copy-start.6 = (bf16[128,4096]{1,0:T(8,128)(2,1)S(1)}, bf16[128,4096]{1,0:T(8,128)(2,1)}, u32[]{:S(2)}) copy-start(bf16[128,4096]{1,0:T(8,128)(2,1)} %g_ref.1) | copy-start | bytes 3145732
  1.5 30.2 %collective-permute-start = (f32[32]{0:T(128)S(1)}, f32[32]{0:T(128)S(1)}, u32[]{:S(2)}, u32[]{:S(2)}) collective-permute-start(f32[32]{0:T(128)S(1)} %convert_reduce_fusion), channel_id=1, source_target_pairs={{0,1},{1,0},{2,3},{3,2},{4,5},{5,4},{6,7},{7,6},{8,9},{9,8},{10,11... | collective-permute-start | bytes 392 | tf_op jit(solution)/shard_map/ppermute | solution.py:162
  4.9 14.8 %collective-permute-start.3 = (f32[1,32]{1,0:T(1,128)S(1)}, f32[1,32]{1,0:T(1,128)S(1)}, u32[]{:S(2)}, u32[]{:S(2)}) collective-permute-start(f32[1,32]{1,0:T(1,128)S(1)} %bitcast.169), channel_id=1, source_target_pairs={{0,1},{1,2},{2,3},{3,4},{4,5},{5,6},{6,7},{7,8},{8,9},{9,10},{10,1... | collective-permute-start | bytes 392 | tf_op jit(solution)/shard_map/ppermute | solution.py:110
  11.3 3.6 %copy-start = (f32[32,128,128]{2,1,0:T(8,128)}, f32[32,128,128]{2,1,0:T(8,128)S(1)}, u32[]{:S(2)}) copy-start(f32[32,128,128]{2,1,0:T(8,128)S(1)} %fusion) | copy-start | bytes 6291460
  11.3 2.0 %copy-start.5 = (bf16[128,4096]{1,0:T(8,128)(2,1)S(1)}, bf16[128,4096]{1,0:T(8,128)(2,1)}, u32[]{:S(2)}) copy-start(bf16[128,4096]{1,0:T(8,128)(2,1)} %k_ref.1) | copy-start | bytes 3145732
  12.4 28.1 %collective-permute-start.16 = (f32[16,128,128]{2,1,0:T(8,128)}, f32[16,128,128]{2,1,0:T(8,128)}, u32[]{:S(2)}, u32[]{:S(2)}) collective-permute-start(f32[16,128,128]{2,1,0:T(8,128)} %constant_dynamic-slice_fusion.18), channel_id=1, source_target_pairs={{0,1},{1,0},{2,3},{3,2},{4,5},{5,4},{6,7},{7,6},{8,9},{9,8},{10,11... | collective-permute-start | bytes 3145736 | tf_op jit(solution)/shard_map/ppermute | solution.py:162
  19.1 25.9 %collective-permute-start.1 = (f32[16,128,128]{2,1,0:T(8,128)}, f32[16,128,128]{2,1,0:T(8,128)S(1)}, u32[]{:S(2)}, u32[]{:S(2)}) collective-permute-start(f32[16,128,128]{2,1,0:T(8,128)} %constant_dynamic-slice_fusion.19), channel_id=1, source_target_pairs={{0,1},{1,0},{2,3},{3,2},{4,5},{5,4},{6,7},{7,6},{8,9},{9,8},{10,11... | collective-permute-start | bytes 3145736 | tf_op jit(solution)/shard_map/ppermute | solution.py:162
  19.6 5.8 %collective-permute-start.4 = (f32[2,32]{1,0:T(2,128)S(1)}, f32[2,32]{1,0:T(2,128)S(1)}, u32[]{:S(2)}, u32[]{:S(2)}) collective-permute-start(f32[2,32]{1,0:T(2,128)S(1)} %pad_maximum_fusion.4), channel_id=1, source_target_pairs={{0,2},{1,3},{2,4},{3,5},{4,6},{5,7},{6,8},{7,9},{8,10},{9,11},{10,... | collective-permute-start | bytes 776 | tf_op jit(solution)/shard_map/ppermute | solution.py:110
  25.5 6.1 %collective-permute-start.5 = (f32[4,32]{1,0:T(4,128)S(1)}, f32[4,32]{1,0:T(4,128)S(1)}, u32[]{:S(2)}, u32[]{:S(2)}) collective-permute-start(f32[4,32]{1,0:T(4,128)S(1)} %pad_maximum_fusion.3), channel_id=1, source_target_pairs={{0,4},{1,5},{2,6},{3,7},{4,8},{5,9},{6,10},{7,11},{8,12},{9,13},{1... | collective-permute-start | bytes 1544 | tf_op jit(solution)/shard_map/ppermute | solution.py:110
  31.6 3.7 %collective-permute-start.6 = (f32[8,32]{1,0:T(8,128)S(1)}, f32[8,32]{1,0:T(8,128)S(1)}, u32[]{:S(2)}, u32[]{:S(2)}) collective-permute-start(f32[8,32]{1,0:T(8,128)S(1)} %pad_maximum_fusion.2), channel_id=1, source_target_pairs={{0,8},{1,9},{2,10},{3,11},{4,12},{5,13},{6,14},{7,15},{8,16},{9,17... | collective-permute-start | bytes 3080 | tf_op jit(solution)/shard_map/ppermute | solution.py:110
  35.4 4.1 %collective-permute-start.7 = (f32[16,32]{1,0:T(8,128)S(1)}, f32[16,32]{1,0:T(8,128)S(1)}, u32[]{:S(2)}, u32[]{:S(2)}) collective-permute-start(f32[16,32]{1,0:T(8,128)S(1)} %concatenate.40), channel_id=1, source_target_pairs={{0,16},{1,17},{2,18},{3,19},{4,20},{5,21},{6,22},{7,23},{8,24},{9,... | collective-permute-start | bytes 6152 | tf_op jit(solution)/shard_map/ppermute | solution.py:110
  42.4 11.6 %collective-permute-start.17 = (f32[8,128,128]{2,1,0:T(8,128)S(1)}, f32[8,128,128]{2,1,0:T(8,128)S(1)}, u32[]{:S(2)}, u32[]{:S(2)}) collective-permute-start(f32[8,128,128]{2,1,0:T(8,128)S(1)} %get-tuple-element.46), channel_id=1, source_target_pairs={{2,0},{3,1},{4,2},{5,3},{6,4},{7,5},{8,6},{9,7},{10,8},{11,9},{12,... | collective-permute-start | bytes 1572872 | tf_op jit(solution)/shard_map/ppermute | solution.py:137
  43.7 10.7 %collective-permute-start.21 = (f32[8,128,128]{2,1,0:T(8,128)S(1)}, f32[8,128,128]{2,1,0:T(8,128)S(1)}, u32[]{:S(2)}, u32[]{:S(2)}) collective-permute-start(f32[8,128,128]{2,1,0:T(8,128)S(1)} %get-tuple-element.47), channel_id=1, source_target_pairs={{8,0},{9,1},{10,2},{11,3},{12,4},{13,5},{14,6},{15,7},{16,8},{17,9... | collective-permute-start | bytes 1572872 | tf_op jit(solution)/shard_map/ppermute | solution.py:137
  45.0 1.0 copy-start.3
  45.9 11.4 %collective-permute-start.2 = (f32[8,128,128]{2,1,0:T(8,128)S(1)}, f32[8,128,128]{2,1,0:T(8,128)S(1)}, u32[]{:S(2)}, u32[]{:S(2)}) collective-permute-start(f32[8,128,128]{2,1,0:T(8,128)S(1)} %get-tuple-element.50), channel_id=1, source_target_pairs={{0,2},{1,3},{2,4},{3,5},{4,6},{5,7},{6,8},{7,9},{8,10},{9,11},{10,... | collective-permute-start | bytes 1572872 | tf_op jit(solution)/shard_map/ppermute | solution.py:137
  50.0 20.5 %collective-permute-start.11 = (f32[8,128,128]{2,1,0:T(8,128)S(1)}, f32[8,128,128]{2,1,0:T(8,128)S(1)}, u32[]{:S(2)}, u32[]{:S(2)}) collective-permute-start(f32[8,128,128]{2,1,0:T(8,128)S(1)} %get-tuple-element.51), channel_id=1, source_target_pairs={{0,8},{1,9},{2,10},{3,11},{4,12},{5,13},{6,14},{7,15},{8,16},{9,17... | collective-permute-start | bytes 1572872 | tf_op jit(solution)/shard_map/ppermute | solution.py:137
  54.5 24.3 %collective-permute-start.18 = (f32[8,128,128]{2,1,0:T(8,128)S(1)}, f32[8,128,128]{2,1,0:T(8,128)S(1)}, u32[]{:S(2)}, u32[]{:S(2)}) collective-permute-start(f32[8,128,128]{2,1,0:T(8,128)S(1)} %get-tuple-element.44), channel_id=1, source_target_pairs={{4,0},{5,1},{6,2},{7,3},{8,4},{9,5},{10,6},{11,7},{12,8},{13,9},{1... | collective-permute-start | bytes 1572872 | tf_op jit(solution)/shard_map/ppermute | solution.py:137
  56.0 42.8 %collective-permute-start.22 = (f32[8,128,128]{2,1,0:T(8,128)S(1)}, f32[8,128,128]{2,1,0:T(8,128)S(1)}, u32[]{:S(2)}, u32[]{:S(2)}) collective-permute-start(f32[8,128,128]{2,1,0:T(8,128)S(1)} %get-tuple-element.45), channel_id=1, source_target_pairs={{16,0},{17,1},{18,2},{19,3},{20,4},{21,5},{22,6},{23,7},{24,8},{25... | collective-permute-start | bytes 1572872 | tf_op jit(solution)/shard_map/ppermute | solution.py:137
  70.7 29.5 %collective-permute-start.8 = (f32[8,128,128]{2,1,0:T(8,128)S(1)}, f32[8,128,128]{2,1,0:T(8,128)S(1)}, u32[]{:S(2)}, u32[]{:S(2)}) collective-permute-start(f32[8,128,128]{2,1,0:T(8,128)S(1)} %get-tuple-element.48), channel_id=1, source_target_pairs={{0,4},{1,5},{2,6},{3,7},{4,8},{5,9},{6,10},{7,11},{8,12},{9,13},{1... | collective-permute-start | bytes 1572872 | tf_op jit(solution)/shard_map/ppermute | solution.py:137
  72.0 29.6 %collective-permute-start.12 = (f32[8,128,128]{2,1,0:T(8,128)S(1)}, f32[8,128,128]{2,1,0:T(8,128)S(1)}, u32[]{:S(2)}, u32[]{:S(2)}) collective-permute-start(f32[8,128,128]{2,1,0:T(8,128)S(1)} %get-tuple-element.49), channel_id=1, source_target_pairs={{0,16},{1,17},{2,18},{3,19},{4,20},{5,21},{6,22},{7,23},{8,24},{9,... | collective-permute-start | bytes 1572872 | tf_op jit(solution)/shard_map/ppermute | solution.py:137
  78.9 26.9 %collective-permute-start.19 = (f32[8,128,128]{2,1,0:T(8,128)S(1)}, f32[8,128,128]{2,1,0:T(8,128)S(1)}, u32[]{:S(2)}, u32[]{:S(2)}) collective-permute-start(f32[8,128,128]{2,1,0:T(8,128)S(1)} %multiply_add_fusion.8), channel_id=1, source_target_pairs={{8,0},{9,1},{10,2},{11,3},{12,4},{13,5},{14,6},{15,7},{16,8},{17,9... | collective-permute-start | bytes 1572872 | tf_op jit(solution)/shard_map/ppermute | solution.py:137
  98.9 14.9 %collective-permute-start.23 = (f32[8,128,128]{2,1,0:T(8,128)S(1)}, f32[8,128,128]{2,1,0:T(8,128)S(1)}, u32[]{:S(2)}, u32[]{:S(2)}) collective-permute-start(f32[8,128,128]{2,1,0:T(8,128)S(1)} %multiply_add_fusion.4), channel_id=1, source_target_pairs={{2,0},{3,1},{4,2},{5,3},{6,4},{7,5},{8,6},{9,7},{10,8},{11,9},{12,... | collective-permute-start | bytes 1572872 | tf_op jit(solution)/shard_map/ppermute | solution.py:137
  100.3 22.5 %collective-permute-start.9 = (f32[8,128,128]{2,1,0:T(8,128)S(1)}, f32[8,128,128]{2,1,0:T(8,128)S(1)}, u32[]{:S(2)}, u32[]{:S(2)}) collective-permute-start(f32[8,128,128]{2,1,0:T(8,128)S(1)} %multiply_add_fusion.16), channel_id=1, source_target_pairs={{0,8},{1,9},{2,10},{3,11},{4,12},{5,13},{6,14},{7,15},{8,16},{9,17... | collective-permute-start | bytes 1572872 | tf_op jit(solution)/shard_map/ppermute | solution.py:137
  101.8 27.1 %collective-permute-start.13 = (f32[8,128,128]{2,1,0:T(8,128)S(1)}, f32[8,128,128]{2,1,0:T(8,128)S(1)}, u32[]{:S(2)}, u32[]{:S(2)}) collective-permute-start(f32[8,128,128]{2,1,0:T(8,128)S(1)} %multiply_add_fusion.12), channel_id=1, source_target_pairs={{0,2},{1,3},{2,4},{3,5},{4,6},{5,7},{6,8},{7,9},{8,10},{9,11},{10,... | collective-permute-start | bytes 1572872 | tf_op jit(solution)/shard_map/ppermute | solution.py:137
  106.0 44.0 %collective-permute-start.20 = (f32[8,128,128]{2,1,0:T(8,128)S(1)}, f32[8,128,128]{2,1,0:T(8,128)S(1)}, u32[]{:S(2)}, u32[]{:S(2)}) collective-permute-start(f32[8,128,128]{2,1,0:T(8,128)S(1)} %multiply_add_fusion.7), channel_id=1, source_target_pairs={{16,0},{17,1},{18,2},{19,3},{20,4},{21,5},{22,6},{23,7},{24,8},{25... | collective-permute-start | bytes 1572872 | tf_op jit(solution)/shard_map/ppermute | solution.py:137
  113.9 36.3 %collective-permute-start.24 = (f32[8,128,128]{2,1,0:T(8,128)S(1)}, f32[8,128,128]{2,1,0:T(8,128)S(1)}, u32[]{:S(2)}, u32[]{:S(2)}) collective-permute-start(f32[8,128,128]{2,1,0:T(8,128)S(1)} %multiply_add_fusion.3), channel_id=1, source_target_pairs={{4,0},{5,1},{6,2},{7,3},{8,4},{9,5},{10,6},{11,7},{12,8},{13,9},{1... | collective-permute-start | bytes 1572872 | tf_op jit(solution)/shard_map/ppermute | solution.py:137
  122.9 31.7 %collective-permute-start.10 = (f32[8,128,128]{2,1,0:T(8,128)S(1)}, f32[8,128,128]{2,1,0:T(8,128)S(1)}, u32[]{:S(2)}, u32[]{:S(2)}) collective-permute-start(f32[8,128,128]{2,1,0:T(8,128)S(1)} %multiply_add_fusion.15), channel_id=1, source_target_pairs={{0,16},{1,17},{2,18},{3,19},{4,20},{5,21},{6,22},{7,23},{8,24},{9,... | collective-permute-start | bytes 1572872 | tf_op jit(solution)/shard_map/ppermute | solution.py:137
  129.0 25.8 %collective-permute-start.14 = (f32[8,128,128]{2,1,0:T(8,128)S(1)}, f32[8,128,128]{2,1,0:T(8,128)S(1)}, u32[]{:S(2)}, u32[]{:S(2)}) collective-permute-start(f32[8,128,128]{2,1,0:T(8,128)S(1)} %multiply_add_fusion.11), channel_id=1, source_target_pairs={{0,4},{1,5},{2,6},{3,7},{4,8},{5,9},{6,10},{7,11},{8,12},{9,13},{1... | collective-permute-start | bytes 1572872 | tf_op jit(solution)/shard_map/ppermute | solution.py:137
  150.0 1.6 copy-start.1
  152.9 5.3 %collective-permute-start.25 = (f32[16,128,128]{2,1,0:T(8,128)}, f32[16,128,128]{2,1,0:T(8,128)}, u32[]{:S(2)}, u32[]{:S(2)}) collective-permute-start(f32[16,128,128]{2,1,0:T(8,128)} %get-tuple-element.41), channel_id=1, source_target_pairs={{0,1},{1,0},{2,3},{3,2},{4,5},{5,4},{6,7},{7,6},{8,9},{9,8},{10,11... | collective-permute-start | bytes 3145736 | tf_op jit(solution)/shard_map/ppermute | solution.py:208
  154.6 1.2 copy-start.4
  157.5 4.0 %collective-permute-start.15 = (f32[16,128,128]{2,1,0:T(8,128)}, f32[16,128,128]{2,1,0:T(8,128)S(1)}, u32[]{:S(2)}, u32[]{:S(2)}) collective-permute-start(f32[16,128,128]{2,1,0:T(8,128)} %get-tuple-element.43), channel_id=1, source_target_pairs={{0,1},{1,0},{2,3},{3,2},{4,5},{5,4},{6,7},{7,6},{8,9},{9,8},{10,11... | collective-permute-start | bytes 3145736 | tf_op jit(solution)/shard_map/ppermute | solution.py:208
  158.1 3.3 %copy-start.2 = (f32[16,128,128]{2,1,0:T(8,128)S(1)}, f32[16,128,128]{2,1,0:T(8,128)}, u32[]{:S(2)}) copy-start(f32[16,128,128]{2,1,0:T(8,128)} %get-tuple-element.42) | copy-start | bytes 3145732

commit v2 on v1

--- a/solution.py
+++ b/solution.py
@@ -172,7 +172,8 @@
     bwd_a = jnp.where(first, one, jnp.exp(other_total_half))[:, None, None]
     bwd_b = jnp.where(first, jnp.exp(own_total_half), one)[:, None, None]
     chip_grad = bwd_a * mine_grad + bwd_b * other_grad
-    every_total = gather_rows(total, axis)
+    padded = jnp.zeros((64, 128), total.dtype).at[0, :total.shape[0]].set(total)
+    every_total = lax.all_gather(padded, axis)[:, 0, :total.shape[0]]
     chip_totals = every_total[0::2] + every_total[1::2]
     chip = lax.axis_index(axis) // 2
     steps = []

time: 178 us -> 201 us (1.13)
  between operations: 1.31 us -> 14.5 us
  starting transfers between devices: 45.7 us -> 55.5 us
  waiting for transfers between devices: 84.8 us -> 77 us
  other arithmetic: 13.6 us -> 21.1 us
    all_gather x0 -> x1, waiting for transfers between devices: none -> 31.2 us  [shards(): every_total = lax.all_gather(padded, axis)[:, 0, :total.shape[0]]]
    ppermute x16, waiting for transfers between devices: 65.7 us -> 43.9 us  [chip_scan(): received = lax.ppermute(sent, axis, pairs)]
    ppermute x5 -> x0, waiting for transfers between devices: 19.1 us -> none  [gather_rows(): known = jnp.concatenate([known, lax.ppermute(known, axis, pairs)], 0)]
    ppermute x16, starting transfers between devices: 39.2 us -> 49.4 us  [chip_scan(): received = lax.ppermute(sent, axis, pairs)]
    add x4, other arithmetic: 0.85 us -> 5.3 us  [chip_scan(): carried = carried + to_start * received]
    add x10, other arithmetic: 1.36 us -> 4.05 us  [chip_scan(): sent = sent + to_end * received]
  transfers between devices with their start and end apart: 26 -> 22, of which waited for: 10 -> 9; matrix products, arithmetic and copies ran while one was open for 15% -> 15% of each run, Pallas kernels for 0% -> 0%
where the time goes in v2:
time: 201 us; the launch traced here: 200 us
  waiting for transfers between devices  77 us (38%)
  starting transfers between devices  55.5 us (28%)
  other arithmetic  21.1 us (10%)
  between operations  14.5 us (7%)
  Pallas kernels  13.7 us (7%)
  local copies, waits for them, and re-layouts  12.9 us (6%)
  matrix products  5.77 us (3%)
    ppermute x16, starting transfers between devices, chip_scan(): received = lax.ppermute(sent, axis, pairs)  49.4 us
    ppermute x16, waiting for transfers between devices, chip_scan(): received = lax.ppermute(sent, axis, pairs)  43.9 us
    all_gather x1, waiting for transfers between devices, shards(): every_total = lax.all_gather(padded, axis)[:, 0, :total.shape[0]]  31.2 us
    pallas_call x1, Pallas kernels, finish(): pl.pallas_call(head_kernel, grid=(heads // block,), in_specs=[tile] * 4 +...  13.7 us
    add x4, other arithmetic, chip_scan(): carried = carried + to_start * received  5.3 us
    select_n x2, other arithmetic, assemble(): jnp.where(first, jnp.concatenate([keep, got], 0), jnp.concatenate([got, k...  4.87 us
    add x10, other arithmetic, chip_scan(): sent = sent + to_end * received  4.05 us
  transfers between devices with their start and end apart: 22, of which 9 were waited for; matrix products, arithmetic and copies ran while one was open for 15% of the time, Pallas kernels for 0%

profile of v2, /device:TPU:1, one launch (start us, length us, event | category | flops | bytes accessed | tf_op | source)
XLA Modules:
  0.0 200.5 jit_solution(4359357729080084630)
XLA Ops:
  7.2 0.9 copy.17
  8.4 2.6 %copy.26 = f32[128,4096]{0,1:T(8,128)} copy(bf16[128,4096]{1,0:T(8,128)(2,1)} %q_ref.1) | data formatting | bytes 3145728 | tf_op jit(solution)/shard_map/convert_element_type | solution.py:19
  11.0 2.8 %fusion = f32[32,128,128]{2,1,0:T(8,128)S(1)} fusion(f32[128,32,128]{0,2,1:T(8,128)} %bitcast.165, f32[128,32]{0,1:T(8,128)S(1)} %copy.22, bf16[128,4096]{1,0:T(8,128)(2,1)S(1)} %copy-done.7), kind=kOutput, calls=%fused_computation.2 | convolution fusion | flops 805830656 | bytes 5259264 | tf_op jit(solution)/shard_map/the,thf->hef/dot_general | solution.py:28
  13.8 1.1 constant_dynamic-slice_fusion.18
  14.9 3.2 %collective-permute-start.11 = (f32[16,128,128]{2,1,0:T(8,128)}, f32[16,128,128]{2,1,0:T(8,128)}, u32[]{:S(2)}, u32[]{:S(2)}) collective-permute-start(f32[16,128,128]{2,1,0:T(8,128)} %constant_dynamic-slice_fusion.18), channel_id=1, source_target_pairs={{0,1},{1,0},{2,3},{3,2},{4,5},{5,4},{6,7},{7,6},{8,9},{9,8},{10,11... | collective-permute-start | bytes 3145736 | tf_op jit(solution)/shard_map/ppermute | solution.py:162
  18.9 1.6 copy.25
  20.6 3.0 %fusion.2 = f32[32,128,128]{2,1,0:T(8,128)S(1)} fusion(f32[128,32,128]{0,2,1:T(8,128)} %bitcast.166, f32[128,32]{0,1:T(8,128)S(1)} %copy.19, bf16[128,4096]{1,0:T(8,128)(2,1)} %v_ref.1), kind=kOutput, calls=%fused_computation.4 | convolution fusion | flops 805830656 | bytes 5259264 | tf_op jit(solution)/shard_map/she,shf->hef/dot_general | solution.py:27
  23.6 1.1 constant_dynamic-slice_fusion.19
  25.2 1.9 collective-permute-done
  27.2 1.7 multiply_add_fusion
  28.9 1.1 fusion.85
  30.1 1.3 collective-permute-start.12
  31.4 1.3 collective-permute-start.16
  32.7 1.0 copy-done.4
  33.6 1.4 multiply_add_fusion.1
  35.1 1.0 fusion.86
  36.1 4.8 %collective-permute-start.2 = (f32[8,128,128]{2,1,0:T(8,128)}, f32[8,128,128]{2,1,0:T(8,128)}, u32[]{:S(2)}, u32[]{:S(2)}) collective-permute-start(f32[8,128,128]{2,1,0:T(8,128)} %get-tuple-element.62), channel_id=1, source_target_pairs={{0,2},{1,3},{2,4},{3,5},{4,6},{5,7},{6,8},{7,9},{8,10},{9,11},{10,... | collective-permute-start | bytes 1572872 | tf_op jit(solution)/shard_map/ppermute | solution.py:137
  40.9 4.0 %collective-permute-start.6 = (f32[8,128,128]{2,1,0:T(8,128)}, f32[8,128,128]{2,1,0:T(8,128)}, u32[]{:S(2)}, u32[]{:S(2)}) collective-permute-start(f32[8,128,128]{2,1,0:T(8,128)} %get-tuple-element.63), channel_id=1, source_target_pairs={{0,8},{1,9},{2,10},{3,11},{4,12},{5,13},{6,14},{7,15},{8,16},{9,17... | collective-permute-start | bytes 1572872 | tf_op jit(solution)/shard_map/ppermute | solution.py:137
  44.9 31.2 %all-gather.2.cloned.1.call-done = f32[32,64,128]{2,1,0:T(8,128)} async-done(((f32[1,64,128]{2,1,0:T(8,128)}), f32[32,64,128]{2,1,0:T(8,128)}) %all-gather.2.cloned.1.call-update) | async-done | bytes 1048592 | tf_op jit(solution)/shard_map/all_gather | solution.py:176
  76.1 0.9 slice.50
  77.3 1.7 multiply_add_fusion.9
  79.0 1.3 collective-permute-start.13
  80.6 1.3 collective-permute-start.17
  82.0 1.4 multiply_add_fusion.17
  83.3 5.5 %collective-permute-start.3 = (f32[8,128,128]{2,1,0:T(8,128)S(1)}, f32[8,128,128]{2,1,0:T(8,128)S(1)}, u32[]{:S(2)}, u32[]{:S(2)}) collective-permute-start(f32[8,128,128]{2,1,0:T(8,128)S(1)} %get-tuple-element.60), channel_id=1, source_target_pairs={{0,4},{1,5},{2,6},{3,7},{4,8},{5,9},{6,10},{7,11},{8,12},{9,13},{1... | collective-permute-start | bytes 1572872 | tf_op jit(solution)/shard_map/ppermute | solution.py:137
  88.9 5.5 %collective-permute-start.7 = (f32[8,128,128]{2,1,0:T(8,128)S(1)}, f32[8,128,128]{2,1,0:T(8,128)S(1)}, u32[]{:S(2)}, u32[]{:S(2)}) collective-permute-start(f32[8,128,128]{2,1,0:T(8,128)S(1)} %get-tuple-element.61), channel_id=1, source_target_pairs={{0,16},{1,17},{2,18},{3,19},{4,20},{5,21},{6,22},{7,23},{8,24},{9,... | collective-permute-start | bytes 1572872 | tf_op jit(solution)/shard_map/ppermute | solution.py:137
  94.4 1.3 collective-permute-done.13
  95.8 1.3 collective-permute-start.14
  97.9 1.3 collective-permute-start.18
  99.7 10.5 %collective-permute-start.4 = (f32[8,128,128]{2,1,0:T(8,128)S(1)}, f32[8,128,128]{2,1,0:T(8,128)S(1)}, u32[]{:S(2)}, u32[]{:S(2)}) collective-permute-start(f32[8,128,128]{2,1,0:T(8,128)S(1)} %multiply_add_fusion.16), channel_id=1, source_target_pairs={{0,8},{1,9},{2,10},{3,11},{4,12},{5,13},{6,14},{7,15},{8,16},{9,17... | collective-permute-start | bytes 1572872 | tf_op jit(solution)/shard_map/ppermute | solution.py:137
  110.2 6.3 %collective-permute-done.7 = f32[8,128,128]{2,1,0:T(8,128)S(1)} collective-permute-done((f32[8,128,128]{2,1,0:T(8,128)S(1)}, f32[8,128,128]{2,1,0:T(8,128)S(1)}, u32[]{:S(2)}, u32[]{:S(2)}) %collective-permute-start.7) | collective-permute-done | bytes 524320 | tf_op jit(solution)/shard_map/ppermute | solution.py:137
  116.6 2.5 %collective-permute-start.8 = (f32[8,128,128]{2,1,0:T(8,128)S(1)}, f32[8,128,128]{2,1,0:T(8,128)S(1)}, u32[]{:S(2)}, u32[]{:S(2)}) collective-permute-start(f32[8,128,128]{2,1,0:T(8,128)S(1)} %multiply_add_fusion.12), channel_id=1, source_target_pairs={{0,2},{1,3},{2,4},{3,5},{4,6},{5,7},{6,8},{7,9},{8,10},{9,11},{10,... | collective-permute-start | bytes 1572872 | tf_op jit(solution)/shard_map/ppermute | solution.py:137
  119.3 1.3 collective-permute-start.15
  120.7 1.3 collective-permute-start.19
  122.0 14.7 %collective-permute-done.4 = f32[8,128,128]{2,1,0:T(8,128)S(1)} collective-permute-done((f32[8,128,128]{2,1,0:T(8,128)S(1)}, f32[8,128,128]{2,1,0:T(8,128)S(1)}, u32[]{:S(2)}, u32[]{:S(2)}) %collective-permute-start.4) | collective-permute-done | bytes 524320 | tf_op jit(solution)/shard_map/ppermute | solution.py:137
  136.8 4.9 %collective-permute-start.5 = (f32[8,128,128]{2,1,0:T(8,128)S(1)}, f32[8,128,128]{2,1,0:T(8,128)S(1)}, u32[]{:S(2)}, u32[]{:S(2)}) collective-permute-start(f32[8,128,128]{2,1,0:T(8,128)S(1)} %multiply_add_fusion.15), channel_id=1, source_target_pairs={{0,16},{1,17},{2,18},{3,19},{4,20},{5,21},{6,22},{7,23},{8,24},{9,... | collective-permute-start | bytes 1572872 | tf_op jit(solution)/shard_map/ppermute | solution.py:137
  141.9 1.3 collective-permute-start.9
  143.3 19.6 %collective-permute-done.15 = f32[8,128,128]{2,1,0:T(8,128)S(1)} collective-permute-done((f32[8,128,128]{2,1,0:T(8,128)S(1)}, f32[8,128,128]{2,1,0:T(8,128)S(1)}, u32[]{:S(2)}, u32[]{:S(2)}) %collective-permute-start.15) | collective-permute-done | bytes 524320 | tf_op jit(solution)/shard_map/ppermute | solution.py:137
  162.9 1.4 multiply_add_fusion.6
  164.4 1.2 multiply_add_fusion.2
  165.6 1.3 fusion.13
  166.9 1.8 collective-permute-start.20
  169.6 1.4 multiply_add_fusion.14
  171.0 1.2 multiply_add_fusion.10
  172.2 1.7 fusion.11
  175.1 3.3 %maximum_select_fusion.1.gs_ref = f32[32,128,128]{2,1,0:T(8,128)} fusion(f32[16,128,128]{2,1,0:T(8,128)} %collective-permute-done.20, f32[16,128,128]{2,1,0:T(8,128)S(1)} %get-tuple-element.52, pred[]{:T(512)S(6)} %eq.5), kind=kLoop, calls=%fused_computation.1 | loop fusion | flops 1572864 | bytes 4194305 | tf_op jit(solution)/shard_map/jit(_where)/select_n | solution.py:212
  178.4 1.6 maximum_select_fusion.s_ref
  180.0 13.7 %shard_map.84 = (bf16[128,4096]{1,0:T(8,128)(2,1)}, bf16[128,4096]{1,0:T(8,128)(2,1)}, bf16[128,4096]{1,0:T(8,128)(2,1)}, bf16[128,4096]{1,0:T(8,128)(2,1)}) custom-call(bf16[128,4096]{1,0:T(8,128)(2,1)} %q_ref.1, bf16[128,4096]{1,0:T(8,128)(2,1)} %k_ref.1, bf16[128,4096]{1,0:T(8,128)(2,1)} %v_ref.1, bf16[128,4096]{1,0:T(8,128)(2,1)} %g_ref.1, ...), custom_call_target="tpu_custom_call" | custom-call | tf_op jit(solution)/shard_map/pallas_call | solution.py:93
  (73 shorter events, 6.4 us)
Async XLA Ops:
  7.2 3.8 %copy-start.7 = (bf16[128,4096]{1,0:T(8,128)(2,1)S(1)}, bf16[128,4096]{1,0:T(8,128)(2,1)}, u32[]{:S(2)}) copy-start(bf16[128,4096]{1,0:T(8,128)(2,1)} %g_ref.1) | copy-start | bytes 3145732
  7.2 68.9 %all-gather.2.cloned.1.call-start = ((), (), s32[]{:S(2)}) async-start(), calls=%async_computation | async-start | bytes 1081344 | tf_op jit(solution)/shard_map/all_gather | solution.py:176
  13.8 6.8 %copy-start = (f32[32,128,128]{2,1,0:T(8,128)}, f32[32,128,128]{2,1,0:T(8,128)S(1)}, u32[]{:S(2)}) copy-start(f32[32,128,128]{2,1,0:T(8,128)S(1)} %fusion) | copy-start | bytes 6291460
  13.8 4.3 %copy-start.8 = (bf16[128,32]{0,1:T(8,128)(2,1)S(1)}, bf16[128,32]{0,1:T(8,128)(2,1)}, u32[]{:S(2)}) copy-start(bf16[128,32]{0,1:T(8,128)(2,1)} %param.11) | copy-start | bytes 24580
  13.8 5.1 %copy-start.6 = (bf16[128,4096]{1,0:T(8,128)(2,1)S(1)}, bf16[128,4096]{1,0:T(8,128)(2,1)}, u32[]{:S(2)}) copy-start(bf16[128,4096]{1,0:T(8,128)(2,1)} %k_ref.1) | copy-start | bytes 3145732
  14.9 12.3 %collective-permute-start.11 = (f32[16,128,128]{2,1,0:T(8,128)}, f32[16,128,128]{2,1,0:T(8,128)}, u32[]{:S(2)}, u32[]{:S(2)}) collective-permute-start(f32[16,128,128]{2,1,0:T(8,128)} %constant_dynamic-slice_fusion.18), channel_id=1, source_target_pairs={{0,1},{1,0},{2,3},{3,2},{4,5},{5,4},{6,7},{7,6},{8,9},{9,8},{10,11... | collective-permute-start | bytes 3145736 | tf_op jit(solution)/shard_map/ppermute | solution.py:162
  24.7 8.0 %collective-permute-start.1 = (f32[16,128,128]{2,1,0:T(8,128)}, f32[16,128,128]{2,1,0:T(8,128)S(1)}, u32[]{:S(2)}, u32[]{:S(2)}) collective-permute-start(f32[16,128,128]{2,1,0:T(8,128)} %constant_dynamic-slice_fusion.19), channel_id=1, source_target_pairs={{0,1},{1,0},{2,3},{3,2},{4,5},{5,4},{6,7},{7,6},{8,9},{9,8},{10,11... | collective-permute-start | bytes 3145736 | tf_op jit(solution)/shard_map/ppermute | solution.py:162
  24.8 2.3 %collective-permute-start = (f32[32]{0:T(128)S(1)}, f32[32]{0:T(128)S(1)}, u32[]{:S(2)}, u32[]{:S(2)}) collective-permute-start(f32[32]{0:T(128)S(1)} %convert_reduce_fusion), channel_id=1, source_target_pairs={{0,1},{1,0},{2,3},{3,2},{4,5},{5,4},{6,7},{7,6},{8,9},{9,8},{10,11... | collective-permute-start | bytes 392 | tf_op jit(solution)/shard_map/ppermute | solution.py:162
  28.9 6.1 %copy-start.2 = (f32[16,128,128]{2,1,0:T(8,128)}, f32[16,128,128]{2,1,0:T(8,128)S(1)}, u32[]{:S(2)}) copy-start(f32[16,128,128]{2,1,0:T(8,128)S(1)} %multiply_add_fusion) | copy-start | bytes 3145732
  30.1 47.2 %collective-permute-start.12 = (f32[8,128,128]{2,1,0:T(8,128)}, f32[8,128,128]{2,1,0:T(8,128)}, u32[]{:S(2)}, u32[]{:S(2)}) collective-permute-start(f32[8,128,128]{2,1,0:T(8,128)} %get-tuple-element.58), channel_id=1, source_target_pairs={{2,0},{3,1},{4,2},{5,3},{6,4},{7,5},{8,6},{9,7},{10,8},{11,9},{12,... | collective-permute-start | bytes 1572872 | tf_op jit(solution)/shard_map/ppermute | solution.py:137
  31.4 45.9 %collective-permute-start.16 = (f32[8,128,128]{2,1,0:T(8,128)}, f32[8,128,128]{2,1,0:T(8,128)}, u32[]{:S(2)}, u32[]{:S(2)}) collective-permute-start(f32[8,128,128]{2,1,0:T(8,128)} %get-tuple-element.59), channel_id=1, source_target_pairs={{8,0},{9,1},{10,2},{11,3},{12,4},{13,5},{14,6},{15,7},{16,8},{17,9... | collective-permute-start | bytes 1572872 | tf_op jit(solution)/shard_map/ppermute | solution.py:137
  32.7 1.0 copy-start.4
  36.1 45.8 %collective-permute-start.2 = (f32[8,128,128]{2,1,0:T(8,128)}, f32[8,128,128]{2,1,0:T(8,128)}, u32[]{:S(2)}, u32[]{:S(2)}) collective-permute-start(f32[8,128,128]{2,1,0:T(8,128)} %get-tuple-element.62), channel_id=1, source_target_pairs={{0,2},{1,3},{2,4},{3,5},{4,6},{5,7},{6,8},{7,9},{8,10},{9,11},{10,... | collective-permute-start | bytes 1572872 | tf_op jit(solution)/shard_map/ppermute | solution.py:137
  40.9 41.1 %collective-permute-start.6 = (f32[8,128,128]{2,1,0:T(8,128)}, f32[8,128,128]{2,1,0:T(8,128)}, u32[]{:S(2)}, u32[]{:S(2)}) collective-permute-start(f32[8,128,128]{2,1,0:T(8,128)} %get-tuple-element.63), channel_id=1, source_target_pairs={{0,8},{1,9},{2,10},{3,11},{4,12},{5,13},{6,14},{7,15},{8,16},{9,17... | collective-permute-start | bytes 1572872 | tf_op jit(solution)/shard_map/ppermute | solution.py:137
  79.0 16.7 %collective-permute-start.13 = (f32[8,128,128]{2,1,0:T(8,128)S(1)}, f32[8,128,128]{2,1,0:T(8,128)S(1)}, u32[]{:S(2)}, u32[]{:S(2)}) collective-permute-start(f32[8,128,128]{2,1,0:T(8,128)S(1)} %get-tuple-element.56), channel_id=1, source_target_pairs={{4,0},{5,1},{6,2},{7,3},{8,4},{9,5},{10,6},{11,7},{12,8},{13,9},{1... | collective-permute-start | bytes 1572872 | tf_op jit(solution)/shard_map/ppermute | solution.py:137
  80.6 17.1 %collective-permute-start.17 = (f32[8,128,128]{2,1,0:T(8,128)S(1)}, f32[8,128,128]{2,1,0:T(8,128)S(1)}, u32[]{:S(2)}, u32[]{:S(2)}) collective-permute-start(f32[8,128,128]{2,1,0:T(8,128)S(1)} %get-tuple-element.57), channel_id=1, source_target_pairs={{16,0},{17,1},{18,2},{19,3},{20,4},{21,5},{22,6},{23,7},{24,8},{25... | collective-permute-start | bytes 1572872 | tf_op jit(solution)/shard_map/ppermute | solution.py:137
  83.3 16.3 %collective-permute-start.3 = (f32[8,128,128]{2,1,0:T(8,128)S(1)}, f32[8,128,128]{2,1,0:T(8,128)S(1)}, u32[]{:S(2)}, u32[]{:S(2)}) collective-permute-start(f32[8,128,128]{2,1,0:T(8,128)S(1)} %get-tuple-element.60), channel_id=1, source_target_pairs={{0,4},{1,5},{2,6},{3,7},{4,8},{5,9},{6,10},{7,11},{8,12},{9,13},{1... | collective-permute-start | bytes 1572872 | tf_op jit(solution)/shard_map/ppermute | solution.py:137
  88.9 27.6 %collective-permute-start.7 = (f32[8,128,128]{2,1,0:T(8,128)S(1)}, f32[8,128,128]{2,1,0:T(8,128)S(1)}, u32[]{:S(2)}, u32[]{:S(2)}) collective-permute-start(f32[8,128,128]{2,1,0:T(8,128)S(1)} %get-tuple-element.61), channel_id=1, source_target_pairs={{0,16},{1,17},{2,18},{3,19},{4,20},{5,21},{6,22},{7,23},{8,24},{9,... | collective-permute-start | bytes 1572872 | tf_op jit(solution)/shard_map/ppermute | solution.py:137
  95.8 23.3 %collective-permute-start.14 = (f32[8,128,128]{2,1,0:T(8,128)S(1)}, f32[8,128,128]{2,1,0:T(8,128)S(1)}, u32[]{:S(2)}, u32[]{:S(2)}) collective-permute-start(f32[8,128,128]{2,1,0:T(8,128)S(1)} %multiply_add_fusion.8), channel_id=1, source_target_pairs={{8,0},{9,1},{10,2},{11,3},{12,4},{13,5},{14,6},{15,7},{16,8},{17,9... | collective-permute-start | bytes 1572872 | tf_op jit(solution)/shard_map/ppermute | solution.py:137
  97.9 22.7 %collective-permute-start.18 = (f32[8,128,128]{2,1,0:T(8,128)S(1)}, f32[8,128,128]{2,1,0:T(8,128)S(1)}, u32[]{:S(2)}, u32[]{:S(2)}) collective-permute-start(f32[8,128,128]{2,1,0:T(8,128)S(1)} %multiply_add_fusion.4), channel_id=1, source_target_pairs={{2,0},{3,1},{4,2},{5,3},{6,4},{7,5},{8,6},{9,7},{10,8},{11,9},{12,... | collective-permute-start | bytes 1572872 | tf_op jit(solution)/shard_map/ppermute | solution.py:137
  99.7 37.0 %collective-permute-start.4 = (f32[8,128,128]{2,1,0:T(8,128)S(1)}, f32[8,128,128]{2,1,0:T(8,128)S(1)}, u32[]{:S(2)}, u32[]{:S(2)}) collective-permute-start(f32[8,128,128]{2,1,0:T(8,128)S(1)} %multiply_add_fusion.16), channel_id=1, source_target_pairs={{0,8},{1,9},{2,10},{3,11},{4,12},{5,13},{6,14},{7,15},{8,16},{9,17... | collective-permute-start | bytes 1572872 | tf_op jit(solution)/shard_map/ppermute | solution.py:137
  116.6 25.1 %collective-permute-start.8 = (f32[8,128,128]{2,1,0:T(8,128)S(1)}, f32[8,128,128]{2,1,0:T(8,128)S(1)}, u32[]{:S(2)}, u32[]{:S(2)}) collective-permute-start(f32[8,128,128]{2,1,0:T(8,128)S(1)} %multiply_add_fusion.12), channel_id=1, source_target_pairs={{0,2},{1,3},{2,4},{3,5},{4,6},{5,7},{6,8},{7,9},{8,10},{9,11},{10,... | collective-permute-start | bytes 1572872 | tf_op jit(solution)/shard_map/ppermute | solution.py:137
  119.3 43.6 %collective-permute-start.15 = (f32[8,128,128]{2,1,0:T(8,128)S(1)}, f32[8,128,128]{2,1,0:T(8,128)S(1)}, u32[]{:S(2)}, u32[]{:S(2)}) collective-permute-start(f32[8,128,128]{2,1,0:T(8,128)S(1)} %multiply_add_fusion.7), channel_id=1, source_target_pairs={{16,0},{17,1},{18,2},{19,3},{20,4},{21,5},{22,6},{23,7},{24,8},{25... | collective-permute-start | bytes 1572872 | tf_op jit(solution)/shard_map/ppermute | solution.py:137
  120.7 43.7 %collective-permute-start.19 = (f32[8,128,128]{2,1,0:T(8,128)S(1)}, f32[8,128,128]{2,1,0:T(8,128)S(1)}, u32[]{:S(2)}, u32[]{:S(2)}) collective-permute-start(f32[8,128,128]{2,1,0:T(8,128)S(1)} %multiply_add_fusion.3), channel_id=1, source_target_pairs={{4,0},{5,1},{6,2},{7,3},{8,4},{9,5},{10,6},{11,7},{12,8},{13,9},{1... | collective-permute-start | bytes 1572872 | tf_op jit(solution)/shard_map/ppermute | solution.py:137
  136.8 32.7 %collective-permute-start.5 = (f32[8,128,128]{2,1,0:T(8,128)S(1)}, f32[8,128,128]{2,1,0:T(8,128)S(1)}, u32[]{:S(2)}, u32[]{:S(2)}) collective-permute-start(f32[8,128,128]{2,1,0:T(8,128)S(1)} %multiply_add_fusion.15), channel_id=1, source_target_pairs={{0,16},{1,17},{2,18},{3,19},{4,20},{5,21},{6,22},{7,23},{8,24},{9,... | collective-permute-start | bytes 1572872 | tf_op jit(solution)/shard_map/ppermute | solution.py:137
  141.9 29.0 %collective-permute-start.9 = (f32[8,128,128]{2,1,0:T(8,128)S(1)}, f32[8,128,128]{2,1,0:T(8,128)S(1)}, u32[]{:S(2)}, u32[]{:S(2)}) collective-permute-start(f32[8,128,128]{2,1,0:T(8,128)S(1)} %multiply_add_fusion.11), channel_id=1, source_target_pairs={{0,4},{1,5},{2,6},{3,7},{4,8},{5,9},{6,10},{7,11},{8,12},{9,13},{1... | collective-permute-start | bytes 1572872 | tf_op jit(solution)/shard_map/ppermute | solution.py:137
  162.9 2.7 %copy-start.1 = (f32[32,128,128]{2,1,0:T(8,128)S(1)}, f32[32,128,128]{2,1,0:T(8,128)}, u32[]{:S(2)}) copy-start(f32[32,128,128]{2,1,0:T(8,128)} %copy-done) | copy-start | bytes 6291460
  166.9 8.1 %collective-permute-start.20 = (f32[16,128,128]{2,1,0:T(8,128)}, f32[16,128,128]{2,1,0:T(8,128)}, u32[]{:S(2)}, u32[]{:S(2)}) collective-permute-start(f32[16,128,128]{2,1,0:T(8,128)} %get-tuple-element.53), channel_id=1, source_target_pairs={{0,1},{1,0},{2,3},{3,2},{4,5},{5,4},{6,7},{7,6},{8,9},{9,8},{10,11... | collective-permute-start | bytes 3145736 | tf_op jit(solution)/shard_map/ppermute | solution.py:209
  169.6 2.6 %copy-start.5 = (f32[16,128,128]{2,1,0:T(8,128)S(1)}, f32[16,128,128]{2,1,0:T(8,128)}, u32[]{:S(2)}) copy-start(f32[16,128,128]{2,1,0:T(8,128)} %copy-done.4) | copy-start | bytes 3145732
  173.9 4.5 %collective-permute-start.10 = (f32[16,128,128]{2,1,0:T(8,128)}, f32[16,128,128]{2,1,0:T(8,128)S(1)}, u32[]{:S(2)}, u32[]{:S(2)}) collective-permute-start(f32[16,128,128]{2,1,0:T(8,128)} %get-tuple-element.55), channel_id=1, source_target_pairs={{0,1},{1,0},{2,3},{3,2},{4,5},{5,4},{6,7},{7,6},{8,9},{9,8},{10,11... | collective-permute-start | bytes 3145736 | tf_op jit(solution)/shard_map/ppermute | solution.py:209
  175.1 3.3 %copy-start.3 = (f32[16,128,128]{2,1,0:T(8,128)S(1)}, f32[16,128,128]{2,1,0:T(8,128)}, u32[]{:S(2)}) copy-start(f32[16,128,128]{2,1,0:T(8,128)} %get-tuple-element.54) | copy-start | bytes 3145732
Sparse Core Ops, SparseCore 0:
  19.0 57.0 all-gather.1

commit v3 on v1

--- a/solution.py
+++ b/solution.py
@@ -104,12 +104,14 @@
     count = lax.axis_size(axis)
     me = lax.axis_index(axis)
     known = row[None]
+    early = None
     step = 1
     while step < count:
         pairs = [(i, (i + step) % count) for i in range(count)]
         known = jnp.concatenate([known, lax.ppermute(known, axis, pairs)], 0)
+        early = known if early is None else early
         step *= 2
-    return known[(me - jnp.arange(count)) % count]
+    return known[(me - jnp.arange(count)) % count], early
 
 
 def window_sum(ordered, place, first, last):
@@ -145,7 +147,11 @@
 
 def shards(queries, key_vectors, values, out_grad, log_decay):
     axis = "ctx"
-    total, state, grad_state, pieces = prepare(queries, key_vectors, values, out_grad, log_decay)
+    total = jnp.sum(log_decay.astype(jnp.float32), axis=0)
+    every_total, early = gather_rows(total, axis)
+    _, queries, key_vectors, values, out_grad = lax.optimization_barrier(
+        (early, queries, key_vectors, values, out_grad))
+    _, state, grad_state, pieces = prepare(queries, key_vectors, values, out_grad, log_decay)
     heads = total.shape[0]
     half = heads // 2
     chips = lax.axis_size(axis) // 2
@@ -172,7 +178,6 @@
     bwd_a = jnp.where(first, one, jnp.exp(other_total_half))[:, None, None]
     bwd_b = jnp.where(first, jnp.exp(own_total_half), one)[:, None, None]
     chip_grad = bwd_a * mine_grad + bwd_b * other_grad
-    every_total = gather_rows(total, axis)
     chip_totals = every_total[0::2] + every_total[1::2]
     chip = lax.axis_index(axis) // 2
     steps = []

time: 178 us -> 176 us (0.989)
  starting transfers between devices: 45.7 us -> 52.6 us
  waiting for transfers between devices: 84.8 us -> 78.8 us
    ppermute x5, waiting for transfers between devices: 19.1 us -> 12 us  [gather_rows(): known = jnp.concatenate([known, lax.ppermute(known, axis, pairs)], 0)]
    ppermute x3, starting transfers between devices: 4.34 us -> 8.34 us  [shards(): other_total, other_state, other_grad = lax.ppermute(sent, axis, partner)]
    ppermute x16, starting transfers between devices: 39.2 us -> 41.5 us  [chip_scan(): received = lax.ppermute(sent, axis, pairs)]
    unnamed x14 -> x16, local copies, waits for them, and re-layouts: 2.97 us -> 3.93 us
  transfers between devices with their start and end apart: 26 -> 26, of which waited for: 10 -> 10; matrix products, arithmetic and copies ran while one was open for 15% -> 13% of each run, Pallas kernels for 0% -> 0%
where the time goes in v3:
time: 176 us
  waiting for transfers between devices  78.8 us (45%)
  starting transfers between devices  52.6 us (30%)
  Pallas kernels  13.7 us (8%)
  other arithmetic  13.6 us (8%)
  local copies, waits for them, and re-layouts  11.7 us (7%)
  matrix products  4.02 us (2%)
    ppermute x16, waiting for transfers between devices, chip_scan(): received = lax.ppermute(sent, axis, pairs)  66.8 us
    ppermute x16, starting transfers between devices, chip_scan(): received = lax.ppermute(sent, axis, pairs)  41.5 us
    pallas_call x1, Pallas kernels, finish(): pl.pallas_call(head_kernel, grid=(heads // block,), in_specs=[tile] * 4 +...  13.7 us
    ppermute x5, waiting for transfers between devices, gather_rows(): known = jnp.concatenate([known, lax.ppermute(known, axis, pairs)], 0)  12 us
    ppermute x3, starting transfers between devices, shards(): other_total, other_state, other_grad = lax.ppermute(sent, axis, partner)  8.34 us
    select_n x2, other arithmetic, assemble(): jnp.where(first, jnp.concatenate([keep, got], 0), jnp.concatenate([got, k...  4.8 us
    unnamed x16, local copies, waits for them, and re-layouts  3.93 us
  transfers between devices with their start and end apart: 26, of which 10 were waited for; matrix products, arithmetic and copies ran while one was open for 13% of the time, Pallas kernels for 0%

profile of v3, /device:TPU:1, one launch (start us, length us, event | category | flops | bytes accessed | tf_op | source)
XLA Modules:
  0.0 175.6 jit_solution(13953532296250982792)
XLA Ops:
  0.6 0.9 convert_reduce_fusion
  1.5 3.3 %collective-permute-start.1 = (f32[32]{0:T(128)S(1)}, f32[32]{0:T(128)S(1)}, u32[]{:S(2)}, u32[]{:S(2)}) collective-permute-start(f32[32]{0:T(128)S(1)} %convert_reduce_fusion), channel_id=1, source_target_pairs={{0,1},{1,0},{2,3},{3,2},{4,5},{5,4},{6,7},{7,6},{8,9},{9,8},{10,11... | collective-permute-start | bytes 392 | tf_op jit(solution)/shard_map/ppermute | solution.py:168
  4.9 0.8 copy.9
  6.1 0.7 collective-permute-start.4
  6.9 1.5 copy.18
  8.4 1.3 fusion
  9.6 1.3 copy-done
  11.0 1.0 constant_dynamic-slice_fusion.18
  12.0 4.5 %collective-permute-start.16 = (f32[16,128,128]{2,1,0:T(8,128)}, f32[16,128,128]{2,1,0:T(8,128)}, u32[]{:S(2)}, u32[]{:S(2)}) collective-permute-start(f32[16,128,128]{2,1,0:T(8,128)} %constant_dynamic-slice_fusion.18), channel_id=1, source_target_pairs={{0,1},{1,0},{2,3},{3,2},{4,5},{5,4},{6,7},{7,6},{8,9},{9,8},{10,11... | collective-permute-start | bytes 3145736 | tf_op jit(solution)/shard_map/ppermute | solution.py:168
  16.5 1.6 copy.17
  18.1 2.8 %fusion.2 = f32[32,128,128]{2,1,0:T(8,128)S(1)} fusion(f32[128,32,128]{0,2,1:T(8,128)} %bitcast.167, f32[128,32]{0,1:T(8,128)S(1)} %copy.11, bf16[128,4096]{1,0:T(8,128)(2,1)S(1)} %copy-done.6), kind=kOutput, calls=%fused_computation.5 | convolution fusion | flops 805830656 | bytes 5259264 | tf_op jit(solution)/shard_map/she,shf->hef/dot_general | solution.py:27
  21.0 1.0 constant_dynamic-slice_fusion.19
  22.6 4.4 %collective-permute-done.5 = f32[4,32]{1,0:T(4,128)S(1)} collective-permute-done((f32[4,32]{1,0:T(4,128)S(1)}, f32[4,32]{1,0:T(4,128)S(1)}, u32[]{:S(2)}, u32[]{:S(2)}) %collective-permute-start.5) | collective-permute-done | bytes 544 | tf_op jit(solution)/shard_map/ppermute | solution.py:111
  27.2 3.6 %collective-permute-done.6 = f32[8,32]{1,0:T(8,128)S(1)} collective-permute-done((f32[8,32]{1,0:T(8,128)S(1)}, f32[8,32]{1,0:T(8,128)S(1)}, u32[]{:S(2)}, u32[]{:S(2)}) %collective-permute-start.6) | collective-permute-done | bytes 1056 | tf_op jit(solution)/shard_map/ppermute | solution.py:111
  30.9 4.0 %collective-permute-done.7 = f32[16,32]{1,0:T(8,128)S(1)} collective-permute-done((f32[16,32]{1,0:T(8,128)S(1)}, f32[16,32]{1,0:T(8,128)S(1)}, u32[]{:S(2)}, u32[]{:S(2)}) %collective-permute-start.7) | collective-permute-done | bytes 2080 | tf_op jit(solution)/shard_map/ppermute | solution.py:111
  36.0 1.7 multiply_add_fusion
  37.8 1.3 collective-permute-start.17
  39.1 1.3 collective-permute-start.21
  41.4 4.0 %collective-permute-start.3 = (f32[8,128,128]{2,1,0:T(8,128)S(1)}, f32[8,128,128]{2,1,0:T(8,128)S(1)}, u32[]{:S(2)}, u32[]{:S(2)}) collective-permute-start(f32[8,128,128]{2,1,0:T(8,128)S(1)} %get-tuple-element.58), channel_id=1, source_target_pairs={{0,2},{1,3},{2,4},{3,5},{4,6},{5,7},{6,8},{7,9},{8,10},{9,11},{10,... | collective-permute-start | bytes 1572872 | tf_op jit(solution)/shard_map/ppermute | solution.py:139
  45.4 4.0 %collective-permute-start.11 = (f32[8,128,128]{2,1,0:T(8,128)S(1)}, f32[8,128,128]{2,1,0:T(8,128)S(1)}, u32[]{:S(2)}, u32[]{:S(2)}) collective-permute-start(f32[8,128,128]{2,1,0:T(8,128)S(1)} %get-tuple-element.59), channel_id=1, source_target_pairs={{0,8},{1,9},{2,10},{3,11},{4,12},{5,13},{6,14},{7,15},{8,16},{9,17... | collective-permute-start | bytes 1572872 | tf_op jit(solution)/shard_map/ppermute | solution.py:139
  49.4 2.2 %collective-permute-done.21 = f32[8,128,128]{2,1,0:T(8,128)S(1)} collective-permute-done((f32[8,128,128]{2,1,0:T(8,128)S(1)}, f32[8,128,128]{2,1,0:T(8,128)S(1)}, u32[]{:S(2)}, u32[]{:S(2)}) %collective-permute-start.21) | collective-permute-done | bytes 524320 | tf_op jit(solution)/shard_map/ppermute | solution.py:139
  51.8 1.3 collective-permute-start.18
  53.2 1.3 collective-permute-start.22
  54.5 14.4 %collective-permute-done.11 = f32[8,128,128]{2,1,0:T(8,128)S(1)} collective-permute-done((f32[8,128,128]{2,1,0:T(8,128)S(1)}, f32[8,128,128]{2,1,0:T(8,128)S(1)}, u32[]{:S(2)}, u32[]{:S(2)}) %collective-permute-start.11) | collective-permute-done | bytes 524320 | tf_op jit(solution)/shard_map/ppermute | solution.py:139
  69.1 1.3 collective-permute-start.8
  70.4 6.8 %collective-permute-start.12 = (f32[8,128,128]{2,1,0:T(8,128)S(1)}, f32[8,128,128]{2,1,0:T(8,128)S(1)}, u32[]{:S(2)}, u32[]{:S(2)}) collective-permute-start(f32[8,128,128]{2,1,0:T(8,128)S(1)} %get-tuple-element.57), channel_id=1, source_target_pairs={{0,16},{1,17},{2,18},{3,19},{4,20},{5,21},{6,22},{7,23},{8,24},{9,... | collective-permute-start | bytes 1572872 | tf_op jit(solution)/shard_map/ppermute | solution.py:139
  77.3 1.3 collective-permute-start.19
  78.6 16.7 %collective-permute-done.22 = f32[8,128,128]{2,1,0:T(8,128)S(1)} collective-permute-done((f32[8,128,128]{2,1,0:T(8,128)S(1)}, f32[8,128,128]{2,1,0:T(8,128)S(1)}, u32[]{:S(2)}, u32[]{:S(2)}) %collective-permute-start.22) | collective-permute-done | bytes 524320 | tf_op jit(solution)/shard_map/ppermute | solution.py:139
  95.4 1.3 collective-permute-start.23
  96.9 1.3 collective-permute-start.9
  98.2 0.7 collective-permute-done.12
  99.1 3.4 %collective-permute-start.13 = (f32[8,128,128]{2,1,0:T(8,128)S(1)}, f32[8,128,128]{2,1,0:T(8,128)S(1)}, u32[]{:S(2)}, u32[]{:S(2)}) collective-permute-start(f32[8,128,128]{2,1,0:T(8,128)S(1)} %multiply_add_fusion.12), channel_id=1, source_target_pairs={{0,2},{1,3},{2,4},{3,5},{4,6},{5,7},{6,8},{7,9},{8,10},{9,11},{10,... | collective-permute-start | bytes 1572872 | tf_op jit(solution)/shard_map/ppermute | solution.py:139
  102.6 1.3 collective-permute-start.20
  103.9 6.4 %collective-permute-done.23 = f32[8,128,128]{2,1,0:T(8,128)S(1)} collective-permute-done((f32[8,128,128]{2,1,0:T(8,128)S(1)}, f32[8,128,128]{2,1,0:T(8,128)S(1)}, u32[]{:S(2)}, u32[]{:S(2)}) %collective-permute-start.23) | collective-permute-done | bytes 524320 | tf_op jit(solution)/shard_map/ppermute | solution.py:139
  110.5 1.5 collective-permute-start.24
  111.9 6.8 %collective-permute-done.9 = f32[8,128,128]{2,1,0:T(8,128)S(1)} collective-permute-done((f32[8,128,128]{2,1,0:T(8,128)S(1)}, f32[8,128,128]{2,1,0:T(8,128)S(1)}, u32[]{:S(2)}, u32[]{:S(2)}) %collective-permute-start.9) | collective-permute-done | bytes 524320 | tf_op jit(solution)/shard_map/ppermute | solution.py:139
  118.8 8.9 %collective-permute-start.10 = (f32[8,128,128]{2,1,0:T(8,128)S(1)}, f32[8,128,128]{2,1,0:T(8,128)S(1)}, u32[]{:S(2)}, u32[]{:S(2)}) collective-permute-start(f32[8,128,128]{2,1,0:T(8,128)S(1)} %multiply_add_fusion.15), channel_id=1, source_target_pairs={{0,16},{1,17},{2,18},{3,19},{4,20},{5,21},{6,22},{7,23},{8,24},{9,... | collective-permute-start | bytes 1572872 | tf_op jit(solution)/shard_map/ppermute | solution.py:139
  127.8 1.3 collective-permute-start.14
  129.2 19.6 %collective-permute-done.20 = f32[8,128,128]{2,1,0:T(8,128)S(1)} collective-permute-done((f32[8,128,128]{2,1,0:T(8,128)S(1)}, f32[8,128,128]{2,1,0:T(8,128)S(1)}, u32[]{:S(2)}, u32[]{:S(2)}) %collective-permute-start.20) | collective-permute-done | bytes 524320 | tf_op jit(solution)/shard_map/ppermute | solution.py:139
  149.3 1.1 copy-done.1
  150.4 1.3 fusion.13
  151.7 1.7 collective-permute-start.25
  153.9 0.8 copy-done.4
  154.7 1.6 fusion.11
  156.3 0.7 copy.10
  157.0 3.3 %maximum_select_fusion.1.gs_ref = f32[32,128,128]{2,1,0:T(8,128)} fusion(f32[16,128,128]{2,1,0:T(8,128)} %collective-permute-done.25, f32[16,128,128]{2,1,0:T(8,128)S(1)} %get-tuple-element.48, pred[]{:T(512)S(6)} %eq.7), kind=kLoop, calls=%fused_computation.2 | loop fusion | flops 1572864 | bytes 4194305 | tf_op jit(solution)/shard_map/jit(_where)/select_n | solution.py:216
  160.3 1.5 maximum_select_fusion.s_ref
  161.8 13.7 %shard_map.84 = (bf16[128,4096]{1,0:T(8,128)(2,1)}, bf16[128,4096]{1,0:T(8,128)(2,1)}, bf16[128,4096]{1,0:T(8,128)(2,1)}, bf16[128,4096]{1,0:T(8,128)(2,1)}) custom-call(bf16[128,4096]{1,0:T(8,128)(2,1)} %q_ref, bf16[128,4096]{1,0:T(8,128)(2,1)} %k_ref, bf16[128,4096]{1,0:T(8,128)(2,1)} %v_ref, bf16[128,4096]{1,0:T(8,128)(2,1)} %g_ref, f32[32,128]{1,0:T(8,128)} %bitcast.168, ...), custom_call_target="tpu_custom_call" | custom-call | tf_op jit(solution)/shard_map/pallas_call | solution.py:93
  (84 shorter events, 5.8 us)
Async XLA Ops:
  0.6 7.7 %copy-start.7 = (bf16[128,4096]{1,0:T(8,128)(2,1)S(1)}, bf16[128,4096]{1,0:T(8,128)(2,1)}, u32[]{:S(2)}) copy-start(bf16[128,4096]{1,0:T(8,128)(2,1)} %g_ref) | copy-start | bytes 3145732
  1.5 25.6 %collective-permute-start.1 = (f32[32]{0:T(128)S(1)}, f32[32]{0:T(128)S(1)}, u32[]{:S(2)}, u32[]{:S(2)}) collective-permute-start(f32[32]{0:T(128)S(1)} %convert_reduce_fusion), channel_id=1, source_target_pairs={{0,1},{1,0},{2,3},{3,2},{4,5},{5,4},{6,7},{7,6},{8,9},{9,8},{10,11... | collective-permute-start | bytes 392 | tf_op jit(solution)/shard_map/ppermute | solution.py:168
  4.9 1.2 collective-permute-start
  6.1 14.8 %collective-permute-start.4 = (f32[2,32]{1,0:T(2,128)S(1)}, f32[2,32]{1,0:T(2,128)S(1)}, u32[]{:S(2)}, u32[]{:S(2)}) collective-permute-start(f32[2,32]{1,0:T(2,128)S(1)} %pad_maximum_fusion.4), channel_id=1, source_target_pairs={{0,2},{1,3},{2,4},{3,5},{4,6},{5,7},{6,8},{7,9},{8,10},{9,11},{10,... | collective-permute-start | bytes 776 | tf_op jit(solution)/shard_map/ppermute | solution.py:111
  9.6 1.3 copy-start
  11.0 5.5 %copy-start.5 = (bf16[128,4096]{1,0:T(8,128)(2,1)S(1)}, bf16[128,4096]{1,0:T(8,128)(2,1)}, u32[]{:S(2)}) copy-start(bf16[128,4096]{1,0:T(8,128)(2,1)} %k_ref) | copy-start | bytes 3145732
  12.0 6.1 %copy-start.6 = (bf16[128,4096]{1,0:T(8,128)(2,1)S(1)}, bf16[128,4096]{1,0:T(8,128)(2,1)}, u32[]{:S(2)}) copy-start(bf16[128,4096]{1,0:T(8,128)(2,1)} %v_ref) | copy-start | bytes 3145732
  12.0 23.9 %collective-permute-start.16 = (f32[16,128,128]{2,1,0:T(8,128)}, f32[16,128,128]{2,1,0:T(8,128)}, u32[]{:S(2)}, u32[]{:S(2)}) collective-permute-start(f32[16,128,128]{2,1,0:T(8,128)} %constant_dynamic-slice_fusion.18), channel_id=1, source_target_pairs={{0,1},{1,0},{2,3},{3,2},{4,5},{5,4},{6,7},{7,6},{8,9},{9,8},{10,11... | collective-permute-start | bytes 3145736 | tf_op jit(solution)/shard_map/ppermute | solution.py:168
  20.9 6.1 %collective-permute-start.5 = (f32[4,32]{1,0:T(4,128)S(1)}, f32[4,32]{1,0:T(4,128)S(1)}, u32[]{:S(2)}, u32[]{:S(2)}) collective-permute-start(f32[4,32]{1,0:T(4,128)S(1)} %pad_maximum_fusion.3), channel_id=1, source_target_pairs={{0,4},{1,5},{2,6},{3,7},{4,8},{5,9},{6,10},{7,11},{8,12},{9,13},{1... | collective-permute-start | bytes 1544 | tf_op jit(solution)/shard_map/ppermute | solution.py:111
  22.1 18.3 %collective-permute-start.2 = (f32[16,128,128]{2,1,0:T(8,128)}, f32[16,128,128]{2,1,0:T(8,128)S(1)}, u32[]{:S(2)}, u32[]{:S(2)}) collective-permute-start(f32[16,128,128]{2,1,0:T(8,128)} %constant_dynamic-slice_fusion.19), channel_id=1, source_target_pairs={{0,1},{1,0},{2,3},{3,2},{4,5},{5,4},{6,7},{7,6},{8,9},{9,8},{10,11... | collective-permute-start | bytes 3145736 | tf_op jit(solution)/shard_map/ppermute | solution.py:168
  27.1 3.7 %collective-permute-start.6 = (f32[8,32]{1,0:T(8,128)S(1)}, f32[8,32]{1,0:T(8,128)S(1)}, u32[]{:S(2)}, u32[]{:S(2)}) collective-permute-start(f32[8,32]{1,0:T(8,128)S(1)} %pad_maximum_fusion.2), channel_id=1, source_target_pairs={{0,8},{1,9},{2,10},{3,11},{4,12},{5,13},{6,14},{7,15},{8,16},{9,17... | collective-permute-start | bytes 3080 | tf_op jit(solution)/shard_map/ppermute | solution.py:111
  30.8 4.1 %collective-permute-start.7 = (f32[16,32]{1,0:T(8,128)S(1)}, f32[16,32]{1,0:T(8,128)S(1)}, u32[]{:S(2)}, u32[]{:S(2)}) collective-permute-start(f32[16,32]{1,0:T(8,128)S(1)} %concatenate.40), channel_id=1, source_target_pairs={{0,16},{1,17},{2,18},{3,19},{4,20},{5,21},{6,22},{7,23},{8,24},{9,... | collective-permute-start | bytes 6152 | tf_op jit(solution)/shard_map/ppermute | solution.py:111
  37.8 11.6 %collective-permute-start.17 = (f32[8,128,128]{2,1,0:T(8,128)S(1)}, f32[8,128,128]{2,1,0:T(8,128)S(1)}, u32[]{:S(2)}, u32[]{:S(2)}) collective-permute-start(f32[8,128,128]{2,1,0:T(8,128)S(1)} %get-tuple-element.54), channel_id=1, source_target_pairs={{2,0},{3,1},{4,2},{5,3},{6,4},{7,5},{8,6},{9,7},{10,8},{11,9},{12,... | collective-permute-start | bytes 1572872 | tf_op jit(solution)/shard_map/ppermute | solution.py:139
  39.1 12.5 %collective-permute-start.21 = (f32[8,128,128]{2,1,0:T(8,128)S(1)}, f32[8,128,128]{2,1,0:T(8,128)S(1)}, u32[]{:S(2)}, u32[]{:S(2)}) collective-permute-start(f32[8,128,128]{2,1,0:T(8,128)S(1)} %get-tuple-element.55), channel_id=1, source_target_pairs={{8,0},{9,1},{10,2},{11,3},{12,4},{13,5},{14,6},{15,7},{16,8},{17,9... | collective-permute-start | bytes 1572872 | tf_op jit(solution)/shard_map/ppermute | solution.py:139
  40.4 1.0 copy-start.3
  41.4 13.1 %collective-permute-start.3 = (f32[8,128,128]{2,1,0:T(8,128)S(1)}, f32[8,128,128]{2,1,0:T(8,128)S(1)}, u32[]{:S(2)}, u32[]{:S(2)}) collective-permute-start(f32[8,128,128]{2,1,0:T(8,128)S(1)} %get-tuple-element.58), channel_id=1, source_target_pairs={{0,2},{1,3},{2,4},{3,5},{4,6},{5,7},{6,8},{7,9},{8,10},{9,11},{10,... | collective-permute-start | bytes 1572872 | tf_op jit(solution)/shard_map/ppermute | solution.py:139
  45.4 23.5 %collective-permute-start.11 = (f32[8,128,128]{2,1,0:T(8,128)S(1)}, f32[8,128,128]{2,1,0:T(8,128)S(1)}, u32[]{:S(2)}, u32[]{:S(2)}) collective-permute-start(f32[8,128,128]{2,1,0:T(8,128)S(1)} %get-tuple-element.59), channel_id=1, source_target_pairs={{0,8},{1,9},{2,10},{3,11},{4,12},{5,13},{6,14},{7,15},{8,16},{9,17... | collective-permute-start | bytes 1572872 | tf_op jit(solution)/shard_map/ppermute | solution.py:139
  51.8 25.4 %collective-permute-start.18 = (f32[8,128,128]{2,1,0:T(8,128)S(1)}, f32[8,128,128]{2,1,0:T(8,128)S(1)}, u32[]{:S(2)}, u32[]{:S(2)}) collective-permute-start(f32[8,128,128]{2,1,0:T(8,128)S(1)} %get-tuple-element.52), channel_id=1, source_target_pairs={{4,0},{5,1},{6,2},{7,3},{8,4},{9,5},{10,6},{11,7},{12,8},{13,9},{1... | collective-permute-start | bytes 1572872 | tf_op jit(solution)/shard_map/ppermute | solution.py:139
  53.2 42.1 %collective-permute-start.22 = (f32[8,128,128]{2,1,0:T(8,128)S(1)}, f32[8,128,128]{2,1,0:T(8,128)S(1)}, u32[]{:S(2)}, u32[]{:S(2)}) collective-permute-start(f32[8,128,128]{2,1,0:T(8,128)S(1)} %get-tuple-element.53), channel_id=1, source_target_pairs={{16,0},{17,1},{18,2},{19,3},{20,4},{21,5},{22,6},{23,7},{24,8},{25... | collective-permute-start | bytes 1572872 | tf_op jit(solution)/shard_map/ppermute | solution.py:139
  69.1 27.6 %collective-permute-start.8 = (f32[8,128,128]{2,1,0:T(8,128)S(1)}, f32[8,128,128]{2,1,0:T(8,128)S(1)}, u32[]{:S(2)}, u32[]{:S(2)}) collective-permute-start(f32[8,128,128]{2,1,0:T(8,128)S(1)} %get-tuple-element.56), channel_id=1, source_target_pairs={{0,4},{1,5},{2,6},{3,7},{4,8},{5,9},{6,10},{7,11},{8,12},{9,13},{1... | collective-permute-start | bytes 1572872 | tf_op jit(solution)/shard_map/ppermute | solution.py:139
  70.4 28.5 %collective-permute-start.12 = (f32[8,128,128]{2,1,0:T(8,128)S(1)}, f32[8,128,128]{2,1,0:T(8,128)S(1)}, u32[]{:S(2)}, u32[]{:S(2)}) collective-permute-start(f32[8,128,128]{2,1,0:T(8,128)S(1)} %get-tuple-element.57), channel_id=1, source_target_pairs={{0,16},{1,17},{2,18},{3,19},{4,20},{5,21},{6,22},{7,23},{8,24},{9,... | collective-permute-start | bytes 1572872 | tf_op jit(solution)/shard_map/ppermute | solution.py:139
  77.3 25.2 %collective-permute-start.19 = (f32[8,128,128]{2,1,0:T(8,128)S(1)}, f32[8,128,128]{2,1,0:T(8,128)S(1)}, u32[]{:S(2)}, u32[]{:S(2)}) collective-permute-start(f32[8,128,128]{2,1,0:T(8,128)S(1)} %multiply_add_fusion.8), channel_id=1, source_target_pairs={{8,0},{9,1},{10,2},{11,3},{12,4},{13,5},{14,6},{15,7},{16,8},{17,9... | collective-permute-start | bytes 1572872 | tf_op jit(solution)/shard_map/ppermute | solution.py:139
  95.4 14.9 %collective-permute-start.23 = (f32[8,128,128]{2,1,0:T(8,128)S(1)}, f32[8,128,128]{2,1,0:T(8,128)S(1)}, u32[]{:S(2)}, u32[]{:S(2)}) collective-permute-start(f32[8,128,128]{2,1,0:T(8,128)S(1)} %multiply_add_fusion.4), channel_id=1, source_target_pairs={{2,0},{3,1},{4,2},{5,3},{6,4},{7,5},{8,6},{9,7},{10,8},{11,9},{12,... | collective-permute-start | bytes 1572872 | tf_op jit(solution)/shard_map/ppermute | solution.py:139
  96.9 21.8 %collective-permute-start.9 = (f32[8,128,128]{2,1,0:T(8,128)S(1)}, f32[8,128,128]{2,1,0:T(8,128)S(1)}, u32[]{:S(2)}, u32[]{:S(2)}) collective-permute-start(f32[8,128,128]{2,1,0:T(8,128)S(1)} %multiply_add_fusion.16), channel_id=1, source_target_pairs={{0,8},{1,9},{2,10},{3,11},{4,12},{5,13},{6,14},{7,15},{8,16},{9,17... | collective-permute-start | bytes 1572872 | tf_op jit(solution)/shard_map/ppermute | solution.py:139
  99.1 28.6 %collective-permute-start.13 = (f32[8,128,128]{2,1,0:T(8,128)S(1)}, f32[8,128,128]{2,1,0:T(8,128)S(1)}, u32[]{:S(2)}, u32[]{:S(2)}) collective-permute-start(f32[8,128,128]{2,1,0:T(8,128)S(1)} %multiply_add_fusion.12), channel_id=1, source_target_pairs={{0,2},{1,3},{2,4},{3,5},{4,6},{5,7},{6,8},{7,9},{8,10},{9,11},{10,... | collective-permute-start | bytes 1572872 | tf_op jit(solution)/shard_map/ppermute | solution.py:139
  102.6 46.2 %collective-permute-start.20 = (f32[8,128,128]{2,1,0:T(8,128)S(1)}, f32[8,128,128]{2,1,0:T(8,128)S(1)}, u32[]{:S(2)}, u32[]{:S(2)}) collective-permute-start(f32[8,128,128]{2,1,0:T(8,128)S(1)} %multiply_add_fusion.7), channel_id=1, source_target_pairs={{16,0},{17,1},{18,2},{19,3},{20,4},{21,5},{22,6},{23,7},{24,8},{25... | collective-permute-start | bytes 1572872 | tf_op jit(solution)/shard_map/ppermute | solution.py:139
  110.5 38.6 %collective-permute-start.24 = (f32[8,128,128]{2,1,0:T(8,128)S(1)}, f32[8,128,128]{2,1,0:T(8,128)S(1)}, u32[]{:S(2)}, u32[]{:S(2)}) collective-permute-start(f32[8,128,128]{2,1,0:T(8,128)S(1)} %multiply_add_fusion.3), channel_id=1, source_target_pairs={{4,0},{5,1},{6,2},{7,3},{8,4},{9,5},{10,6},{11,7},{12,8},{13,9},{1... | collective-permute-start | bytes 1572872 | tf_op jit(solution)/shard_map/ppermute | solution.py:139
  118.8 34.6 %collective-permute-start.10 = (f32[8,128,128]{2,1,0:T(8,128)S(1)}, f32[8,128,128]{2,1,0:T(8,128)S(1)}, u32[]{:S(2)}, u32[]{:S(2)}) collective-permute-start(f32[8,128,128]{2,1,0:T(8,128)S(1)} %multiply_add_fusion.15), channel_id=1, source_target_pairs={{0,16},{1,17},{2,18},{3,19},{4,20},{5,21},{6,22},{7,23},{8,24},{9,... | collective-permute-start | bytes 1572872 | tf_op jit(solution)/shard_map/ppermute | solution.py:139
  127.8 25.8 %collective-permute-start.14 = (f32[8,128,128]{2,1,0:T(8,128)S(1)}, f32[8,128,128]{2,1,0:T(8,128)S(1)}, u32[]{:S(2)}, u32[]{:S(2)}) collective-permute-start(f32[8,128,128]{2,1,0:T(8,128)S(1)} %multiply_add_fusion.11), channel_id=1, source_target_pairs={{0,4},{1,5},{2,6},{3,7},{4,8},{5,9},{6,10},{7,11},{8,12},{9,13},{1... | collective-permute-start | bytes 1572872 | tf_op jit(solution)/shard_map/ppermute | solution.py:139
  148.8 1.6 copy-start.1
  151.7 5.3 %collective-permute-start.25 = (f32[16,128,128]{2,1,0:T(8,128)}, f32[16,128,128]{2,1,0:T(8,128)}, u32[]{:S(2)}, u32[]{:S(2)}) collective-permute-start(f32[16,128,128]{2,1,0:T(8,128)} %get-tuple-element.49), channel_id=1, source_target_pairs={{0,1},{1,0},{2,3},{3,2},{4,5},{5,4},{6,7},{7,6},{8,9},{9,8},{10,11... | collective-permute-start | bytes 3145736 | tf_op jit(solution)/shard_map/ppermute | solution.py:213
  153.4 1.2 copy-start.4
  156.3 4.0 %collective-permute-start.15 = (f32[16,128,128]{2,1,0:T(8,128)}, f32[16,128,128]{2,1,0:T(8,128)S(1)}, u32[]{:S(2)}, u32[]{:S(2)}) collective-permute-start(f32[16,128,128]{2,1,0:T(8,128)} %get-tuple-element.51), channel_id=1, source_target_pairs={{0,1},{1,0},{2,3},{3,2},{4,5},{5,4},{6,7},{7,6},{8,9},{9,8},{10,11... | collective-permute-start | bytes 3145736 | tf_op jit(solution)/shard_map/ppermute | solution.py:213
  157.0 3.3 %copy-start.2 = (f32[16,128,128]{2,1,0:T(8,128)S(1)}, f32[16,128,128]{2,1,0:T(8,128)}, u32[]{:S(2)}) copy-start(f32[16,128,128]{2,1,0:T(8,128)} %get-tuple-element.50) | copy-start | bytes 3145732

commit v4 on v3

--- a/solution.py
+++ b/solution.py
@@ -36,7 +36,8 @@
     return high, (x - high.astype(jnp.float32)).astype(jnp.bfloat16)
 
 
-def head_kernel(q_ref, k_ref, v_ref, g_ref, cum_ref, s_ref, gs_ref, att_ref, qg_ref, kg_ref, vg_ref):
+def head_kernel(core_ref, q_ref, k_ref, v_ref, g_ref, cum_ref, keep_ref, got_ref, keep_g_ref, got_g_ref,
+                att_ref, qg_ref, kg_ref, vg_ref):
     f32 = jnp.float32
     nn = (((1,), (0,)), ((), ()))
     nt = (((1,), (1,)), ((), ()))
@@ -56,6 +57,7 @@
     block = cum_ref.shape[0]
     dk = q_ref.shape[1] // block
     later = lax.broadcasted_iota(jnp.int32, (size, size), 0) >= lax.broadcasted_iota(jnp.int32, (size, size), 1)
+    kept = pl.program_id(0) // (keep_ref.shape[0] * 2 // block) == core_ref[0]
     for j in range(block):
         cols = slice(j * dk, (j + 1) * dk)
         q = q_ref[:, cols]
@@ -73,31 +75,36 @@
         grad_scores = mm(g, v, nt) * weights
         qd = jnp.exp(col)
         kd = jnp.exp(last - col)
-        state = s_ref[j]
-        grad_in = gs_ref[j]
+        state = jnp.where(kept, keep_ref[j], got_ref[j])
+        grad_in = jnp.where(kept, keep_g_ref[j], got_g_ref[j])
         att_ref[:, cols] = (mm_left(scores, v, nn) + qd * mm_right(q, state, nn)).astype(att_ref.dtype)
         qg_ref[:, cols] = (mm_left(grad_scores, k, nn) + qd * mm_right(g, state, nt)).astype(qg_ref.dtype)
         kg_ref[:, cols] = (mm_left(grad_scores.T, q, nn) + kd * mm_right(v, grad_in, nt)).astype(kg_ref.dtype)
         vg_ref[:, cols] = (mm_left(scores.T, g, nn) + kd * mm_right(k, grad_in, nn)).astype(vg_ref.dtype)
 
 
-def finish(inputs, cumul_heads, state_in, grad_in):
+def finish(inputs, cumul_heads, core, halves):
     queries = inputs[0]
     length, width = queries.shape
-    heads = state_in.shape[0]
+    half = halves[0].shape[0]
+    heads = 2 * half
     dk = width // heads
     block = 8
-    tile = pl.BlockSpec((length, block * dk), lambda h: (0, h))
-    states = pl.BlockSpec((block, dk, dk), lambda h: (h, 0, 0))
+    steps = half // block
+    tile = pl.BlockSpec((length, block * dk), lambda h, c: (0, h))
+    states = pl.BlockSpec((block, dk, dk), lambda h, c: (h % steps, 0, 0))
     out = jax.ShapeDtypeStruct((length, width), jnp.bfloat16)
     return pl.pallas_call(
         head_kernel,
-        grid=(heads // block,),
-        in_specs=[tile] * 4 + [pl.BlockSpec((block, length), lambda h: (h, 0)), states, states],
-        out_specs=[tile] * 4,
+        grid_spec=pltpu.PrefetchScalarGridSpec(
+            num_scalar_prefetch=1,
+            grid=(heads // block,),
+            in_specs=[tile] * 4 + [pl.BlockSpec((block, length), lambda h, c: (h, 0))] + [states] * 4,
+            out_specs=[tile] * 4,
+        ),
         out_shape=[out] * 4,
         compiler_params=pltpu.CompilerParams(dimension_semantics=("arbitrary",)),
-    )(*inputs, cumul_heads, state_in, grad_in)
+    )(core.astype(jnp.int32).reshape(1), *inputs, cumul_heads, *halves)
 
 
 def gather_rows(row, axis):
@@ -198,25 +205,20 @@
             )
         scans.append(jnp.concatenate(parts, 0))
     before, after = scans
-    total_c0 = jnp.where(first, own_total_half, other_total_half)
-    total_c1 = jnp.where(first, other_total_half, own_total_half)
-    state_c0 = jnp.where(first, mine_state, other_state)
-    grad_c1 = jnp.where(first, other_grad, mine_grad)
-    fwd_core0 = before
-    fwd_core1 = jnp.exp(total_c0)[:, None, None] * before + state_c0
-    bwd_core0 = jnp.exp(total_c1)[:, None, None] * after + grad_c1
-    bwd_core1 = after
-    keep_fwd = jnp.where(first, fwd_core0, fwd_core1)
-    keep_bwd = jnp.where(first, bwd_core0, bwd_core1)
-    give_fwd = jnp.where(first, fwd_core1, fwd_core0)
-    give_bwd = jnp.where(first, bwd_core1, bwd_core0)
+    zero = jnp.zeros_like(own_total_half)
+    own_decay = jnp.exp(own_total_half)
+    other_decay = jnp.exp(other_total_half)
+
+    def mix(a, x, b, y):
+        return a[:, None, None] * x + b[:, None, None] * y
+
+    keep_fwd = mix(jnp.where(first, one, other_decay), before, jnp.where(first, zero, one), other_state)
+    give_fwd = mix(jnp.where(first, own_decay, one), before, jnp.where(first, one, zero), mine_state)
+    keep_bwd = mix(jnp.where(first, other_decay, one), after, jnp.where(first, one, zero), other_grad)
+    give_bwd = mix(jnp.where(first, one, own_decay), after, jnp.where(first, zero, one), mine_grad)
     got_fwd, got_bwd = lax.ppermute((give_fwd, give_bwd), axis, partner)
-
-    def assemble(keep, got):
-        return jnp.where(first, jnp.concatenate([keep, got], 0), jnp.concatenate([got, keep], 0))
-
     inputs = (queries, key_vectors, values, out_grad)
-    return tuple(finish(inputs, pieces, assemble(keep_fwd, got_fwd), assemble(keep_bwd, got_bwd)))
+    return tuple(finish(inputs, pieces, core, (keep_fwd, got_fwd, keep_bwd, got_bwd)))
 
 
 def solution(mesh):

time: 176 us -> 279 us (1.59)
  the two profiles are of different devices: /device:TPU:1 before, /device:TPU:15 now
where the time goes in v4:
time: 279 us; the launch traced here: 278 us
  waiting for transfers between devices  129 us (46%)
  starting transfers between devices  105 us (38%)
  Pallas kernels  14.1 us (5%)
  other arithmetic  14 us (5%)
  local copies, waits for them, and re-layouts  10.8 us (4%)
  matrix products  3.97 us (1%)
    ppermute x16, waiting for transfers between devices, chip_scan(): received = lax.ppermute(sent, axis, pairs)  121 us
    ppermute x16, starting transfers between devices, chip_scan(): received = lax.ppermute(sent, axis, pairs)  88.6 us
    pallas_call x1, Pallas kernels, finish(): pl.pallas_call(head_kernel, grid_spec=pltpu.PrefetchScalarGridSpec(num_sc...  14.1 us
    ppermute x5, starting transfers between devices, gather_rows(): known = jnp.concatenate([known, lax.ppermute(known, axis, pairs)], 0)  11.5 us
    ppermute x5, waiting for transfers between devices, gather_rows(): known = jnp.concatenate([known, lax.ppermute(known, axis, pairs)], 0)  5.66 us
  transfers between devices with their start and end apart: 26, of which 16 were waited for; matrix products, arithmetic and copies ran while one was open for 6% of the time, Pallas kernels for 0%

profile of v4, /device:TPU:15, one launch (start us, length us, event | category | flops | bytes accessed | tf_op | source)
XLA Modules:
  0.0 278.1 jit_solution(11387318328225848475)
XLA Ops:
  1.5 1.8 collective-permute-start
  4.5 2.6 copy.17
  7.1 2.8 fusion.2
  9.9 1.1 constant_dynamic-slice_fusion.19
  11.9 3.4 %collective-permute-start.4 = (f32[2,32]{1,0:T(2,128)S(1)}, f32[2,32]{1,0:T(2,128)S(1)}, u32[]{:S(2)}, u32[]{:S(2)}) collective-permute-start(f32[2,32]{1,0:T(2,128)S(1)} %pad_maximum_fusion.4), channel_id=1, source_target_pairs={{0,2},{1,3},{2,4},{3,5},{4,6},{5,7},{6,8},{7,9},{8,10},{9,11},{10,... | collective-permute-start | bytes 776 | tf_op jit(solution)/shard_map/ppermute | solution.py:118
  16.0 1.5 collective-permute-start.5
  17.5 2.5 collective-permute-done.5
  20.0 1.1 collective-permute-start.6
  21.1 1.5 collective-permute-done.6
  22.6 3.7 %collective-permute-start.7 = (f32[16,32]{1,0:T(8,128)S(1)}, f32[16,32]{1,0:T(8,128)S(1)}, u32[]{:S(2)}, u32[]{:S(2)}) collective-permute-start(f32[16,32]{1,0:T(8,128)S(1)} %concatenate.28), channel_id=1, source_target_pairs={{0,16},{1,17},{2,18},{3,19},{4,20},{5,21},{6,22},{7,23},{8,24},{9,... | collective-permute-start | bytes 6152 | tf_op jit(solution)/shard_map/ppermute | solution.py:118
  29.1 9.8 %collective-permute-start.3 = (f32[8,128,128]{2,1,0:T(8,128)S(1)}, f32[8,128,128]{2,1,0:T(8,128)S(1)}, u32[]{:S(2)}, u32[]{:S(2)}) collective-permute-start(f32[8,128,128]{2,1,0:T(8,128)S(1)} %get-tuple-element.55), channel_id=1, source_target_pairs={{0,2},{1,3},{2,4},{3,5},{4,6},{5,7},{6,8},{7,9},{8,10},{9,11},{10,... | collective-permute-start | bytes 1572872 | tf_op jit(solution)/shard_map/ppermute | solution.py:146
  38.9 2.8 %collective-permute-start.11 = (f32[8,128,128]{2,1,0:T(8,128)S(1)}, f32[8,128,128]{2,1,0:T(8,128)S(1)}, u32[]{:S(2)}, u32[]{:S(2)}) collective-permute-start(f32[8,128,128]{2,1,0:T(8,128)S(1)} %get-tuple-element.56), channel_id=1, source_target_pairs={{0,8},{1,9},{2,10},{3,11},{4,12},{5,13},{6,14},{7,15},{8,16},{9,17... | collective-permute-start | bytes 1572872 | tf_op jit(solution)/shard_map/ppermute | solution.py:146
  42.0 3.4 %collective-permute-done.3 = f32[8,128,128]{2,1,0:T(8,128)S(1)} collective-permute-done((f32[8,128,128]{2,1,0:T(8,128)S(1)}, f32[8,128,128]{2,1,0:T(8,128)S(1)}, u32[]{:S(2)}, u32[]{:S(2)}) %collective-permute-start.3) | collective-permute-done | bytes 524320 | tf_op jit(solution)/shard_map/ppermute | solution.py:146
  45.4 3.5 %collective-permute-done.11 = f32[8,128,128]{2,1,0:T(8,128)S(1)} collective-permute-done((f32[8,128,128]{2,1,0:T(8,128)S(1)}, f32[8,128,128]{2,1,0:T(8,128)S(1)}, u32[]{:S(2)}, u32[]{:S(2)}) %collective-permute-start.11) | collective-permute-done | bytes 524320 | tf_op jit(solution)/shard_map/ppermute | solution.py:146
  49.0 1.9 collective-permute-start.8
  50.9 2.6 collective-permute-start.12
  53.6 1.7 copy.18
  55.3 5.1 %collective-permute-done.8 = f32[8,128,128]{2,1,0:T(8,128)S(1)} collective-permute-done((f32[8,128,128]{2,1,0:T(8,128)S(1)}, f32[8,128,128]{2,1,0:T(8,128)S(1)}, u32[]{:S(2)}, u32[]{:S(2)}) %collective-permute-start.8) | collective-permute-done | bytes 524320 | tf_op jit(solution)/shard_map/ppermute | solution.py:146
  61.4 2.8 %collective-permute-start.9 = (f32[8,128,128]{2,1,0:T(8,128)}, f32[8,128,128]{2,1,0:T(8,128)}, u32[]{:S(2)}, u32[]{:S(2)}) collective-permute-start(f32[8,128,128]{2,1,0:T(8,128)} %multiply_add_fusion.20), channel_id=1, source_target_pairs={{0,8},{1,9},{2,10},{3,11},{4,12},{5,13},{6,14},{7,15},{8,16},{9,17... | collective-permute-start | bytes 1572872 | tf_op jit(solution)/shard_map/ppermute | solution.py:146
  65.2 44.5 %collective-permute-start.13 = (f32[8,128,128]{2,1,0:T(8,128)}, f32[8,128,128]{2,1,0:T(8,128)}, u32[]{:S(2)}, u32[]{:S(2)}) collective-permute-start(f32[8,128,128]{2,1,0:T(8,128)} %multiply_add_fusion.16), channel_id=1, source_target_pairs={{0,2},{1,3},{2,4},{3,5},{4,6},{5,7},{6,8},{7,9},{8,10},{9,11},{10,... | collective-permute-start | bytes 1572872 | tf_op jit(solution)/shard_map/ppermute | solution.py:146
  109.7 1.2 fusion
  113.0 1.4 multiply_add_fusion.19
  114.4 1.3 collective-permute-start.10
  115.7 6.1 %collective-permute-done.13 = f32[8,128,128]{2,1,0:T(8,128)} collective-permute-done((f32[8,128,128]{2,1,0:T(8,128)}, f32[8,128,128]{2,1,0:T(8,128)}, u32[]{:S(2)}, u32[]{:S(2)}) %collective-permute-start.13) | collective-permute-done | bytes 524320 | tf_op jit(solution)/shard_map/ppermute | solution.py:146
  121.8 1.4 multiply_add_fusion.15
  123.2 3.0 %collective-permute-start.14 = (f32[8,128,128]{2,1,0:T(8,128)S(1)}, f32[8,128,128]{2,1,0:T(8,128)S(1)}, u32[]{:S(2)}, u32[]{:S(2)}) collective-permute-start(f32[8,128,128]{2,1,0:T(8,128)S(1)} %multiply_add_fusion.15), channel_id=1, source_target_pairs={{0,4},{1,5},{2,6},{3,7},{4,8},{5,9},{6,10},{7,11},{8,12},{9,13},{1... | collective-permute-start | bytes 1572872 | tf_op jit(solution)/shard_map/ppermute | solution.py:146
  127.2 1.4 multiply_add_fusion.18
  128.6 9.3 %collective-permute-done.14 = f32[8,128,128]{2,1,0:T(8,128)S(1)} collective-permute-done((f32[8,128,128]{2,1,0:T(8,128)S(1)}, f32[8,128,128]{2,1,0:T(8,128)S(1)}, u32[]{:S(2)}, u32[]{:S(2)}) %collective-permute-start.14) | collective-permute-done | bytes 524320 | tf_op jit(solution)/shard_map/ppermute | solution.py:146
  138.0 1.2 multiply_add_fusion.14
  139.2 1.9 multiply_add_fusion.3
  141.3 4.0 %collective-permute-start.17 = (f32[8,128,128]{2,1,0:T(8,128)S(1)}, f32[8,128,128]{2,1,0:T(8,128)S(1)}, u32[]{:S(2)}, u32[]{:S(2)}) collective-permute-start(f32[8,128,128]{2,1,0:T(8,128)S(1)} %get-tuple-element.49), channel_id=1, source_target_pairs={{2,0},{3,1},{4,2},{5,3},{6,4},{7,5},{8,6},{9,7},{10,8},{11,9},{12,... | collective-permute-start | bytes 1572872 | tf_op jit(solution)/shard_map/ppermute | solution.py:146
  145.3 1.9 collective-permute-start.21
  147.3 24.1 %collective-permute-done.17 = f32[8,128,128]{2,1,0:T(8,128)S(1)} collective-permute-done((f32[8,128,128]{2,1,0:T(8,128)S(1)}, f32[8,128,128]{2,1,0:T(8,128)S(1)}, u32[]{:S(2)}, u32[]{:S(2)}) %collective-permute-start.17) | collective-permute-done | bytes 524320 | tf_op jit(solution)/shard_map/ppermute | solution.py:146
  171.5 5.1 %collective-permute-start.18 = (f32[8,128,128]{2,1,0:T(8,128)S(1)}, f32[8,128,128]{2,1,0:T(8,128)S(1)}, u32[]{:S(2)}, u32[]{:S(2)}) collective-permute-start(f32[8,128,128]{2,1,0:T(8,128)S(1)} %get-tuple-element.47), channel_id=1, source_target_pairs={{4,0},{5,1},{6,2},{7,3},{8,4},{9,5},{10,6},{11,7},{12,8},{13,9},{1... | collective-permute-start | bytes 1572872 | tf_op jit(solution)/shard_map/ppermute | solution.py:146
  176.6 1.3 collective-permute-start.22
  177.9 9.5 %collective-permute-done.18 = f32[8,128,128]{2,1,0:T(8,128)S(1)} collective-permute-done((f32[8,128,128]{2,1,0:T(8,128)S(1)}, f32[8,128,128]{2,1,0:T(8,128)S(1)}, u32[]{:S(2)}, u32[]{:S(2)}) %collective-permute-start.18) | collective-permute-done | bytes 524320 | tf_op jit(solution)/shard_map/ppermute | solution.py:146
  187.6 2.5 collective-permute-start.19
  190.1 22.3 %collective-permute-done.22 = f32[8,128,128]{2,1,0:T(8,128)S(1)} collective-permute-done((f32[8,128,128]{2,1,0:T(8,128)S(1)}, f32[8,128,128]{2,1,0:T(8,128)S(1)}, u32[]{:S(2)}, u32[]{:S(2)}) %collective-permute-start.22) | collective-permute-done | bytes 524320 | tf_op jit(solution)/shard_map/ppermute | solution.py:146
  212.5 1.9 collective-permute-start.23
  214.6 1.3 collective-permute-start.20
  215.9 16.0 %collective-permute-done.23 = f32[8,128,128]{2,1,0:T(8,128)S(1)} collective-permute-done((f32[8,128,128]{2,1,0:T(8,128)S(1)}, f32[8,128,128]{2,1,0:T(8,128)S(1)}, u32[]{:S(2)}, u32[]{:S(2)}) %collective-permute-start.23) | collective-permute-done | bytes 524320 | tf_op jit(solution)/shard_map/ppermute | solution.py:146
  232.0 1.9 collective-permute-start.24
  234.0 2.5 collective-permute-start.15
  236.5 20.8 %collective-permute-done.20 = f32[8,128,128]{2,1,0:T(8,128)S(1)} collective-permute-done((f32[8,128,128]{2,1,0:T(8,128)S(1)}, f32[8,128,128]{2,1,0:T(8,128)S(1)}, u32[]{:S(2)}, u32[]{:S(2)}) %collective-permute-start.20) | collective-permute-done | bytes 524320 | tf_op jit(solution)/shard_map/ppermute | solution.py:146
  257.7 1.6 multiply_add_fusion
  259.4 1.1 collective-permute-start.25
  261.1 1.8 collective-permute-done.25.got_g_ref
  263.9 14.1 %shard_map.84 = (bf16[128,4096]{1,0:T(8,128)(2,1)}, bf16[128,4096]{1,0:T(8,128)(2,1)}, bf16[128,4096]{1,0:T(8,128)(2,1)}, bf16[128,4096]{1,0:T(8,128)(2,1)}) custom-call(s32[1]{0:T(128)} %bitcast.core_ref, bf16[128,4096]{1,0:T(8,128)(2,1)} %q_ref, bf16[128,4096]{1,0:T(8,128)(2,1)} %k_ref, bf16[128,4096]{1,0:T(8,128)(2,1)} %v_ref, bf16[128,4096]{1,0:T(8,128)(2,1)} %g_ref, ...), custom_call_target="tpu_custom_call" | custom-call | tf_op jit(solution)/shard_map/pallas_call | solution.py:97
  (99 shorter events, 14.6 us)
Async XLA Ops:
  0.6 6.5 %copy-start.4 = (bf16[128,4096]{1,0:T(8,128)(2,1)S(1)}, bf16[128,4096]{1,0:T(8,128)(2,1)}, u32[]{:S(2)}) copy-start(bf16[128,4096]{1,0:T(8,128)(2,1)} %v_ref) | copy-start | bytes 3145732
  1.5 2.9 %collective-permute-start = (f32[1,32]{1,0:T(1,128)S(1)}, f32[1,32]{1,0:T(1,128)S(1)}, u32[]{:S(2)}, u32[]{:S(2)}) collective-permute-start(f32[1,32]{1,0:T(1,128)S(1)} %bitcast.170), channel_id=1, source_target_pairs={{0,1},{1,2},{2,3},{3,4},{4,5},{5,6},{6,7},{7,8},{8,9},{9,10},{10,1... | collective-permute-start | bytes 392 | tf_op jit(solution)/shard_map/ppermute | solution.py:118
  9.9 18.4 %copy-start = (f32[32,128,128]{2,1,0:T(8,128)}, f32[32,128,128]{2,1,0:T(8,128)S(1)}, u32[]{:S(2)}) copy-start(f32[32,128,128]{2,1,0:T(8,128)S(1)} %fusion.2) | copy-start | bytes 6291460
  11.0 17.0 %collective-permute-start.2 = (f32[16,128,128]{2,1,0:T(8,128)}, f32[16,128,128]{2,1,0:T(8,128)S(1)}, u32[]{:S(2)}, u32[]{:S(2)}) collective-permute-start(f32[16,128,128]{2,1,0:T(8,128)} %constant_dynamic-slice_fusion.19), channel_id=1, source_target_pairs={{0,1},{1,0},{2,3},{3,2},{4,5},{5,4},{6,7},{7,6},{8,9},{9,8},{10,11... | collective-permute-start | bytes 3145736 | tf_op jit(solution)/shard_map/ppermute | solution.py:175
  11.8 14.5 %collective-permute-start.1 = (f32[32]{0:T(128)S(1)}, f32[32]{0:T(128)S(1)}, u32[]{:S(2)}, u32[]{:S(2)}) collective-permute-start(f32[32]{0:T(128)S(1)} %convert_reduce_fusion), channel_id=1, source_target_pairs={{0,1},{1,0},{2,3},{3,2},{4,5},{5,4},{6,7},{7,6},{8,9},{9,8},{10,11... | collective-permute-start | bytes 392 | tf_op jit(solution)/shard_map/ppermute | solution.py:175
  11.9 4.1 %collective-permute-start.4 = (f32[2,32]{1,0:T(2,128)S(1)}, f32[2,32]{1,0:T(2,128)S(1)}, u32[]{:S(2)}, u32[]{:S(2)}) collective-permute-start(f32[2,32]{1,0:T(2,128)S(1)} %pad_maximum_fusion.4), channel_id=1, source_target_pairs={{0,2},{1,3},{2,4},{3,5},{4,6},{5,7},{6,8},{7,9},{8,10},{9,11},{10,... | collective-permute-start | bytes 776 | tf_op jit(solution)/shard_map/ppermute | solution.py:118
  16.0 4.0 %collective-permute-start.5 = (f32[4,32]{1,0:T(4,128)S(1)}, f32[4,32]{1,0:T(4,128)S(1)}, u32[]{:S(2)}, u32[]{:S(2)}) collective-permute-start(f32[4,32]{1,0:T(4,128)S(1)} %pad_maximum_fusion.3), channel_id=1, source_target_pairs={{0,4},{1,5},{2,6},{3,7},{4,8},{5,9},{6,10},{7,11},{8,12},{9,13},{1... | collective-permute-start | bytes 1544 | tf_op jit(solution)/shard_map/ppermute | solution.py:118
  20.0 2.5 collective-permute-start.6
  22.6 4.7 %collective-permute-start.7 = (f32[16,32]{1,0:T(8,128)S(1)}, f32[16,32]{1,0:T(8,128)S(1)}, u32[]{:S(2)}, u32[]{:S(2)}) collective-permute-start(f32[16,32]{1,0:T(8,128)S(1)} %concatenate.28), channel_id=1, source_target_pairs={{0,16},{1,17},{2,18},{3,19},{4,20},{5,21},{6,22},{7,23},{8,24},{9,... | collective-permute-start | bytes 6152 | tf_op jit(solution)/shard_map/ppermute | solution.py:118
  28.0 1.0 copy-start.6
  29.1 24.5 %copy-start.3 = (bf16[128,4096]{1,0:T(8,128)(2,1)S(1)}, bf16[128,4096]{1,0:T(8,128)(2,1)}, u32[]{:S(2)}) copy-start(bf16[128,4096]{1,0:T(8,128)(2,1)} %q_ref) | copy-start | bytes 3145732
  29.1 16.2 %collective-permute-start.3 = (f32[8,128,128]{2,1,0:T(8,128)S(1)}, f32[8,128,128]{2,1,0:T(8,128)S(1)}, u32[]{:S(2)}, u32[]{:S(2)}) collective-permute-start(f32[8,128,128]{2,1,0:T(8,128)S(1)} %get-tuple-element.55), channel_id=1, source_target_pairs={{0,2},{1,3},{2,4},{3,5},{4,6},{5,7},{6,8},{7,9},{8,10},{9,11},{10,... | collective-permute-start | bytes 1572872 | tf_op jit(solution)/shard_map/ppermute | solution.py:146
  38.9 9.9 %collective-permute-start.11 = (f32[8,128,128]{2,1,0:T(8,128)S(1)}, f32[8,128,128]{2,1,0:T(8,128)S(1)}, u32[]{:S(2)}, u32[]{:S(2)}) collective-permute-start(f32[8,128,128]{2,1,0:T(8,128)S(1)} %get-tuple-element.56), channel_id=1, source_target_pairs={{0,8},{1,9},{2,10},{3,11},{4,12},{5,13},{6,14},{7,15},{8,16},{9,17... | collective-permute-start | bytes 1572872 | tf_op jit(solution)/shard_map/ppermute | solution.py:146
  45.3 5.6 %copy-start.14 = (f32[8,128,128]{2,1,0:T(8,128)}, f32[8,128,128]{2,1,0:T(8,128)S(1)}, u32[]{:S(2)}) copy-start(f32[8,128,128]{2,1,0:T(8,128)S(1)} %collective-permute-done.3) | copy-start | bytes 1572868
  48.8 2.1 copy-start.12
  49.0 11.4 %collective-permute-start.8 = (f32[8,128,128]{2,1,0:T(8,128)S(1)}, f32[8,128,128]{2,1,0:T(8,128)S(1)}, u32[]{:S(2)}, u32[]{:S(2)}) collective-permute-start(f32[8,128,128]{2,1,0:T(8,128)S(1)} %get-tuple-element.53), channel_id=1, source_target_pairs={{0,4},{1,5},{2,6},{3,7},{4,8},{5,9},{6,10},{7,11},{8,12},{9,13},{1... | collective-permute-start | bytes 1572872 | tf_op jit(solution)/shard_map/ppermute | solution.py:146
  50.9 13.3 %collective-permute-start.12 = (f32[8,128,128]{2,1,0:T(8,128)S(1)}, f32[8,128,128]{2,1,0:T(8,128)S(1)}, u32[]{:S(2)}, u32[]{:S(2)}) collective-permute-start(f32[8,128,128]{2,1,0:T(8,128)S(1)} %get-tuple-element.54), channel_id=1, source_target_pairs={{0,16},{1,17},{2,18},{3,19},{4,20},{5,21},{6,22},{7,23},{8,24},{9,... | collective-permute-start | bytes 1572872 | tf_op jit(solution)/shard_map/ppermute | solution.py:146
  55.3 54.4 %copy-start.2 = (f32[128,4096]{0,1:T(8,128)S(1)}, f32[128,4096]{0,1:T(8,128)}, u32[]{:S(2)}) copy-start(f32[128,4096]{0,1:T(8,128)} %copy.18) | copy-start | bytes 6291460
  55.3 54.4 %copy-start.5 = (bf16[128,4096]{1,0:T(8,128)(2,1)S(1)}, bf16[128,4096]{1,0:T(8,128)(2,1)}, u32[]{:S(2)}) copy-start(bf16[128,4096]{1,0:T(8,128)(2,1)} %g_ref) | copy-start | bytes 3145732
  60.4 49.3 %copy-start.10 = (f32[8,128,128]{2,1,0:T(8,128)}, f32[8,128,128]{2,1,0:T(8,128)S(1)}, u32[]{:S(2)}) copy-start(f32[8,128,128]{2,1,0:T(8,128)S(1)} %collective-permute-done.8) | copy-start | bytes 1572868
  61.4 51.6 %collective-permute-start.9 = (f32[8,128,128]{2,1,0:T(8,128)}, f32[8,128,128]{2,1,0:T(8,128)}, u32[]{:S(2)}, u32[]{:S(2)}) collective-permute-start(f32[8,128,128]{2,1,0:T(8,128)} %multiply_add_fusion.20), channel_id=1, source_target_pairs={{0,8},{1,9},{2,10},{3,11},{4,12},{5,13},{6,14},{7,15},{8,16},{9,17... | collective-permute-start | bytes 1572872 | tf_op jit(solution)/shard_map/ppermute | solution.py:146
  64.2 45.4 %copy-start.8 = (f32[8,128,128]{2,1,0:T(8,128)}, f32[8,128,128]{2,1,0:T(8,128)S(1)}, u32[]{:S(2)}) copy-start(f32[8,128,128]{2,1,0:T(8,128)S(1)} %collective-permute-done.12) | copy-start | bytes 1572868
  65.2 56.6 %collective-permute-start.13 = (f32[8,128,128]{2,1,0:T(8,128)}, f32[8,128,128]{2,1,0:T(8,128)}, u32[]{:S(2)}, u32[]{:S(2)}) collective-permute-start(f32[8,128,128]{2,1,0:T(8,128)} %multiply_add_fusion.16), channel_id=1, source_target_pairs={{0,2},{1,3},{2,4},{3,5},{4,6},{5,7},{6,8},{7,9},{8,10},{9,11},{10,... | collective-permute-start | bytes 1572872 | tf_op jit(solution)/shard_map/ppermute | solution.py:146
  112.0 27.2 %collective-permute-start.16 = (f32[16,128,128]{2,1,0:T(8,128)}, f32[16,128,128]{2,1,0:T(8,128)S(1)}, u32[]{:S(2)}, u32[]{:S(2)}) collective-permute-start(f32[16,128,128]{2,1,0:T(8,128)} %constant_dynamic-slice_fusion.18), channel_id=1, source_target_pairs={{0,1},{1,0},{2,3},{3,2},{4,5},{5,4},{6,7},{7,6},{8,9},{9,8},{10,11... | collective-permute-start | bytes 3145736 | tf_op jit(solution)/shard_map/ppermute | solution.py:175
  113.0 14.3 %copy-start.11 = (f32[8,128,128]{2,1,0:T(8,128)S(1)}, f32[8,128,128]{2,1,0:T(8,128)}, u32[]{:S(2)}) copy-start(f32[8,128,128]{2,1,0:T(8,128)} %copy-done.10) | copy-start | bytes 1572868
  113.0 14.3 %copy-start.15 = (f32[8,128,128]{2,1,0:T(8,128)S(1)}, f32[8,128,128]{2,1,0:T(8,128)}, u32[]{:S(2)}) copy-start(f32[8,128,128]{2,1,0:T(8,128)} %copy-done.14) | copy-start | bytes 1572868
  114.4 12.8 %collective-permute-start.10 = (f32[8,128,128]{2,1,0:T(8,128)S(1)}, f32[8,128,128]{2,1,0:T(8,128)S(1)}, u32[]{:S(2)}, u32[]{:S(2)}) collective-permute-start(f32[8,128,128]{2,1,0:T(8,128)S(1)} %multiply_add_fusion.19), channel_id=1, source_target_pairs={{0,16},{1,17},{2,18},{3,19},{4,20},{5,21},{6,22},{7,23},{8,24},{9,... | collective-permute-start | bytes 1572872 | tf_op jit(solution)/shard_map/ppermute | solution.py:146
  121.8 16.1 %copy-start.9 = (f32[8,128,128]{2,1,0:T(8,128)S(1)}, f32[8,128,128]{2,1,0:T(8,128)}, u32[]{:S(2)}) copy-start(f32[8,128,128]{2,1,0:T(8,128)} %copy-done.8) | copy-start | bytes 1572868
  121.8 16.1 %copy-start.13 = (f32[8,128,128]{2,1,0:T(8,128)S(1)}, f32[8,128,128]{2,1,0:T(8,128)}, u32[]{:S(2)}) copy-start(f32[8,128,128]{2,1,0:T(8,128)} %copy-done.12) | copy-start | bytes 1572868
  123.2 14.7 %collective-permute-start.14 = (f32[8,128,128]{2,1,0:T(8,128)S(1)}, f32[8,128,128]{2,1,0:T(8,128)S(1)}, u32[]{:S(2)}, u32[]{:S(2)}) collective-permute-start(f32[8,128,128]{2,1,0:T(8,128)S(1)} %multiply_add_fusion.15), channel_id=1, source_target_pairs={{0,4},{1,5},{2,6},{3,7},{4,8},{5,9},{6,10},{7,11},{8,12},{9,13},{1... | collective-permute-start | bytes 1572872 | tf_op jit(solution)/shard_map/ppermute | solution.py:146
  127.2 12.0 %copy-start.1 = (f32[32,128,128]{2,1,0:T(8,128)S(1)}, f32[32,128,128]{2,1,0:T(8,128)}, u32[]{:S(2)}) copy-start(f32[32,128,128]{2,1,0:T(8,128)} %copy-done) | copy-start | bytes 6291460
  127.2 12.0 %copy-start.7 = (f32[16,128,128]{2,1,0:T(8,128)S(1)}, f32[16,128,128]{2,1,0:T(8,128)}, u32[]{:S(2)}) copy-start(f32[16,128,128]{2,1,0:T(8,128)} %copy-done.6) | copy-start | bytes 3145732
  141.3 30.1 %collective-permute-start.17 = (f32[8,128,128]{2,1,0:T(8,128)S(1)}, f32[8,128,128]{2,1,0:T(8,128)S(1)}, u32[]{:S(2)}, u32[]{:S(2)}) collective-permute-start(f32[8,128,128]{2,1,0:T(8,128)S(1)} %get-tuple-element.49), channel_id=1, source_target_pairs={{2,0},{3,1},{4,2},{5,3},{6,4},{7,5},{8,6},{9,7},{10,8},{11,9},{12,... | collective-permute-start | bytes 1572872 | tf_op jit(solution)/shard_map/ppermute | solution.py:146
  145.3 26.1 %collective-permute-start.21 = (f32[8,128,128]{2,1,0:T(8,128)S(1)}, f32[8,128,128]{2,1,0:T(8,128)S(1)}, u32[]{:S(2)}, u32[]{:S(2)}) collective-permute-start(f32[8,128,128]{2,1,0:T(8,128)S(1)} %get-tuple-element.50), channel_id=1, source_target_pairs={{8,0},{9,1},{10,2},{11,3},{12,4},{13,5},{14,6},{15,7},{16,8},{17,9... | collective-permute-start | bytes 1572872 | tf_op jit(solution)/shard_map/ppermute | solution.py:146
  171.5 16.0 %collective-permute-start.18 = (f32[8,128,128]{2,1,0:T(8,128)S(1)}, f32[8,128,128]{2,1,0:T(8,128)S(1)}, u32[]{:S(2)}, u32[]{:S(2)}) collective-permute-start(f32[8,128,128]{2,1,0:T(8,128)S(1)} %get-tuple-element.47), channel_id=1, source_target_pairs={{4,0},{5,1},{6,2},{7,3},{8,4},{9,5},{10,6},{11,7},{12,8},{13,9},{1... | collective-permute-start | bytes 1572872 | tf_op jit(solution)/shard_map/ppermute | solution.py:146
  176.6 35.8 %collective-permute-start.22 = (f32[8,128,128]{2,1,0:T(8,128)S(1)}, f32[8,128,128]{2,1,0:T(8,128)S(1)}, u32[]{:S(2)}, u32[]{:S(2)}) collective-permute-start(f32[8,128,128]{2,1,0:T(8,128)S(1)} %get-tuple-element.48), channel_id=1, source_target_pairs={{16,0},{17,1},{18,2},{19,3},{20,4},{21,5},{22,6},{23,7},{24,8},{25... | collective-permute-start | bytes 1572872 | tf_op jit(solution)/shard_map/ppermute | solution.py:146
  187.6 26.9 %collective-permute-start.19 = (f32[8,128,128]{2,1,0:T(8,128)S(1)}, f32[8,128,128]{2,1,0:T(8,128)S(1)}, u32[]{:S(2)}, u32[]{:S(2)}) collective-permute-start(f32[8,128,128]{2,1,0:T(8,128)S(1)} %multiply_add_fusion.12), channel_id=1, source_target_pairs={{8,0},{9,1},{10,2},{11,3},{12,4},{13,5},{14,6},{15,7},{16,8},{17,9... | collective-permute-start | bytes 1572872 | tf_op jit(solution)/shard_map/ppermute | solution.py:146
  212.5 19.4 %collective-permute-start.23 = (f32[8,128,128]{2,1,0:T(8,128)S(1)}, f32[8,128,128]{2,1,0:T(8,128)S(1)}, u32[]{:S(2)}, u32[]{:S(2)}) collective-permute-start(f32[8,128,128]{2,1,0:T(8,128)S(1)} %multiply_add_fusion.8), channel_id=1, source_target_pairs={{2,0},{3,1},{4,2},{5,3},{6,4},{7,5},{8,6},{9,7},{10,8},{11,9},{12,... | collective-permute-start | bytes 1572872 | tf_op jit(solution)/shard_map/ppermute | solution.py:146
  214.6 42.7 %collective-permute-start.20 = (f32[8,128,128]{2,1,0:T(8,128)S(1)}, f32[8,128,128]{2,1,0:T(8,128)S(1)}, u32[]{:S(2)}, u32[]{:S(2)}) collective-permute-start(f32[8,128,128]{2,1,0:T(8,128)S(1)} %multiply_add_fusion.11), channel_id=1, source_target_pairs={{16,0},{17,1},{18,2},{19,3},{20,4},{21,5},{22,6},{23,7},{24,8},{25... | collective-permute-start | bytes 1572872 | tf_op jit(solution)/shard_map/ppermute | solution.py:146
  232.0 25.5 %collective-permute-start.24 = (f32[8,128,128]{2,1,0:T(8,128)S(1)}, f32[8,128,128]{2,1,0:T(8,128)S(1)}, u32[]{:S(2)}, u32[]{:S(2)}) collective-permute-start(f32[8,128,128]{2,1,0:T(8,128)S(1)} %multiply_add_fusion.7), channel_id=1, source_target_pairs={{4,0},{5,1},{6,2},{7,3},{8,4},{9,5},{10,6},{11,7},{12,8},{13,9},{1... | collective-permute-start | bytes 1572872 | tf_op jit(solution)/shard_map/ppermute | solution.py:146
  234.0 27.1 %collective-permute-start.15 = (f32[16,128,128]{2,1,0:T(8,128)}, f32[16,128,128]{2,1,0:T(8,128)}, u32[]{:S(2)}, u32[]{:S(2)}) collective-permute-start(f32[16,128,128]{2,1,0:T(8,128)} %get-tuple-element.51), channel_id=1, source_target_pairs={{0,1},{1,0},{2,3},{3,2},{4,5},{5,4},{6,7},{7,6},{8,9},{9,8},{10,11... | collective-permute-start | bytes 3145736 | tf_op jit(solution)/shard_map/ppermute | solution.py:219
  259.4 3.6 %collective-permute-start.25 = (f32[16,128,128]{2,1,0:T(8,128)}, f32[16,128,128]{2,1,0:T(8,128)S(1)}, u32[]{:S(2)}, u32[]{:S(2)}) collective-permute-start(f32[16,128,128]{2,1,0:T(8,128)} %get-tuple-element.45), channel_id=1, source_target_pairs={{0,1},{1,0},{2,3},{3,2},{4,5},{5,4},{6,7},{7,6},{8,9},{9,8},{10,11... | collective-permute-start | bytes 3145736 | tf_op jit(solution)/shard_map/ppermute | solution.py:219
  262.9 1.0 copy-start.16

commit v5 on v3

--- a/solution.py
+++ b/solution.py
@@ -100,47 +100,46 @@
     )(*inputs, cumul_heads, state_in, grad_in)
 
 
-def gather_rows(row, axis):
+def gather_round(known, axis, step):
     count = lax.axis_size(axis)
-    me = lax.axis_index(axis)
-    known = row[None]
-    early = None
-    step = 1
-    while step < count:
-        pairs = [(i, (i + step) % count) for i in range(count)]
-        known = jnp.concatenate([known, lax.ppermute(known, axis, pairs)], 0)
-        early = known if early is None else early
-        step *= 2
-    return known[(me - jnp.arange(count)) % count], early
-
-
-def window_sum(ordered, place, first, last):
-    total = jnp.zeros_like(ordered[0])
-    for back in range(first, last + 1):
+    pairs = [(i, (i + step) % count) for i in range(count)]
+    return jnp.concatenate([known, lax.ppermute(known, axis, pairs)], 0)
+
+
+def shift_pairs(chips, step, reverse):
+    direction = -1 if reverse else 1
+    pairs = []
+    for c in range(chips):
+        target = c + direction * step
+        if 0 <= target < chips:
+            for core in range(2):
+                pairs.append((2 * c + core, 2 * target + core))
+    return pairs
+
+
+def window_sum(ordered, place, first, last, own):
+    total = own if first == 0 else jnp.zeros_like(own)
+    for back in range(max(first, 1), last + 1):
         index = place - back
         picked = lax.dynamic_index_in_dim(ordered, jnp.maximum(index, 0), 0, False)
         total = total + jnp.where(index >= 0, picked, jnp.zeros_like(picked))
     return total
 
 
-def chip_scan(chip_totals, state, axis, chip, chips, reverse, steps):
-    direction = -1 if reverse else 1
+def chip_scan(chip_totals, own, state, axis, chip, chips, reverse, steps, first_received):
     ordered = chip_totals[::-1] if reverse else chip_totals
     place = chips - 1 - chip if reverse else chip
     sent = state
     carried = jnp.zeros_like(state)
     for count, step in enumerate(steps):
-        pairs = []
-        for c in range(chips):
-            target = c + direction * step
-            if 0 <= target < chips:
-                for core in range(2):
-                    pairs.append((2 * c + core, 2 * target + core))
-        received = lax.ppermute(sent, axis, pairs)
-        to_start = jnp.exp(window_sum(ordered, place, 1, step - 1))[:, None, None]
+        if count == 0:
+            received = first_received
+        else:
+            received = lax.ppermute(sent, axis, shift_pairs(chips, step, reverse))
+        to_start = jnp.exp(window_sum(ordered, place, 1, step - 1, own))[:, None, None]
         carried = carried + to_start * received
         if count + 1 < len(steps):
-            to_end = jnp.exp(window_sum(ordered, place, 0, step - 1))[:, None, None]
+            to_end = jnp.exp(window_sum(ordered, place, 0, step - 1, own))[:, None, None]
             sent = sent + to_end * received
     return carried
 
@@ -148,7 +147,8 @@
 def shards(queries, key_vectors, values, out_grad, log_decay):
     axis = "ctx"
     total = jnp.sum(log_decay.astype(jnp.float32), axis=0)
-    every_total, early = gather_rows(total, axis)
+    early = gather_round(total[None], axis, 1)
+    known = gather_round(early, axis, 2)
     _, queries, key_vectors, values, out_grad = lax.optimization_barrier(
         (early, queries, key_vectors, values, out_grad))
     _, state, grad_state, pieces = prepare(queries, key_vectors, values, out_grad, log_decay)
@@ -178,8 +178,6 @@
     bwd_a = jnp.where(first, one, jnp.exp(other_total_half))[:, None, None]
     bwd_b = jnp.where(first, jnp.exp(own_total_half), one)[:, None, None]
     chip_grad = bwd_a * mine_grad + bwd_b * other_grad
-    chip_totals = every_total[0::2] + every_total[1::2]
-    chip = lax.axis_index(axis) // 2
     steps = []
     step = 1
     while step < chips:
@@ -188,14 +186,32 @@
     turn = len(steps) // 2
     orders = (steps, steps[turn:] + steps[:turn])
     group = half // 2
+    firsts = tuple(
+        lax.ppermute(chip_sum[g * group:(g + 1) * group], axis, shift_pairs(chips, order[0], reverse))
+        for chip_sum, reverse in ((chip_state, False), (chip_grad, True))
+        for g, order in enumerate(orders))
+    known, firsts = lax.optimization_barrier((known, firsts))
+    step = 4
+    while step < lax.axis_size(axis):
+        known = gather_round(known, axis, step)
+        step *= 2
+    count = lax.axis_size(axis)
+    every_total = known[(lax.axis_index(axis) - jnp.arange(count)) % count]
+    chip_totals = every_total[0::2] + every_total[1::2]
+    chip = lax.axis_index(axis) // 2
+    own_chip = own_half(total + other_total)
     scans = []
+    first_index = 0
     for chip_sum, reverse in ((chip_state, False), (chip_grad, True)):
         parts = []
         for g, order in enumerate(orders):
             group_totals = lax.dynamic_slice_in_dim(chip_totals, core * half + g * group, group, 1)
             parts.append(
-                chip_scan(group_totals, chip_sum[g * group:(g + 1) * group], axis, chip, chips, reverse, order)
+                chip_scan(group_totals, own_chip[g * group:(g + 1) * group], chip_sum[g * group:(g + 1) * group],
+                          axis, chip, chips, reverse, order,
+                          firsts[first_index])
             )
+            first_index += 1
         scans.append(jnp.concatenate(parts, 0))
     before, after = scans
     total_c0 = jnp.where(first, own_total_half, other_total_half)

time: 176 us -> 197 us (1.12)
  starting transfers between devices: 52.6 us -> 73.1 us
  waiting for transfers between devices: 78.8 us -> 65 us
  other arithmetic: 13.6 us -> 22.1 us
  local copies, waits for them, and re-layouts: 11.7 us -> 15.1 us
    ppermute x21, starting transfers between devices: 42.5 us -> 65.1 us  [the longest x12 48.7 us: chip_scan(): received = lax.ppermute(sent, axis, shift_pairs(chips, step, reverse))]
    ppermute x21, waiting for transfers between devices: 78.8 us -> 63.2 us  [the longest x12 33.7 us: chip_scan(): received = lax.ppermute(sent, axis, shift_pairs(chips, step, reverse))]
    add x4, other arithmetic: 0.86 us -> 5.25 us  [chip_scan(): carried = carried + to_start * received]
    ppermute x3, starting transfers between devices: 8.34 us -> 6.18 us  [shards(): other_total, other_state, other_grad = lax.ppermute(sent, axis, partner)]
  transfers between devices with their start and end apart: 26 -> 26, of which waited for: 10 -> 11; matrix products, arithmetic and copies ran while one was open for 13% -> 14% of each run, Pallas kernels for 0% -> 0%
where the time goes in v5:
time: 197 us; the launch traced here: 196 us
  starting transfers between devices  73.1 us (37%)
  waiting for transfers between devices  65 us (33%)
  other arithmetic  22.1 us (11%)
  local copies, waits for them, and re-layouts  15.1 us (8%)
  Pallas kernels  13.7 us (7%)
  matrix products  5.83 us (3%)
    ppermute x12, starting transfers between devices, chip_scan(): received = lax.ppermute(sent, axis, shift_pairs(chips, step, reverse))  48.7 us
    ppermute x12, waiting for transfers between devices, chip_scan(): received = lax.ppermute(sent, axis, shift_pairs(chips, step, reverse))  33.7 us
    ppermute x5, waiting for transfers between devices, gather_round(): return jnp.concatenate([known, lax.ppermute(known, axis, pairs)], 0)  21.8 us
    pallas_call x1, Pallas kernels, finish(): pl.pallas_call(head_kernel, grid=(heads // block,), in_specs=[tile] * 4 +...  13.7 us
    ppermute x4, starting transfers between devices, shards(): lax.ppermute(chip_sum[g * group:(g + 1) * group], axis, shift_pairs(chips...  12.2 us
    ppermute x4, waiting for transfers between devices, shards(): lax.ppermute(chip_sum[g * group:(g + 1) * group], axis, shift_pairs(chips...  7.7 us
    ppermute x3, starting transfers between devices, shards(): other_total, other_state, other_grad = lax.ppermute(sent, axis, partner)  6.18 us
    add x4, other arithmetic, chip_scan(): carried = carried + to_start * received  5.25 us
  transfers between devices with their start and end apart: 26, of which 11 were waited for; matrix products, arithmetic and copies ran while one was open for 14% of the time, Pallas kernels for 0%

profile of v5, /device:TPU:1, one launch (start us, length us, event | category | flops | bytes accessed | tf_op | source)
XLA Modules:
  0.0 196.1 jit_solution(12588675665423620323)
XLA Ops:
  1.5 2.7 %collective-permute-start = (f32[1,32]{1,0:T(1,128)S(1)}, f32[1,32]{1,0:T(1,128)S(1)}, u32[]{:S(2)}, u32[]{:S(2)}) collective-permute-start(f32[1,32]{1,0:T(1,128)S(1)} %bitcast.153), channel_id=1, source_target_pairs={{0,1},{1,2},{2,3},{3,4},{4,5},{5,6},{6,7},{7,8},{8,9},{9,10},{10,1... | collective-permute-start | bytes 392 | tf_op jit(solution)/shard_map/ppermute | solution.py:106
  5.5 2.6 %copy.18 = f32[128,4096]{0,1:T(8,128)} copy(bf16[128,4096]{1,0:T(8,128)(2,1)} %q_ref) | data formatting | bytes 3145728 | tf_op jit(solution)/shard_map/convert_element_type | solution.py:19
  8.1 2.8 %fusion = f32[32,128,128]{2,1,0:T(8,128)S(1)} fusion(f32[128,32,128]{0,2,1:T(8,128)} %bitcast.150, f32[128,32]{0,1:T(8,128)S(1)} %copy.14, bf16[128,4096]{1,0:T(8,128)(2,1)S(1)} %copy-done.7), kind=kOutput, calls=%fused_computation.3 | convolution fusion | flops 805830656 | bytes 5259264 | tf_op jit(solution)/shard_map/the,thf->hef/dot_general | solution.py:28
  10.8 1.1 constant_dynamic-slice_fusion.16
  11.9 5.7 %collective-permute-start.6 = (f32[16,128,128]{2,1,0:T(8,128)}, f32[16,128,128]{2,1,0:T(8,128)S(1)}, u32[]{:S(2)}, u32[]{:S(2)}) collective-permute-start(f32[16,128,128]{2,1,0:T(8,128)} %constant_dynamic-slice_fusion.16), channel_id=1, source_target_pairs={{0,1},{1,0},{2,3},{3,2},{4,5},{5,4},{6,7},{7,6},{8,9},{9,8},{10,11... | collective-permute-start | bytes 3145736 | tf_op jit(solution)/shard_map/ppermute | solution.py:168
  17.6 2.6 %copy.17 = f32[128,4096]{0,1:T(8,128)} copy(bf16[128,4096]{1,0:T(8,128)(2,1)} %k_ref) | data formatting | bytes 3145728 | tf_op jit(solution)/shard_map/convert_element_type | solution.py:20
  20.2 3.1 %fusion.2 = f32[32,128,128]{2,1,0:T(8,128)S(1)} fusion(f32[128,32,128]{0,2,1:T(8,128)} %bitcast.151, f32[128,32]{0,1:T(8,128)S(1)} %copy.11, bf16[128,4096]{1,0:T(8,128)(2,1)} %v_ref), kind=kOutput, calls=%fused_computation.5 | convolution fusion | flops 805830656 | bytes 5259264 | tf_op jit(solution)/shard_map/she,shf->hef/dot_general | solution.py:27
  23.3 1.3 copy-done
  26.2 1.8 collective-permute-done.2
  29.1 1.6 multiply_add_fusion
  31.7 1.3 collective-permute-start.8
  33.0 1.3 collective-permute-start.7
  34.3 1.4 multiply_add_fusion.1
  36.7 1.1 fusion.81
  37.8 5.4 %collective-permute-start.5 = (f32[8,128,128]{2,1,0:T(8,128)}, f32[8,128,128]{2,1,0:T(8,128)}, u32[]{:S(2)}, u32[]{:S(2)}) collective-permute-start(f32[8,128,128]{2,1,0:T(8,128)} %get-tuple-element.62), channel_id=1, source_target_pairs={{0,8},{1,9},{2,10},{3,11},{4,12},{5,13},{6,14},{7,15},{8,16},{9,17... | collective-permute-start | bytes 1572872 | tf_op jit(solution)/shard_map/ppermute | solution.py:190
  43.2 4.2 %collective-permute-start.4 = (f32[8,128,128]{2,1,0:T(8,128)}, f32[8,128,128]{2,1,0:T(8,128)}, u32[]{:S(2)}, u32[]{:S(2)}) collective-permute-start(f32[8,128,128]{2,1,0:T(8,128)} %get-tuple-element.63), channel_id=1, source_target_pairs={{0,2},{1,3},{2,4},{3,5},{4,6},{5,7},{6,8},{7,9},{8,10},{9,11},{10,... | collective-permute-start | bytes 1572872 | tf_op jit(solution)/shard_map/ppermute | solution.py:190
  47.5 9.4 %collective-permute-done.1 = f32[2,32]{1,0:T(2,128)S(1)} collective-permute-done((f32[2,32]{1,0:T(2,128)S(1)}, f32[2,32]{1,0:T(2,128)S(1)}, u32[]{:S(2)}, u32[]{:S(2)}) %collective-permute-start.1) | collective-permute-done | bytes 288 | tf_op jit(solution)/shard_map/ppermute | solution.py:106
  56.9 7.7 %collective-permute-done.5 = f32[8,128,128]{2,1,0:T(8,128)} collective-permute-done((f32[8,128,128]{2,1,0:T(8,128)}, f32[8,128,128]{2,1,0:T(8,128)}, u32[]{:S(2)}, u32[]{:S(2)}) %collective-permute-start.5) | collective-permute-done | bytes 524320 | tf_op jit(solution)/shard_map/ppermute | solution.py:190
  64.6 6.0 %collective-permute-done.9 = f32[4,32]{1,0:T(4,128)S(1)} collective-permute-done((f32[4,32]{1,0:T(4,128)S(1)}, f32[4,32]{1,0:T(4,128)S(1)}, u32[]{:S(2)}, u32[]{:S(2)}) %collective-permute-start.9) | collective-permute-done | bytes 544 | tf_op jit(solution)/shard_map/ppermute | solution.py:106
  70.7 1.1 collective-permute-start.10
  71.7 2.7 %collective-permute-done.10 = f32[8,32]{1,0:T(8,128)S(1)} collective-permute-done((f32[8,32]{1,0:T(8,128)S(1)}, f32[8,32]{1,0:T(8,128)S(1)}, u32[]{:S(2)}, u32[]{:S(2)}) %collective-permute-start.10) | collective-permute-done | bytes 1056 | tf_op jit(solution)/shard_map/ppermute | solution.py:106
  75.0 3.5 %collective-permute-done.11 = f32[16,32]{1,0:T(8,128)S(1)} collective-permute-done((f32[16,32]{1,0:T(8,128)S(1)}, f32[16,32]{1,0:T(8,128)S(1)}, u32[]{:S(2)}, u32[]{:S(2)}) %collective-permute-start.11) | collective-permute-done | bytes 2080 | tf_op jit(solution)/shard_map/ppermute | solution.py:106
  79.7 2.1 %multiply_add_fusion.9 = (f32[8,128,128]{2,1,0:T(8,128)S(1)}, f32[8,128,128]{2,1,0:T(8,128)S(1)}, f32[8,128,128]{2,1,0:T(8,128)S(1)}, f32[8,128,128]{2,1,0:T(8,128)S(1)}) fusion(f32[8,128,128]{2,1,0:T(8,128)} %collective-permute-done.7, f32[8]{0:T(128)S(1)} %get-tuple-element.83, f32[16,128,128]{2,1,0:T(8,128)S(1)} %multiply_add_fusion, ...), kind=kLoop, calls=%fused_computation.30 | loop fusion | flops 1048576 | bytes 6291552 | tf_op jit(solution)/shard_map/add | solution.py:143
  81.9 1.3 collective-permute-start.22
  83.2 5.6 %collective-permute-start.15 = (f32[8,128,128]{2,1,0:T(8,128)S(1)}, f32[8,128,128]{2,1,0:T(8,128)S(1)}, u32[]{:S(2)}, u32[]{:S(2)}) collective-permute-start(f32[8,128,128]{2,1,0:T(8,128)S(1)} %get-tuple-element.84), channel_id=1, source_target_pairs={{0,16},{1,17},{2,18},{3,19},{4,20},{5,21},{6,22},{7,23},{8,24},{9,... | collective-permute-start | bytes 1572872 | tf_op jit(solution)/shard_map/ppermute | solution.py:138
  88.8 1.3 collective-permute-start.19
  90.1 5.5 %collective-permute-start.12 = (f32[8,128,128]{2,1,0:T(8,128)S(1)}, f32[8,128,128]{2,1,0:T(8,128)S(1)}, u32[]{:S(2)}, u32[]{:S(2)}) collective-permute-start(f32[8,128,128]{2,1,0:T(8,128)S(1)} %get-tuple-element.85), channel_id=1, source_target_pairs={{0,4},{1,5},{2,6},{3,7},{4,8},{5,9},{6,10},{7,11},{8,12},{9,13},{1... | collective-permute-start | bytes 1572872 | tf_op jit(solution)/shard_map/ppermute | solution.py:138
  95.8 1.3 collective-permute-start.23
  97.2 4.0 %collective-permute-start.16 = (f32[8,128,128]{2,1,0:T(8,128)S(1)}, f32[8,128,128]{2,1,0:T(8,128)S(1)}, u32[]{:S(2)}, u32[]{:S(2)}) collective-permute-start(f32[8,128,128]{2,1,0:T(8,128)S(1)} %multiply_add_fusion.12), channel_id=1, source_target_pairs={{0,2},{1,3},{2,4},{3,5},{4,6},{5,7},{6,8},{7,9},{8,10},{9,11},{10,... | collective-permute-start | bytes 1572872 | tf_op jit(solution)/shard_map/ppermute | solution.py:138
  101.8 12.6 %collective-permute-start.13 = (f32[8,128,128]{2,1,0:T(8,128)S(1)}, f32[8,128,128]{2,1,0:T(8,128)S(1)}, u32[]{:S(2)}, u32[]{:S(2)}) collective-permute-start(f32[8,128,128]{2,1,0:T(8,128)S(1)} %multiply_add_fusion.16), channel_id=1, source_target_pairs={{0,8},{1,9},{2,10},{3,11},{4,12},{5,13},{6,14},{7,15},{8,16},{9,17... | collective-permute-start | bytes 1572872 | tf_op jit(solution)/shard_map/ppermute | solution.py:138
  114.5 1.3 collective-permute-start.20
  116.1 8.8 %collective-permute-start.17 = (f32[8,128,128]{2,1,0:T(8,128)S(1)}, f32[8,128,128]{2,1,0:T(8,128)S(1)}, u32[]{:S(2)}, u32[]{:S(2)}) collective-permute-start(f32[8,128,128]{2,1,0:T(8,128)S(1)} %get-tuple-element.88), channel_id=1, source_target_pairs={{0,4},{1,5},{2,6},{3,7},{4,8},{5,9},{6,10},{7,11},{8,12},{9,13},{1... | collective-permute-start | bytes 1572872 | tf_op jit(solution)/shard_map/ppermute | solution.py:138
  124.9 25.1 %collective-permute-done.13 = f32[8,128,128]{2,1,0:T(8,128)S(1)} collective-permute-done((f32[8,128,128]{2,1,0:T(8,128)S(1)}, f32[8,128,128]{2,1,0:T(8,128)S(1)}, u32[]{:S(2)}, u32[]{:S(2)}) %collective-permute-start.13) | collective-permute-done | bytes 524320 | tf_op jit(solution)/shard_map/ppermute | solution.py:138
  150.1 4.4 %collective-permute-start.14 = (f32[8,128,128]{2,1,0:T(8,128)S(1)}, f32[8,128,128]{2,1,0:T(8,128)S(1)}, u32[]{:S(2)}, u32[]{:S(2)}) collective-permute-start(f32[8,128,128]{2,1,0:T(8,128)S(1)} %multiply_add_fusion.15), channel_id=1, source_target_pairs={{0,16},{1,17},{2,18},{3,19},{4,20},{5,21},{6,22},{7,23},{8,24},{9,... | collective-permute-start | bytes 1572872 | tf_op jit(solution)/shard_map/ppermute | solution.py:138
  154.6 1.3 collective-permute-start.21
  155.9 1.3 collective-permute-start.24
  157.3 1.4 multiply_add_fusion.10
  158.6 6.4 %collective-permute-done.14 = f32[8,128,128]{2,1,0:T(8,128)S(1)} collective-permute-done((f32[8,128,128]{2,1,0:T(8,128)S(1)}, f32[8,128,128]{2,1,0:T(8,128)S(1)}, u32[]{:S(2)}, u32[]{:S(2)}) %collective-permute-start.14) | collective-permute-done | bytes 524320 | tf_op jit(solution)/shard_map/ppermute | solution.py:138
  165.1 1.2 multiply_add_fusion.14
  166.3 2.5 %fusion.11 = (f32[16,128,128]{2,1,0:T(8,128)S(1)}, f32[16,128,128]{2,1,0:T(8,128)}) fusion(f32[16,128,128]{2,1,0:T(8,128)} %collective-permute-done.3, f32[32,128,128]{2,1,0:T(8,128)S(1)} %copy-done.2, s32[]{:T(128)S(6)} %select_n.674, f32[8,128,128]{2,1,0:T(8,128)S(1)} %multiply_add_fusion.10, f32[8,128,128]{2,1,0:T(8,128)S(1)} %multiply_add_fusion.14, ...), kind=kLoop, calls=%fused_computation.20 | loop fusion | flops 1572864 | bytes 5242949 | tf_op jit(solution)/shard_map/jit(_where)/select_n | solution.py:225
  169.0 1.7 collective-permute-done.21
  170.7 1.4 multiply_add_fusion.6
  172.1 1.2 multiply_add_fusion.2
  173.4 1.7 fusion.13
  175.0 1.7 collective-permute-start.25
  177.4 3.3 %maximum_select_fusion.s_ref = f32[32,128,128]{2,1,0:T(8,128)} fusion(f32[16,128,128]{2,1,0:T(8,128)} %collective-permute-done.18, f32[16,128,128]{2,1,0:T(8,128)S(1)} %get-tuple-element.54, pred[]{:T(512)S(6)} %eq.7), kind=kLoop, calls=%fused_computation.1 | loop fusion | flops 1572864 | bytes 4194305 | tf_op jit(solution)/shard_map/jit(_where)/select_n | solution.py:232
  180.6 1.6 maximum_select_fusion.1.gs_ref
  182.3 13.7 %shard_map.84 = (bf16[128,4096]{1,0:T(8,128)(2,1)}, bf16[128,4096]{1,0:T(8,128)(2,1)}, bf16[128,4096]{1,0:T(8,128)(2,1)}, bf16[128,4096]{1,0:T(8,128)(2,1)}) custom-call(bf16[128,4096]{1,0:T(8,128)(2,1)} %q_ref, bf16[128,4096]{1,0:T(8,128)(2,1)} %k_ref, bf16[128,4096]{1,0:T(8,128)(2,1)} %v_ref, bf16[128,4096]{1,0:T(8,128)(2,1)} %g_ref, f32[32,128]{1,0:T(8,128)} %bitcast.152, ...), custom_call_target="tpu_custom_call" | custom-call | tf_op jit(solution)/shard_map/pallas_call | solution.py:93
  (84 shorter events, 11.0 us)
Async XLA Ops:
  0.6 7.4 %copy-start.7 = (bf16[128,4096]{1,0:T(8,128)(2,1)S(1)}, bf16[128,4096]{1,0:T(8,128)(2,1)}, u32[]{:S(2)}) copy-start(bf16[128,4096]{1,0:T(8,128)(2,1)} %g_ref) | copy-start | bytes 3145732
  1.5 3.9 %collective-permute-start = (f32[1,32]{1,0:T(1,128)S(1)}, f32[1,32]{1,0:T(1,128)S(1)}, u32[]{:S(2)}, u32[]{:S(2)}) collective-permute-start(f32[1,32]{1,0:T(1,128)S(1)} %bitcast.153), channel_id=1, source_target_pairs={{0,1},{1,2},{2,3},{3,4},{4,5},{5,6},{6,7},{7,8},{8,9},{9,10},{10,1... | collective-permute-start | bytes 392 | tf_op jit(solution)/shard_map/ppermute | solution.py:106
  11.9 16.2 %collective-permute-start.6 = (f32[16,128,128]{2,1,0:T(8,128)}, f32[16,128,128]{2,1,0:T(8,128)S(1)}, u32[]{:S(2)}, u32[]{:S(2)}) collective-permute-start(f32[16,128,128]{2,1,0:T(8,128)} %constant_dynamic-slice_fusion.16), channel_id=1, source_target_pairs={{0,1},{1,0},{2,3},{3,2},{4,5},{5,4},{6,7},{7,6},{8,9},{9,8},{10,11... | collective-permute-start | bytes 3145736 | tf_op jit(solution)/shard_map/ppermute | solution.py:168
  23.3 1.3 copy-start
  25.7 8.6 %collective-permute-start.3 = (f32[16,128,128]{2,1,0:T(8,128)}, f32[16,128,128]{2,1,0:T(8,128)}, u32[]{:S(2)}, u32[]{:S(2)}) collective-permute-start(f32[16,128,128]{2,1,0:T(8,128)} %constant_dynamic-slice_fusion.17), channel_id=1, source_target_pairs={{0,1},{1,0},{2,3},{3,2},{4,5},{5,4},{6,7},{7,6},{8,9},{9,8},{10,11... | collective-permute-start | bytes 3145736 | tf_op jit(solution)/shard_map/ppermute | solution.py:168
  25.7 2.3 %collective-permute-start.2 = (f32[32]{0:T(128)S(1)}, f32[32]{0:T(128)S(1)}, u32[]{:S(2)}, u32[]{:S(2)}) collective-permute-start(f32[32]{0:T(128)S(1)} %convert_reduce_fusion), channel_id=1, source_target_pairs={{0,1},{1,0},{2,3},{3,2},{4,5},{5,4},{6,7},{7,6},{8,9},{9,8},{10,11... | collective-permute-start | bytes 392 | tf_op jit(solution)/shard_map/ppermute | solution.py:168
  28.1 1.0 copy-start.5
  29.1 5.2 %copy-start.1 = (f32[32,128,128]{2,1,0:T(8,128)S(1)}, f32[32,128,128]{2,1,0:T(8,128)}, u32[]{:S(2)}) copy-start(f32[32,128,128]{2,1,0:T(8,128)} %copy-done) | copy-start | bytes 6291460
  31.7 25.2 %collective-permute-start.8 = (f32[8,128,128]{2,1,0:T(8,128)}, f32[8,128,128]{2,1,0:T(8,128)}, u32[]{:S(2)}, u32[]{:S(2)}) collective-permute-start(f32[8,128,128]{2,1,0:T(8,128)} %get-tuple-element.60), channel_id=1, source_target_pairs={{8,0},{9,1},{10,2},{11,3},{12,4},{13,5},{14,6},{15,7},{16,8},{17,9... | collective-permute-start | bytes 1572872 | tf_op jit(solution)/shard_map/ppermute | solution.py:190
  33.0 23.9 %collective-permute-start.7 = (f32[8,128,128]{2,1,0:T(8,128)}, f32[8,128,128]{2,1,0:T(8,128)}, u32[]{:S(2)}, u32[]{:S(2)}) collective-permute-start(f32[8,128,128]{2,1,0:T(8,128)} %get-tuple-element.61), channel_id=1, source_target_pairs={{2,0},{3,1},{4,2},{5,3},{6,4},{7,5},{8,6},{9,7},{10,8},{11,9},{12,... | collective-permute-start | bytes 1572872 | tf_op jit(solution)/shard_map/ppermute | solution.py:190
  35.7 1.0 copy-start.3
  37.8 26.8 %collective-permute-start.5 = (f32[8,128,128]{2,1,0:T(8,128)}, f32[8,128,128]{2,1,0:T(8,128)}, u32[]{:S(2)}, u32[]{:S(2)}) collective-permute-start(f32[8,128,128]{2,1,0:T(8,128)} %get-tuple-element.62), channel_id=1, source_target_pairs={{0,8},{1,9},{2,10},{3,11},{4,12},{5,13},{6,14},{7,15},{8,16},{9,17... | collective-permute-start | bytes 1572872 | tf_op jit(solution)/shard_map/ppermute | solution.py:190
  43.2 21.4 %collective-permute-start.4 = (f32[8,128,128]{2,1,0:T(8,128)}, f32[8,128,128]{2,1,0:T(8,128)}, u32[]{:S(2)}, u32[]{:S(2)}) collective-permute-start(f32[8,128,128]{2,1,0:T(8,128)} %get-tuple-element.63), channel_id=1, source_target_pairs={{0,2},{1,3},{2,4},{3,5},{4,6},{5,7},{6,8},{7,9},{8,10},{9,11},{10,... | collective-permute-start | bytes 1572872 | tf_op jit(solution)/shard_map/ppermute | solution.py:190
  47.4 9.5 %collective-permute-start.1 = (f32[2,32]{1,0:T(2,128)S(1)}, f32[2,32]{1,0:T(2,128)S(1)}, u32[]{:S(2)}, u32[]{:S(2)}) collective-permute-start(f32[2,32]{1,0:T(2,128)S(1)} %pad_maximum_fusion.6), channel_id=1, source_target_pairs={{0,2},{1,3},{2,4},{3,5},{4,6},{5,7},{6,8},{7,9},{8,10},{9,11},{10,... | collective-permute-start | bytes 776 | tf_op jit(solution)/shard_map/ppermute | solution.py:106
  64.6 6.0 %collective-permute-start.9 = (f32[4,32]{1,0:T(4,128)S(1)}, f32[4,32]{1,0:T(4,128)S(1)}, u32[]{:S(2)}, u32[]{:S(2)}) collective-permute-start(f32[4,32]{1,0:T(4,128)S(1)} %pad_maximum_fusion.5), channel_id=1, source_target_pairs={{0,4},{1,5},{2,6},{3,7},{4,8},{5,9},{6,10},{7,11},{8,12},{9,13},{1... | collective-permute-start | bytes 1544 | tf_op jit(solution)/shard_map/ppermute | solution.py:106
  70.7 3.7 %collective-permute-start.10 = (f32[8,32]{1,0:T(8,128)S(1)}, f32[8,32]{1,0:T(8,128)S(1)}, u32[]{:S(2)}, u32[]{:S(2)}) collective-permute-start(f32[8,32]{1,0:T(8,128)S(1)} %pad_maximum_fusion.4), channel_id=1, source_target_pairs={{0,8},{1,9},{2,10},{3,11},{4,12},{5,13},{6,14},{7,15},{8,16},{9,17... | collective-permute-start | bytes 3080 | tf_op jit(solution)/shard_map/ppermute | solution.py:106
  74.4 4.1 %collective-permute-start.11 = (f32[16,32]{1,0:T(8,128)S(1)}, f32[16,32]{1,0:T(8,128)S(1)}, u32[]{:S(2)}, u32[]{:S(2)}) collective-permute-start(f32[16,32]{1,0:T(8,128)S(1)} %pad_maximum_fusion.3), channel_id=1, source_target_pairs={{0,16},{1,17},{2,18},{3,19},{4,20},{5,21},{6,22},{7,23},{8,24},{9,... | collective-permute-start | bytes 6152 | tf_op jit(solution)/shard_map/ppermute | solution.py:106
  81.9 13.8 %collective-permute-start.22 = (f32[8,128,128]{2,1,0:T(8,128)S(1)}, f32[8,128,128]{2,1,0:T(8,128)S(1)}, u32[]{:S(2)}, u32[]{:S(2)}) collective-permute-start(f32[8,128,128]{2,1,0:T(8,128)S(1)} %get-tuple-element.57), channel_id=1, source_target_pairs={{16,0},{17,1},{18,2},{19,3},{20,4},{21,5},{22,6},{23,7},{24,8},{25... | collective-permute-start | bytes 1572872 | tf_op jit(solution)/shard_map/ppermute | solution.py:138
  83.2 13.9 %collective-permute-start.15 = (f32[8,128,128]{2,1,0:T(8,128)S(1)}, f32[8,128,128]{2,1,0:T(8,128)S(1)}, u32[]{:S(2)}, u32[]{:S(2)}) collective-permute-start(f32[8,128,128]{2,1,0:T(8,128)S(1)} %get-tuple-element.84), channel_id=1, source_target_pairs={{0,16},{1,17},{2,18},{3,19},{4,20},{5,21},{6,22},{7,23},{8,24},{9,... | collective-permute-start | bytes 1572872 | tf_op jit(solution)/shard_map/ppermute | solution.py:138
  88.8 25.6 %collective-permute-start.19 = (f32[8,128,128]{2,1,0:T(8,128)S(1)}, f32[8,128,128]{2,1,0:T(8,128)S(1)}, u32[]{:S(2)}, u32[]{:S(2)}) collective-permute-start(f32[8,128,128]{2,1,0:T(8,128)S(1)} %get-tuple-element.56), channel_id=1, source_target_pairs={{4,0},{5,1},{6,2},{7,3},{8,4},{9,5},{10,6},{11,7},{12,8},{13,9},{1... | collective-permute-start | bytes 1572872 | tf_op jit(solution)/shard_map/ppermute | solution.py:138
  90.1 11.6 %collective-permute-start.12 = (f32[8,128,128]{2,1,0:T(8,128)S(1)}, f32[8,128,128]{2,1,0:T(8,128)S(1)}, u32[]{:S(2)}, u32[]{:S(2)}) collective-permute-start(f32[8,128,128]{2,1,0:T(8,128)S(1)} %get-tuple-element.85), channel_id=1, source_target_pairs={{0,4},{1,5},{2,6},{3,7},{4,8},{5,9},{6,10},{7,11},{8,12},{9,13},{1... | collective-permute-start | bytes 1572872 | tf_op jit(solution)/shard_map/ppermute | solution.py:138
  95.8 20.1 %collective-permute-start.23 = (f32[8,128,128]{2,1,0:T(8,128)S(1)}, f32[8,128,128]{2,1,0:T(8,128)S(1)}, u32[]{:S(2)}, u32[]{:S(2)}) collective-permute-start(f32[8,128,128]{2,1,0:T(8,128)S(1)} %multiply_add_fusion.4), channel_id=1, source_target_pairs={{2,0},{3,1},{4,2},{5,3},{6,4},{7,5},{8,6},{9,7},{10,8},{11,9},{12,... | collective-permute-start | bytes 1572872 | tf_op jit(solution)/shard_map/ppermute | solution.py:138
  97.2 18.6 %collective-permute-start.16 = (f32[8,128,128]{2,1,0:T(8,128)S(1)}, f32[8,128,128]{2,1,0:T(8,128)S(1)}, u32[]{:S(2)}, u32[]{:S(2)}) collective-permute-start(f32[8,128,128]{2,1,0:T(8,128)S(1)} %multiply_add_fusion.12), channel_id=1, source_target_pairs={{0,2},{1,3},{2,4},{3,5},{4,6},{5,7},{6,8},{7,9},{8,10},{9,11},{10,... | collective-permute-start | bytes 1572872 | tf_op jit(solution)/shard_map/ppermute | solution.py:138
  101.8 48.1 %collective-permute-start.13 = (f32[8,128,128]{2,1,0:T(8,128)S(1)}, f32[8,128,128]{2,1,0:T(8,128)S(1)}, u32[]{:S(2)}, u32[]{:S(2)}) collective-permute-start(f32[8,128,128]{2,1,0:T(8,128)S(1)} %multiply_add_fusion.16), channel_id=1, source_target_pairs={{0,8},{1,9},{2,10},{3,11},{4,12},{5,13},{6,14},{7,15},{8,16},{9,17... | collective-permute-start | bytes 1572872 | tf_op jit(solution)/shard_map/ppermute | solution.py:138
  114.5 40.0 %collective-permute-start.20 = (f32[8,128,128]{2,1,0:T(8,128)S(1)}, f32[8,128,128]{2,1,0:T(8,128)S(1)}, u32[]{:S(2)}, u32[]{:S(2)}) collective-permute-start(f32[8,128,128]{2,1,0:T(8,128)S(1)} %multiply_add_fusion.8), channel_id=1, source_target_pairs={{8,0},{9,1},{10,2},{11,3},{12,4},{13,5},{14,6},{15,7},{16,8},{17,9... | collective-permute-start | bytes 1572872 | tf_op jit(solution)/shard_map/ppermute | solution.py:138
  116.1 41.2 %collective-permute-start.17 = (f32[8,128,128]{2,1,0:T(8,128)S(1)}, f32[8,128,128]{2,1,0:T(8,128)S(1)}, u32[]{:S(2)}, u32[]{:S(2)}) collective-permute-start(f32[8,128,128]{2,1,0:T(8,128)S(1)} %get-tuple-element.88), channel_id=1, source_target_pairs={{0,4},{1,5},{2,6},{3,7},{4,8},{5,9},{6,10},{7,11},{8,12},{9,13},{1... | collective-permute-start | bytes 1572872 | tf_op jit(solution)/shard_map/ppermute | solution.py:138
  150.1 15.0 %collective-permute-start.14 = (f32[8,128,128]{2,1,0:T(8,128)S(1)}, f32[8,128,128]{2,1,0:T(8,128)S(1)}, u32[]{:S(2)}, u32[]{:S(2)}) collective-permute-start(f32[8,128,128]{2,1,0:T(8,128)S(1)} %multiply_add_fusion.15), channel_id=1, source_target_pairs={{0,16},{1,17},{2,18},{3,19},{4,20},{5,21},{6,22},{7,23},{8,24},{9,... | collective-permute-start | bytes 1572872 | tf_op jit(solution)/shard_map/ppermute | solution.py:138
  154.6 16.1 %collective-permute-start.21 = (f32[8,128,128]{2,1,0:T(8,128)S(1)}, f32[8,128,128]{2,1,0:T(8,128)S(1)}, u32[]{:S(2)}, u32[]{:S(2)}) collective-permute-start(f32[8,128,128]{2,1,0:T(8,128)S(1)} %multiply_add_fusion.7), channel_id=1, source_target_pairs={{16,0},{17,1},{18,2},{19,3},{20,4},{21,5},{22,6},{23,7},{24,8},{25... | collective-permute-start | bytes 1572872 | tf_op jit(solution)/shard_map/ppermute | solution.py:138
  155.9 16.2 %collective-permute-start.24 = (f32[8,128,128]{2,1,0:T(8,128)S(1)}, f32[8,128,128]{2,1,0:T(8,128)S(1)}, u32[]{:S(2)}, u32[]{:S(2)}) collective-permute-start(f32[8,128,128]{2,1,0:T(8,128)S(1)} %get-tuple-element.87), channel_id=1, source_target_pairs={{4,0},{5,1},{6,2},{7,3},{8,4},{9,5},{10,6},{11,7},{12,8},{13,9},{1... | collective-permute-start | bytes 1572872 | tf_op jit(solution)/shard_map/ppermute | solution.py:138
  157.2 9.1 %copy-start.2 = (f32[32,128,128]{2,1,0:T(8,128)S(1)}, f32[32,128,128]{2,1,0:T(8,128)}, u32[]{:S(2)}) copy-start(f32[32,128,128]{2,1,0:T(8,128)} %copy-done) | copy-start | bytes 6291460
  168.9 8.5 %collective-permute-start.18 = (f32[16,128,128]{2,1,0:T(8,128)}, f32[16,128,128]{2,1,0:T(8,128)}, u32[]{:S(2)}, u32[]{:S(2)}) collective-permute-start(f32[16,128,128]{2,1,0:T(8,128)} %get-tuple-element.55), channel_id=1, source_target_pairs={{0,1},{1,0},{2,3},{3,2},{4,5},{5,4},{6,7},{7,6},{8,9},{9,8},{10,11... | collective-permute-start | bytes 3145736 | tf_op jit(solution)/shard_map/ppermute | solution.py:229
  170.7 2.7 %copy-start.6 = (f32[16,128,128]{2,1,0:T(8,128)S(1)}, f32[16,128,128]{2,1,0:T(8,128)}, u32[]{:S(2)}) copy-start(f32[16,128,128]{2,1,0:T(8,128)} %copy-done.5) | copy-start | bytes 3145732
  175.0 5.6 %collective-permute-start.25 = (f32[16,128,128]{2,1,0:T(8,128)}, f32[16,128,128]{2,1,0:T(8,128)S(1)}, u32[]{:S(2)}, u32[]{:S(2)}) collective-permute-start(f32[16,128,128]{2,1,0:T(8,128)} %get-tuple-element.53), channel_id=1, source_target_pairs={{0,1},{1,0},{2,3},{3,2},{4,5},{5,4},{6,7},{7,6},{8,9},{9,8},{10,11... | collective-permute-start | bytes 3145736 | tf_op jit(solution)/shard_map/ppermute | solution.py:229
  177.4 3.3 %copy-start.4 = (f32[16,128,128]{2,1,0:T(8,128)S(1)}, f32[16,128,128]{2,1,0:T(8,128)}, u32[]{:S(2)}) copy-start(f32[16,128,128]{2,1,0:T(8,128)} %get-tuple-element.52) | copy-start | bytes 3145732

commit v6 on v3

--- a/solution.py
+++ b/solution.py
@@ -103,15 +103,25 @@
 def gather_rows(row, axis):
     count = lax.axis_size(axis)
     me = lax.axis_index(axis)
-    known = row[None]
+    back = row[None]
+    ahead = row[None]
     early = None
     step = 1
-    while step < count:
-        pairs = [(i, (i + step) % count) for i in range(count)]
-        known = jnp.concatenate([known, lax.ppermute(known, axis, pairs)], 0)
-        early = known if early is None else early
+    while 2 * step <= count // 2:
+        down = [(i, (i + step) % count) for i in range(count)]
+        up = [(i, (i - step) % count) for i in range(count)]
+        back = jnp.concatenate([back, lax.ppermute(back, axis, down)], 0)
+        ahead = jnp.concatenate([ahead, lax.ppermute(ahead, axis, up)], 0)
+        early = (back, ahead) if early is None else early
         step *= 2
-    return known[(me - jnp.arange(count)) % count], early
+    reach = back.shape[0]
+    devices = jnp.arange(count)
+    from_back = back[jnp.clip(me - devices, 0, reach - 1)]
+    from_ahead = ahead[jnp.clip(devices - me, 0, reach - 1)]
+    near_back = ((me - devices >= 0) & (me - devices < reach))[:, None]
+    near_ahead = ((devices - me > 0) & (devices - me < reach))[:, None]
+    rows = jnp.where(near_back, from_back, jnp.where(near_ahead, from_ahead, jnp.zeros_like(from_back)))
+    return rows, early
 
 
 def window_sum(ordered, place, first, last):

time: 176 us -> 192 us (1.091)
  starting transfers between devices: 52.6 us -> 80.9 us
  waiting for transfers between devices: 78.8 us -> 65.4 us
    ppermute x16, starting transfers between devices: 41.5 us -> 60.7 us  [chip_scan(): received = lax.ppermute(sent, axis, pairs)]
    ppermute x5 -> x8, starting transfers between devices: 0.99 us -> 12.7 us  [the longest x4 8.24 us: gather_rows(): ahead = jnp.concatenate([ahead, lax.ppermute(ahead, axis, up)], 0)]
    ppermute x5 -> x8, waiting for transfers between devices: 12 us -> 4.81 us  [the longest x4 2.93 us: gather_rows(): back = jnp.concatenate([back, lax.ppermute(back, axis, down)], 0)]
    ppermute x16, waiting for transfers between devices: 66.8 us -> 60.6 us  [chip_scan(): received = lax.ppermute(sent, axis, pairs)]
    ppermute x3, starting transfers between devices: 8.34 us -> 5.78 us  [shards(): other_total, other_state, other_grad = lax.ppermute(sent, axis, partner)]
  transfers between devices with their start and end apart: 26 -> 29, of which waited for: 10 -> 11; matrix products, arithmetic and copies ran while one was open for 13% -> 12% of each run, Pallas kernels for 0% -> 0%
where the time goes in v6:
time: 192 us; the launch traced here: 191 us
  starting transfers between devices  80.9 us (42%)
  waiting for transfers between devices  65.4 us (34%)
  other arithmetic  13.7 us (7%)
  Pallas kernels  13.7 us (7%)
  local copies, waits for them, and re-layouts  12.3 us (6%)
  matrix products  4.02 us (2%)
    ppermute x16, starting transfers between devices, chip_scan(): received = lax.ppermute(sent, axis, pairs)  60.7 us
    ppermute x16, waiting for transfers between devices, chip_scan(): received = lax.ppermute(sent, axis, pairs)  60.6 us
    pallas_call x1, Pallas kernels, finish(): pl.pallas_call(head_kernel, grid=(heads // block,), in_specs=[tile] * 4 +...  13.7 us
    ppermute x4, starting transfers between devices, gather_rows(): ahead = jnp.concatenate([ahead, lax.ppermute(ahead, axis, up)], 0)  8.24 us
    ppermute x3, starting transfers between devices, shards(): other_total, other_state, other_grad = lax.ppermute(sent, axis, partner)  5.78 us
    select_n x2, other arithmetic, assemble(): jnp.where(first, jnp.concatenate([keep, got], 0), jnp.concatenate([got, k...  4.82 us
    ppermute x4, starting transfers between devices, gather_rows(): back = jnp.concatenate([back, lax.ppermute(back, axis, down)], 0)  4.41 us
    unnamed x16, local copies, waits for them, and re-layouts  3.97 us
  transfers between devices with their start and end apart: 29, of which 11 were waited for; matrix products, arithmetic and copies ran while one was open for 12% of the time, Pallas kernels for 0%

profile of v6, /device:TPU:1, one launch (start us, length us, event | category | flops | bytes accessed | tf_op | source)
XLA Modules:
  0.0 191.3 jit_solution(9647945580569455816)
XLA Ops:
  0.6 0.9 convert_reduce_fusion
  1.5 3.3 %collective-permute-start.1 = (f32[1,32]{1,0:T(1,128)S(1)}, f32[1,32]{1,0:T(1,128)S(1)}, u32[]{:S(2)}, u32[]{:S(2)}) collective-permute-start(f32[1,32]{1,0:T(1,128)S(1)} %bitcast.171), channel_id=1, source_target_pairs={{0,31},{1,0},{2,1},{3,2},{4,3},{5,4},{6,5},{7,6},{8,7},{9,8},{10,9... | collective-permute-start | bytes 392 | tf_op jit(solution)/shard_map/ppermute | solution.py:114
  4.9 2.9 %collective-permute-start.2 = (f32[32]{0:T(128)S(1)}, f32[32]{0:T(128)S(1)}, u32[]{:S(2)}, u32[]{:S(2)}) collective-permute-start(f32[32]{0:T(128)S(1)} %convert_reduce_fusion), channel_id=1, source_target_pairs={{0,1},{1,0},{2,3},{3,2},{4,5},{5,4},{6,7},{7,6},{8,9},{9,8},{10,11... | collective-permute-start | bytes 392 | tf_op jit(solution)/shard_map/ppermute | solution.py:178
  9.1 4.8 %collective-permute-start.8 = (f32[2,32]{1,0:T(2,128)S(1)}, f32[2,32]{1,0:T(2,128)S(1)}, u32[]{:S(2)}, u32[]{:S(2)}) collective-permute-start(f32[2,32]{1,0:T(2,128)S(1)} %get-tuple-element.94), channel_id=1, source_target_pairs={{0,30},{1,31},{2,0},{3,1},{4,2},{5,3},{6,4},{7,5},{8,6},{9,7},{10,... | collective-permute-start | bytes 776 | tf_op jit(solution)/shard_map/ppermute | solution.py:114
  13.8 1.5 copy.18
  15.3 1.3 fusion
  16.6 1.3 copy-done
  18.0 1.0 constant_dynamic-slice_fusion.18
  19.0 2.3 %collective-permute-start.19 = (f32[16,128,128]{2,1,0:T(8,128)}, f32[16,128,128]{2,1,0:T(8,128)}, u32[]{:S(2)}, u32[]{:S(2)}) collective-permute-start(f32[16,128,128]{2,1,0:T(8,128)} %constant_dynamic-slice_fusion.18), channel_id=1, source_target_pairs={{0,1},{1,0},{2,3},{3,2},{4,5},{5,4},{6,7},{7,6},{8,9},{9,8},{10,11... | collective-permute-start | bytes 3145736 | tf_op jit(solution)/shard_map/ppermute | solution.py:178
  21.3 1.6 copy.17
  23.0 2.8 %fusion.2 = f32[32,128,128]{2,1,0:T(8,128)S(1)} fusion(f32[128,32,128]{0,2,1:T(8,128)} %bitcast.169, f32[128,32]{0,1:T(8,128)S(1)} %copy.11, bf16[128,4096]{1,0:T(8,128)(2,1)S(1)} %copy-done.6), kind=kOutput, calls=%fused_computation.6 | convolution fusion | flops 805830656 | bytes 5259264 | tf_op jit(solution)/shard_map/she,shf->hef/dot_general | solution.py:27
  25.7 1.0 constant_dynamic-slice_fusion.19
  27.5 3.0 %collective-permute-start.6 = (f32[4,32]{1,0:T(4,128)S(1)}, f32[4,32]{1,0:T(4,128)S(1)}, u32[]{:S(2)}, u32[]{:S(2)}) collective-permute-start(f32[4,32]{1,0:T(4,128)S(1)} %get-tuple-element.93), channel_id=1, source_target_pairs={{0,4},{1,5},{2,6},{3,7},{4,8},{5,9},{6,10},{7,11},{8,12},{9,13},{1... | collective-permute-start | bytes 1544 | tf_op jit(solution)/shard_map/ppermute | solution.py:113
  30.5 0.9 collective-permute-done.9
  31.4 2.2 %collective-permute-done.6 = f32[4,32]{1,0:T(4,128)S(1)} collective-permute-done((f32[4,32]{1,0:T(4,128)S(1)}, f32[4,32]{1,0:T(4,128)S(1)}, u32[]{:S(2)}, u32[]{:S(2)}) %collective-permute-start.6) | collective-permute-done | bytes 544 | tf_op jit(solution)/shard_map/ppermute | solution.py:113
  33.7 1.5 collective-permute-start.7
  35.1 1.0 collective-permute-done.10
  38.7 1.7 multiply_add_fusion
  40.6 1.5 collective-permute-start.20
  42.0 1.3 collective-permute-start.24
  44.3 6.6 %collective-permute-start.4 = (f32[8,128,128]{2,1,0:T(8,128)S(1)}, f32[8,128,128]{2,1,0:T(8,128)S(1)}, u32[]{:S(2)}, u32[]{:S(2)}) collective-permute-start(f32[8,128,128]{2,1,0:T(8,128)S(1)} %get-tuple-element.58), channel_id=1, source_target_pairs={{0,2},{1,3},{2,4},{3,5},{4,6},{5,7},{6,8},{7,9},{8,10},{9,11},{10,... | collective-permute-start | bytes 1572872 | tf_op jit(solution)/shard_map/ppermute | solution.py:149
  50.9 4.0 %collective-permute-start.14 = (f32[8,128,128]{2,1,0:T(8,128)S(1)}, f32[8,128,128]{2,1,0:T(8,128)S(1)}, u32[]{:S(2)}, u32[]{:S(2)}) collective-permute-start(f32[8,128,128]{2,1,0:T(8,128)S(1)} %get-tuple-element.59), channel_id=1, source_target_pairs={{0,8},{1,9},{2,10},{3,11},{4,12},{5,13},{6,14},{7,15},{8,16},{9,17... | collective-permute-start | bytes 1572872 | tf_op jit(solution)/shard_map/ppermute | solution.py:149
  54.9 1.2 collective-permute-done.20
  56.1 2.6 %collective-permute-done.24 = f32[8,128,128]{2,1,0:T(8,128)S(1)} collective-permute-done((f32[8,128,128]{2,1,0:T(8,128)S(1)}, f32[8,128,128]{2,1,0:T(8,128)S(1)}, u32[]{:S(2)}, u32[]{:S(2)}) %collective-permute-start.24) | collective-permute-done | bytes 524320 | tf_op jit(solution)/shard_map/ppermute | solution.py:149
  58.9 1.3 collective-permute-start.21
  60.3 1.3 collective-permute-start.25
  61.6 13.7 %collective-permute-done.14 = f32[8,128,128]{2,1,0:T(8,128)S(1)} collective-permute-done((f32[8,128,128]{2,1,0:T(8,128)S(1)}, f32[8,128,128]{2,1,0:T(8,128)S(1)}, u32[]{:S(2)}, u32[]{:S(2)}) %collective-permute-start.14) | collective-permute-done | bytes 524320 | tf_op jit(solution)/shard_map/ppermute | solution.py:149
  75.5 1.3 collective-permute-start.11
  76.8 6.8 %collective-permute-start.15 = (f32[8,128,128]{2,1,0:T(8,128)S(1)}, f32[8,128,128]{2,1,0:T(8,128)S(1)}, u32[]{:S(2)}, u32[]{:S(2)}) collective-permute-start(f32[8,128,128]{2,1,0:T(8,128)S(1)} %get-tuple-element.57), channel_id=1, source_target_pairs={{0,16},{1,17},{2,18},{3,19},{4,20},{5,21},{6,22},{7,23},{8,24},{9,... | collective-permute-start | bytes 1572872 | tf_op jit(solution)/shard_map/ppermute | solution.py:149
  83.7 1.3 collective-permute-start.22
  85.0 16.0 %collective-permute-done.25 = f32[8,128,128]{2,1,0:T(8,128)S(1)} collective-permute-done((f32[8,128,128]{2,1,0:T(8,128)S(1)}, f32[8,128,128]{2,1,0:T(8,128)S(1)}, u32[]{:S(2)}, u32[]{:S(2)}) %collective-permute-start.25) | collective-permute-done | bytes 524320 | tf_op jit(solution)/shard_map/ppermute | solution.py:149
  101.2 1.3 collective-permute-start.26
  102.6 1.3 collective-permute-start.12
  103.9 1.4 collective-permute-done.15
  105.5 3.2 %collective-permute-start.16 = (f32[8,128,128]{2,1,0:T(8,128)S(1)}, f32[8,128,128]{2,1,0:T(8,128)S(1)}, u32[]{:S(2)}, u32[]{:S(2)}) collective-permute-start(f32[8,128,128]{2,1,0:T(8,128)S(1)} %multiply_add_fusion.12), channel_id=1, source_target_pairs={{0,2},{1,3},{2,4},{3,5},{4,6},{5,7},{6,8},{7,9},{8,10},{9,11},{10,... | collective-permute-start | bytes 1572872 | tf_op jit(solution)/shard_map/ppermute | solution.py:149
  108.8 1.3 collective-permute-start.23
  110.1 5.9 %collective-permute-done.26 = f32[8,128,128]{2,1,0:T(8,128)S(1)} collective-permute-done((f32[8,128,128]{2,1,0:T(8,128)S(1)}, f32[8,128,128]{2,1,0:T(8,128)S(1)}, u32[]{:S(2)}, u32[]{:S(2)}) %collective-permute-start.26) | collective-permute-done | bytes 524320 | tf_op jit(solution)/shard_map/ppermute | solution.py:149
  116.2 1.3 collective-permute-start.27
  117.6 25.7 %collective-permute-start.13 = (f32[8,128,128]{2,1,0:T(8,128)S(1)}, f32[8,128,128]{2,1,0:T(8,128)S(1)}, u32[]{:S(2)}, u32[]{:S(2)}) collective-permute-start(f32[8,128,128]{2,1,0:T(8,128)S(1)} %multiply_add_fusion.15), channel_id=1, source_target_pairs={{0,16},{1,17},{2,18},{3,19},{4,20},{5,21},{6,22},{7,23},{8,24},{9,... | collective-permute-start | bytes 1572872 | tf_op jit(solution)/shard_map/ppermute | solution.py:149
  143.5 1.3 collective-permute-start.17
  144.8 19.6 %collective-permute-done.23 = f32[8,128,128]{2,1,0:T(8,128)S(1)} collective-permute-done((f32[8,128,128]{2,1,0:T(8,128)S(1)}, f32[8,128,128]{2,1,0:T(8,128)S(1)}, u32[]{:S(2)}, u32[]{:S(2)}) %collective-permute-start.23) | collective-permute-done | bytes 524320 | tf_op jit(solution)/shard_map/ppermute | solution.py:149
  164.9 1.1 copy-done.1
  166.1 1.3 fusion.13
  167.4 1.7 collective-permute-start.28
  170.3 1.6 fusion.11
  172.6 3.3 %maximum_select_fusion.1.gs_ref = f32[32,128,128]{2,1,0:T(8,128)} fusion(f32[16,128,128]{2,1,0:T(8,128)} %collective-permute-done.28, f32[16,128,128]{2,1,0:T(8,128)S(1)} %get-tuple-element.48, pred[]{:T(512)S(6)} %eq.5), kind=kLoop, calls=%fused_computation.3 | loop fusion | flops 1572864 | bytes 4194305 | tf_op jit(solution)/shard_map/jit(_where)/select_n | solution.py:226
  175.9 1.5 maximum_select_fusion.s_ref
  177.5 13.7 %shard_map.84 = (bf16[128,4096]{1,0:T(8,128)(2,1)}, bf16[128,4096]{1,0:T(8,128)(2,1)}, bf16[128,4096]{1,0:T(8,128)(2,1)}, bf16[128,4096]{1,0:T(8,128)(2,1)}) custom-call(bf16[128,4096]{1,0:T(8,128)(2,1)} %q_ref, bf16[128,4096]{1,0:T(8,128)(2,1)} %k_ref, bf16[128,4096]{1,0:T(8,128)(2,1)} %v_ref, bf16[128,4096]{1,0:T(8,128)(2,1)} %g_ref, f32[32,128]{1,0:T(8,128)} %bitcast.170, ...), custom_call_target="tpu_custom_call" | custom-call | tf_op jit(solution)/shard_map/pallas_call | solution.py:93
  (97 shorter events, 9.3 us)
Async XLA Ops:
  0.6 14.7 %copy-start.7 = (bf16[128,4096]{1,0:T(8,128)(2,1)S(1)}, bf16[128,4096]{1,0:T(8,128)(2,1)}, u32[]{:S(2)}) copy-start(bf16[128,4096]{1,0:T(8,128)(2,1)} %g_ref) | copy-start | bytes 3145732
  1.5 7.5 %collective-permute-start.1 = (f32[1,32]{1,0:T(1,128)S(1)}, f32[1,32]{1,0:T(1,128)S(1)}, u32[]{:S(2)}, u32[]{:S(2)}) collective-permute-start(f32[1,32]{1,0:T(1,128)S(1)} %bitcast.171), channel_id=1, source_target_pairs={{0,31},{1,0},{2,1},{3,2},{4,3},{5,4},{6,5},{7,6},{8,7},{9,8},{10,9... | collective-permute-start | bytes 392 | tf_op jit(solution)/shard_map/ppermute | solution.py:114
  4.9 4.2 %collective-permute-start = (f32[1,32]{1,0:T(1,128)S(1)}, f32[1,32]{1,0:T(1,128)S(1)}, u32[]{:S(2)}, u32[]{:S(2)}) collective-permute-start(f32[1,32]{1,0:T(1,128)S(1)} %bitcast.172), channel_id=1, source_target_pairs={{0,1},{1,2},{2,3},{3,4},{4,5},{5,6},{6,7},{7,8},{8,9},{9,10},{10,1... | collective-permute-start | bytes 392 | tf_op jit(solution)/shard_map/ppermute | solution.py:113
  4.9 25.6 %collective-permute-start.2 = (f32[32]{0:T(128)S(1)}, f32[32]{0:T(128)S(1)}, u32[]{:S(2)}, u32[]{:S(2)}) collective-permute-start(f32[32]{0:T(128)S(1)} %convert_reduce_fusion), channel_id=1, source_target_pairs={{0,1},{1,0},{2,3},{3,2},{4,5},{5,4},{6,7},{7,6},{8,9},{9,8},{10,11... | collective-permute-start | bytes 392 | tf_op jit(solution)/shard_map/ppermute | solution.py:178
  9.1 18.3 %collective-permute-start.8 = (f32[2,32]{1,0:T(2,128)S(1)}, f32[2,32]{1,0:T(2,128)S(1)}, u32[]{:S(2)}, u32[]{:S(2)}) collective-permute-start(f32[2,32]{1,0:T(2,128)S(1)} %get-tuple-element.94), channel_id=1, source_target_pairs={{0,30},{1,31},{2,0},{3,1},{4,2},{5,3},{6,4},{7,5},{8,6},{9,7},{10,... | collective-permute-start | bytes 776 | tf_op jit(solution)/shard_map/ppermute | solution.py:114
  13.8 13.5 %collective-permute-start.5 = (f32[2,32]{1,0:T(2,128)S(1)}, f32[2,32]{1,0:T(2,128)S(1)}, u32[]{:S(2)}, u32[]{:S(2)}) collective-permute-start(f32[2,32]{1,0:T(2,128)S(1)} %get-tuple-element.95), channel_id=1, source_target_pairs={{0,2},{1,3},{2,4},{3,5},{4,6},{5,7},{6,8},{7,9},{8,10},{9,11},{10,... | collective-permute-start | bytes 776 | tf_op jit(solution)/shard_map/ppermute | solution.py:113
  16.6 1.4 copy-start
  18.0 3.4 %copy-start.5 = (bf16[128,4096]{1,0:T(8,128)(2,1)S(1)}, bf16[128,4096]{1,0:T(8,128)(2,1)}, u32[]{:S(2)}) copy-start(bf16[128,4096]{1,0:T(8,128)(2,1)} %k_ref) | copy-start | bytes 3145732
  19.0 4.0 %copy-start.6 = (bf16[128,4096]{1,0:T(8,128)(2,1)S(1)}, bf16[128,4096]{1,0:T(8,128)(2,1)}, u32[]{:S(2)}) copy-start(bf16[128,4096]{1,0:T(8,128)(2,1)} %v_ref) | copy-start | bytes 3145732
  19.0 19.7 %collective-permute-start.19 = (f32[16,128,128]{2,1,0:T(8,128)}, f32[16,128,128]{2,1,0:T(8,128)}, u32[]{:S(2)}, u32[]{:S(2)}) collective-permute-start(f32[16,128,128]{2,1,0:T(8,128)} %constant_dynamic-slice_fusion.18), channel_id=1, source_target_pairs={{0,1},{1,0},{2,3},{3,2},{4,5},{5,4},{6,7},{7,6},{8,9},{9,8},{10,11... | collective-permute-start | bytes 3145736 | tf_op jit(solution)/shard_map/ppermute | solution.py:178
  26.8 16.5 %collective-permute-start.3 = (f32[16,128,128]{2,1,0:T(8,128)}, f32[16,128,128]{2,1,0:T(8,128)S(1)}, u32[]{:S(2)}, u32[]{:S(2)}) collective-permute-start(f32[16,128,128]{2,1,0:T(8,128)} %constant_dynamic-slice_fusion.19), channel_id=1, source_target_pairs={{0,1},{1,0},{2,3},{3,2},{4,5},{5,4},{6,7},{7,6},{8,9},{9,8},{10,11... | collective-permute-start | bytes 3145736 | tf_op jit(solution)/shard_map/ppermute | solution.py:178
  27.4 4.0 %collective-permute-start.9 = (f32[4,32]{1,0:T(4,128)S(1)}, f32[4,32]{1,0:T(4,128)S(1)}, u32[]{:S(2)}, u32[]{:S(2)}) collective-permute-start(f32[4,32]{1,0:T(4,128)S(1)} %get-tuple-element.92), channel_id=1, source_target_pairs={{0,28},{1,29},{2,30},{3,31},{4,0},{5,1},{6,2},{7,3},{8,4},{9,5},{1... | collective-permute-start | bytes 1544 | tf_op jit(solution)/shard_map/ppermute | solution.py:114
  27.5 6.1 %collective-permute-start.6 = (f32[4,32]{1,0:T(4,128)S(1)}, f32[4,32]{1,0:T(4,128)S(1)}, u32[]{:S(2)}, u32[]{:S(2)}) collective-permute-start(f32[4,32]{1,0:T(4,128)S(1)} %get-tuple-element.93), channel_id=1, source_target_pairs={{0,4},{1,5},{2,6},{3,7},{4,8},{5,9},{6,10},{7,11},{8,12},{9,13},{1... | collective-permute-start | bytes 1544 | tf_op jit(solution)/shard_map/ppermute | solution.py:113
  33.6 2.5 %collective-permute-start.10 = (f32[8,32]{1,0:T(8,128)S(1)}, f32[8,32]{1,0:T(8,128)S(1)}, u32[]{:S(2)}, u32[]{:S(2)}) collective-permute-start(f32[8,32]{1,0:T(8,128)S(1)} %get-tuple-element.90), channel_id=1, source_target_pairs={{0,24},{1,25},{2,26},{3,27},{4,28},{5,29},{6,30},{7,31},{8,0},{9,1... | collective-permute-start | bytes 3080 | tf_op jit(solution)/shard_map/ppermute | solution.py:114
  33.7 3.7 %collective-permute-start.7 = (f32[8,32]{1,0:T(8,128)S(1)}, f32[8,32]{1,0:T(8,128)S(1)}, u32[]{:S(2)}, u32[]{:S(2)}) collective-permute-start(f32[8,32]{1,0:T(8,128)S(1)} %get-tuple-element.91), channel_id=1, source_target_pairs={{0,8},{1,9},{2,10},{3,11},{4,12},{5,13},{6,14},{7,15},{8,16},{9,17... | collective-permute-start | bytes 3080 | tf_op jit(solution)/shard_map/ppermute | solution.py:113
  40.6 15.6 %collective-permute-start.20 = (f32[8,128,128]{2,1,0:T(8,128)S(1)}, f32[8,128,128]{2,1,0:T(8,128)S(1)}, u32[]{:S(2)}, u32[]{:S(2)}) collective-permute-start(f32[8,128,128]{2,1,0:T(8,128)S(1)} %get-tuple-element.54), channel_id=1, source_target_pairs={{2,0},{3,1},{4,2},{5,3},{6,4},{7,5},{8,6},{9,7},{10,8},{11,9},{12,... | collective-permute-start | bytes 1572872 | tf_op jit(solution)/shard_map/ppermute | solution.py:149
  42.0 16.7 %collective-permute-start.24 = (f32[8,128,128]{2,1,0:T(8,128)S(1)}, f32[8,128,128]{2,1,0:T(8,128)S(1)}, u32[]{:S(2)}, u32[]{:S(2)}) collective-permute-start(f32[8,128,128]{2,1,0:T(8,128)S(1)} %get-tuple-element.55), channel_id=1, source_target_pairs={{8,0},{9,1},{10,2},{11,3},{12,4},{13,5},{14,6},{15,7},{16,8},{17,9... | collective-permute-start | bytes 1572872 | tf_op jit(solution)/shard_map/ppermute | solution.py:149
  43.3 1.0 copy-start.3
  44.3 17.2 %collective-permute-start.4 = (f32[8,128,128]{2,1,0:T(8,128)S(1)}, f32[8,128,128]{2,1,0:T(8,128)S(1)}, u32[]{:S(2)}, u32[]{:S(2)}) collective-permute-start(f32[8,128,128]{2,1,0:T(8,128)S(1)} %get-tuple-element.58), channel_id=1, source_target_pairs={{0,2},{1,3},{2,4},{3,5},{4,6},{5,7},{6,8},{7,9},{8,10},{9,11},{10,... | collective-permute-start | bytes 1572872 | tf_op jit(solution)/shard_map/ppermute | solution.py:149
  50.9 24.4 %collective-permute-start.14 = (f32[8,128,128]{2,1,0:T(8,128)S(1)}, f32[8,128,128]{2,1,0:T(8,128)S(1)}, u32[]{:S(2)}, u32[]{:S(2)}) collective-permute-start(f32[8,128,128]{2,1,0:T(8,128)S(1)} %get-tuple-element.59), channel_id=1, source_target_pairs={{0,8},{1,9},{2,10},{3,11},{4,12},{5,13},{6,14},{7,15},{8,16},{9,17... | collective-permute-start | bytes 1572872 | tf_op jit(solution)/shard_map/ppermute | solution.py:149
  58.9 24.7 %collective-permute-start.21 = (f32[8,128,128]{2,1,0:T(8,128)S(1)}, f32[8,128,128]{2,1,0:T(8,128)S(1)}, u32[]{:S(2)}, u32[]{:S(2)}) collective-permute-start(f32[8,128,128]{2,1,0:T(8,128)S(1)} %get-tuple-element.52), channel_id=1, source_target_pairs={{4,0},{5,1},{6,2},{7,3},{8,4},{9,5},{10,6},{11,7},{12,8},{13,9},{1... | collective-permute-start | bytes 1572872 | tf_op jit(solution)/shard_map/ppermute | solution.py:149
  60.3 40.8 %collective-permute-start.25 = (f32[8,128,128]{2,1,0:T(8,128)S(1)}, f32[8,128,128]{2,1,0:T(8,128)S(1)}, u32[]{:S(2)}, u32[]{:S(2)}) collective-permute-start(f32[8,128,128]{2,1,0:T(8,128)S(1)} %get-tuple-element.53), channel_id=1, source_target_pairs={{16,0},{17,1},{18,2},{19,3},{20,4},{21,5},{22,6},{23,7},{24,8},{25... | collective-permute-start | bytes 1572872 | tf_op jit(solution)/shard_map/ppermute | solution.py:149
  75.5 27.0 %collective-permute-start.11 = (f32[8,128,128]{2,1,0:T(8,128)S(1)}, f32[8,128,128]{2,1,0:T(8,128)S(1)}, u32[]{:S(2)}, u32[]{:S(2)}) collective-permute-start(f32[8,128,128]{2,1,0:T(8,128)S(1)} %get-tuple-element.56), channel_id=1, source_target_pairs={{0,4},{1,5},{2,6},{3,7},{4,8},{5,9},{6,10},{7,11},{8,12},{9,13},{1... | collective-permute-start | bytes 1572872 | tf_op jit(solution)/shard_map/ppermute | solution.py:149
  76.8 28.5 %collective-permute-start.15 = (f32[8,128,128]{2,1,0:T(8,128)S(1)}, f32[8,128,128]{2,1,0:T(8,128)S(1)}, u32[]{:S(2)}, u32[]{:S(2)}) collective-permute-start(f32[8,128,128]{2,1,0:T(8,128)S(1)} %get-tuple-element.57), channel_id=1, source_target_pairs={{0,16},{1,17},{2,18},{3,19},{4,20},{5,21},{6,22},{7,23},{8,24},{9,... | collective-permute-start | bytes 1572872 | tf_op jit(solution)/shard_map/ppermute | solution.py:149
  83.7 25.0 %collective-permute-start.22 = (f32[8,128,128]{2,1,0:T(8,128)S(1)}, f32[8,128,128]{2,1,0:T(8,128)S(1)}, u32[]{:S(2)}, u32[]{:S(2)}) collective-permute-start(f32[8,128,128]{2,1,0:T(8,128)S(1)} %multiply_add_fusion.8), channel_id=1, source_target_pairs={{8,0},{9,1},{10,2},{11,3},{12,4},{13,5},{14,6},{15,7},{16,8},{17,9... | collective-permute-start | bytes 1572872 | tf_op jit(solution)/shard_map/ppermute | solution.py:149
  101.2 14.9 %collective-permute-start.26 = (f32[8,128,128]{2,1,0:T(8,128)S(1)}, f32[8,128,128]{2,1,0:T(8,128)S(1)}, u32[]{:S(2)}, u32[]{:S(2)}) collective-permute-start(f32[8,128,128]{2,1,0:T(8,128)S(1)} %multiply_add_fusion.4), channel_id=1, source_target_pairs={{2,0},{3,1},{4,2},{5,3},{6,4},{7,5},{8,6},{9,7},{10,8},{11,9},{12,... | collective-permute-start | bytes 1572872 | tf_op jit(solution)/shard_map/ppermute | solution.py:149
  102.6 14.9 %collective-permute-start.12 = (f32[8,128,128]{2,1,0:T(8,128)S(1)}, f32[8,128,128]{2,1,0:T(8,128)S(1)}, u32[]{:S(2)}, u32[]{:S(2)}) collective-permute-start(f32[8,128,128]{2,1,0:T(8,128)S(1)} %multiply_add_fusion.16), channel_id=1, source_target_pairs={{0,8},{1,9},{2,10},{3,11},{4,12},{5,13},{6,14},{7,15},{8,16},{9,17... | collective-permute-start | bytes 1572872 | tf_op jit(solution)/shard_map/ppermute | solution.py:149
  105.5 37.9 %collective-permute-start.16 = (f32[8,128,128]{2,1,0:T(8,128)S(1)}, f32[8,128,128]{2,1,0:T(8,128)S(1)}, u32[]{:S(2)}, u32[]{:S(2)}) collective-permute-start(f32[8,128,128]{2,1,0:T(8,128)S(1)} %multiply_add_fusion.12), channel_id=1, source_target_pairs={{0,2},{1,3},{2,4},{3,5},{4,6},{5,7},{6,8},{7,9},{8,10},{9,11},{10,... | collective-permute-start | bytes 1572872 | tf_op jit(solution)/shard_map/ppermute | solution.py:149
  108.8 55.6 %collective-permute-start.23 = (f32[8,128,128]{2,1,0:T(8,128)S(1)}, f32[8,128,128]{2,1,0:T(8,128)S(1)}, u32[]{:S(2)}, u32[]{:S(2)}) collective-permute-start(f32[8,128,128]{2,1,0:T(8,128)S(1)} %multiply_add_fusion.7), channel_id=1, source_target_pairs={{16,0},{17,1},{18,2},{19,3},{20,4},{21,5},{22,6},{23,7},{24,8},{25... | collective-permute-start | bytes 1572872 | tf_op jit(solution)/shard_map/ppermute | solution.py:149
  116.2 48.5 %collective-permute-start.27 = (f32[8,128,128]{2,1,0:T(8,128)S(1)}, f32[8,128,128]{2,1,0:T(8,128)S(1)}, u32[]{:S(2)}, u32[]{:S(2)}) collective-permute-start(f32[8,128,128]{2,1,0:T(8,128)S(1)} %multiply_add_fusion.3), channel_id=1, source_target_pairs={{4,0},{5,1},{6,2},{7,3},{8,4},{9,5},{10,6},{11,7},{12,8},{13,9},{1... | collective-permute-start | bytes 1572872 | tf_op jit(solution)/shard_map/ppermute | solution.py:149
  117.6 51.4 %collective-permute-start.13 = (f32[8,128,128]{2,1,0:T(8,128)S(1)}, f32[8,128,128]{2,1,0:T(8,128)S(1)}, u32[]{:S(2)}, u32[]{:S(2)}) collective-permute-start(f32[8,128,128]{2,1,0:T(8,128)S(1)} %multiply_add_fusion.15), channel_id=1, source_target_pairs={{0,16},{1,17},{2,18},{3,19},{4,20},{5,21},{6,22},{7,23},{8,24},{9,... | collective-permute-start | bytes 1572872 | tf_op jit(solution)/shard_map/ppermute | solution.py:149
  143.5 25.8 %collective-permute-start.17 = (f32[8,128,128]{2,1,0:T(8,128)S(1)}, f32[8,128,128]{2,1,0:T(8,128)S(1)}, u32[]{:S(2)}, u32[]{:S(2)}) collective-permute-start(f32[8,128,128]{2,1,0:T(8,128)S(1)} %multiply_add_fusion.11), channel_id=1, source_target_pairs={{0,4},{1,5},{2,6},{3,7},{4,8},{5,9},{6,10},{7,11},{8,12},{9,13},{1... | collective-permute-start | bytes 1572872 | tf_op jit(solution)/shard_map/ppermute | solution.py:149
  164.5 1.6 copy-start.1
  167.4 5.3 %collective-permute-start.28 = (f32[16,128,128]{2,1,0:T(8,128)}, f32[16,128,128]{2,1,0:T(8,128)}, u32[]{:S(2)}, u32[]{:S(2)}) collective-permute-start(f32[16,128,128]{2,1,0:T(8,128)} %get-tuple-element.49), channel_id=1, source_target_pairs={{0,1},{1,0},{2,3},{3,2},{4,5},{5,4},{6,7},{7,6},{8,9},{9,8},{10,11... | collective-permute-start | bytes 3145736 | tf_op jit(solution)/shard_map/ppermute | solution.py:223
  169.1 1.2 copy-start.4
  172.0 4.0 %collective-permute-start.18 = (f32[16,128,128]{2,1,0:T(8,128)}, f32[16,128,128]{2,1,0:T(8,128)S(1)}, u32[]{:S(2)}, u32[]{:S(2)}) collective-permute-start(f32[16,128,128]{2,1,0:T(8,128)} %get-tuple-element.51), channel_id=1, source_target_pairs={{0,1},{1,0},{2,3},{3,2},{4,5},{5,4},{6,7},{7,6},{8,9},{9,8},{10,11... | collective-permute-start | bytes 3145736 | tf_op jit(solution)/shard_map/ppermute | solution.py:223
  172.6 3.3 %copy-start.2 = (f32[16,128,128]{2,1,0:T(8,128)S(1)}, f32[16,128,128]{2,1,0:T(8,128)}, u32[]{:S(2)}) copy-start(f32[16,128,128]{2,1,0:T(8,128)} %get-tuple-element.50) | copy-start | bytes 3145732

commit v7 on v3

--- a/solution.py
+++ b/solution.py
@@ -56,6 +56,7 @@
     block = cum_ref.shape[0]
     dk = q_ref.shape[1] // block
     later = lax.broadcasted_iota(jnp.int32, (size, size), 0) >= lax.broadcasted_iota(jnp.int32, (size, size), 1)
+    columns = cum_ref[...].T
     for j in range(block):
         cols = slice(j * dk, (j + 1) * dk)
         q = q_ref[:, cols]
@@ -63,22 +64,23 @@
         v = v_ref[:, cols]
         g = g_ref[:, cols]
         row = cum_ref[j:j + 1, :]
-        grid_row = jnp.broadcast_to(row, (size, size))
-        col = jnp.sum(jnp.where(later & (~(lax.broadcasted_iota(jnp.int32, (size, size), 0) >
-                                           lax.broadcasted_iota(jnp.int32, (size, size), 1))), grid_row, 0.0),
-                      axis=1, keepdims=True)
+        col = columns[:, j:j + 1]
         last = row[:, size - 1:size]
         weights = jnp.where(later, jnp.exp(jnp.where(later, col - row, 0.0)), 0.0)
         scores = mm(q, k, nt) * weights
         grad_scores = mm(g, v, nt) * weights
         qd = jnp.exp(col)
         kd = jnp.exp(last - col)
-        state = s_ref[j]
-        grad_in = gs_ref[j]
-        att_ref[:, cols] = (mm_left(scores, v, nn) + qd * mm_right(q, state, nn)).astype(att_ref.dtype)
-        qg_ref[:, cols] = (mm_left(grad_scores, k, nn) + qd * mm_right(g, state, nt)).astype(qg_ref.dtype)
-        kg_ref[:, cols] = (mm_left(grad_scores.T, q, nn) + kd * mm_right(v, grad_in, nt)).astype(kg_ref.dtype)
-        vg_ref[:, cols] = (mm_left(scores.T, g, nn) + kd * mm_right(k, grad_in, nn)).astype(vg_ref.dtype)
+        state_high, state_low = split(s_ref[j])
+        grad_high, grad_low = split(gs_ref[j])
+
+        def carried(a, high, low, dims):
+            return mm(a, high, dims) + mm(a, low, dims)
+
+        att_ref[:, cols] = (mm_left(scores, v, nn) + qd * carried(q, state_high, state_low, nn)).astype(att_ref.dtype)
+        qg_ref[:, cols] = (mm_left(grad_scores, k, nn) + qd * carried(g, state_high, state_low, nt)).astype(qg_ref.dtype)
+        kg_ref[:, cols] = (mm_left(grad_scores.T, q, nn) + kd * carried(v, grad_high, grad_low, nt)).astype(kg_ref.dtype)
+        vg_ref[:, cols] = (mm_left(scores.T, g, nn) + kd * carried(k, grad_high, grad_low, nn)).astype(vg_ref.dtype)
 
 
 def finish(inputs, cumul_heads, state_in, grad_in):

time: 176 us -> 177 us (level)
  no operation moved by 1% of the time
where the time goes in v7:
time: 177 us; the launch traced here: 176 us
  waiting for transfers between devices  78.8 us (45%)
  starting transfers between devices  52.6 us (30%)
  Pallas kernels  14.1 us (8%)
  other arithmetic  13.6 us (8%)
  local copies, waits for them, and re-layouts  11.7 us (7%)
  matrix products  4.02 us (2%)
    ppermute x16, waiting for transfers between devices, chip_scan(): received = lax.ppermute(sent, axis, pairs)  66.8 us
    ppermute x16, starting transfers between devices, chip_scan(): received = lax.ppermute(sent, axis, pairs)  41.5 us
    pallas_call x1, Pallas kernels, finish(): pl.pallas_call(head_kernel, grid=(heads // block,), in_specs=[tile] * 4 +...  14.1 us
    ppermute x5, waiting for transfers between devices, gather_rows(): known = jnp.concatenate([known, lax.ppermute(known, axis, pairs)], 0)  12 us
    ppermute x3, starting transfers between devices, shards(): other_total, other_state, other_grad = lax.ppermute(sent, axis, partner)  8.34 us
    select_n x2, other arithmetic, assemble(): jnp.where(first, jnp.concatenate([keep, got], 0), jnp.concatenate([got, k...  4.8 us
    unnamed x16, local copies, waits for them, and re-layouts  3.93 us
  transfers between devices with their start and end apart: 26, of which 10 were waited for; matrix products, arithmetic and copies ran while one was open for 13% of the time, Pallas kernels for 0%

profile of v7, /device:TPU:1, one launch (start us, length us, event | category | flops | bytes accessed | tf_op | source)
XLA Modules:
  0.0 176.1 jit_solution(7235567440677971518)
XLA Ops:
  0.6 0.9 convert_reduce_fusion
  1.5 3.3 %collective-permute-start.1 = (f32[32]{0:T(128)S(1)}, f32[32]{0:T(128)S(1)}, u32[]{:S(2)}, u32[]{:S(2)}) collective-permute-start(f32[32]{0:T(128)S(1)} %convert_reduce_fusion), channel_id=1, source_target_pairs={{0,1},{1,0},{2,3},{3,2},{4,5},{5,4},{6,7},{7,6},{8,9},{9,8},{10,11... | collective-permute-start | bytes 392 | tf_op jit(solution)/shard_map/ppermute | solution.py:170
  4.9 0.8 copy.9
  6.1 0.7 collective-permute-start.4
  6.9 1.5 copy.18
  8.4 1.3 fusion
  9.6 1.3 copy-done
  11.0 1.0 constant_dynamic-slice_fusion.18
  12.0 4.5 %collective-permute-start.16 = (f32[16,128,128]{2,1,0:T(8,128)}, f32[16,128,128]{2,1,0:T(8,128)}, u32[]{:S(2)}, u32[]{:S(2)}) collective-permute-start(f32[16,128,128]{2,1,0:T(8,128)} %constant_dynamic-slice_fusion.18), channel_id=1, source_target_pairs={{0,1},{1,0},{2,3},{3,2},{4,5},{5,4},{6,7},{7,6},{8,9},{9,8},{10,11... | collective-permute-start | bytes 3145736 | tf_op jit(solution)/shard_map/ppermute | solution.py:170
  16.5 1.6 copy.17
  18.1 2.8 %fusion.2 = f32[32,128,128]{2,1,0:T(8,128)S(1)} fusion(f32[128,32,128]{0,2,1:T(8,128)} %bitcast.167, f32[128,32]{0,1:T(8,128)S(1)} %copy.11, bf16[128,4096]{1,0:T(8,128)(2,1)S(1)} %copy-done.6), kind=kOutput, calls=%fused_computation.5 | convolution fusion | flops 805830656 | bytes 5259264 | tf_op jit(solution)/shard_map/she,shf->hef/dot_general | solution.py:27
  21.0 1.0 constant_dynamic-slice_fusion.19
  22.6 4.4 %collective-permute-done.5 = f32[4,32]{1,0:T(4,128)S(1)} collective-permute-done((f32[4,32]{1,0:T(4,128)S(1)}, f32[4,32]{1,0:T(4,128)S(1)}, u32[]{:S(2)}, u32[]{:S(2)}) %collective-permute-start.5) | collective-permute-done | bytes 544 | tf_op jit(solution)/shard_map/ppermute | solution.py:113
  27.2 3.6 %collective-permute-done.6 = f32[8,32]{1,0:T(8,128)S(1)} collective-permute-done((f32[8,32]{1,0:T(8,128)S(1)}, f32[8,32]{1,0:T(8,128)S(1)}, u32[]{:S(2)}, u32[]{:S(2)}) %collective-permute-start.6) | collective-permute-done | bytes 1056 | tf_op jit(solution)/shard_map/ppermute | solution.py:113
  30.9 4.0 %collective-permute-done.7 = f32[16,32]{1,0:T(8,128)S(1)} collective-permute-done((f32[16,32]{1,0:T(8,128)S(1)}, f32[16,32]{1,0:T(8,128)S(1)}, u32[]{:S(2)}, u32[]{:S(2)}) %collective-permute-start.7) | collective-permute-done | bytes 2080 | tf_op jit(solution)/shard_map/ppermute | solution.py:113
  36.0 1.7 multiply_add_fusion
  37.8 1.3 collective-permute-start.17
  39.1 1.3 collective-permute-start.21
  41.4 4.0 %collective-permute-start.3 = (f32[8,128,128]{2,1,0:T(8,128)S(1)}, f32[8,128,128]{2,1,0:T(8,128)S(1)}, u32[]{:S(2)}, u32[]{:S(2)}) collective-permute-start(f32[8,128,128]{2,1,0:T(8,128)S(1)} %get-tuple-element.58), channel_id=1, source_target_pairs={{0,2},{1,3},{2,4},{3,5},{4,6},{5,7},{6,8},{7,9},{8,10},{9,11},{10,... | collective-permute-start | bytes 1572872 | tf_op jit(solution)/shard_map/ppermute | solution.py:141
  45.4 4.0 %collective-permute-start.11 = (f32[8,128,128]{2,1,0:T(8,128)S(1)}, f32[8,128,128]{2,1,0:T(8,128)S(1)}, u32[]{:S(2)}, u32[]{:S(2)}) collective-permute-start(f32[8,128,128]{2,1,0:T(8,128)S(1)} %get-tuple-element.59), channel_id=1, source_target_pairs={{0,8},{1,9},{2,10},{3,11},{4,12},{5,13},{6,14},{7,15},{8,16},{9,17... | collective-permute-start | bytes 1572872 | tf_op jit(solution)/shard_map/ppermute | solution.py:141
  49.4 2.2 %collective-permute-done.21 = f32[8,128,128]{2,1,0:T(8,128)S(1)} collective-permute-done((f32[8,128,128]{2,1,0:T(8,128)S(1)}, f32[8,128,128]{2,1,0:T(8,128)S(1)}, u32[]{:S(2)}, u32[]{:S(2)}) %collective-permute-start.21) | collective-permute-done | bytes 524320 | tf_op jit(solution)/shard_map/ppermute | solution.py:141
  51.8 1.3 collective-permute-start.18
  53.2 1.3 collective-permute-start.22
  54.5 14.4 %collective-permute-done.11 = f32[8,128,128]{2,1,0:T(8,128)S(1)} collective-permute-done((f32[8,128,128]{2,1,0:T(8,128)S(1)}, f32[8,128,128]{2,1,0:T(8,128)S(1)}, u32[]{:S(2)}, u32[]{:S(2)}) %collective-permute-start.11) | collective-permute-done | bytes 524320 | tf_op jit(solution)/shard_map/ppermute | solution.py:141
  69.1 1.3 collective-permute-start.8
  70.4 6.8 %collective-permute-start.12 = (f32[8,128,128]{2,1,0:T(8,128)S(1)}, f32[8,128,128]{2,1,0:T(8,128)S(1)}, u32[]{:S(2)}, u32[]{:S(2)}) collective-permute-start(f32[8,128,128]{2,1,0:T(8,128)S(1)} %get-tuple-element.57), channel_id=1, source_target_pairs={{0,16},{1,17},{2,18},{3,19},{4,20},{5,21},{6,22},{7,23},{8,24},{9,... | collective-permute-start | bytes 1572872 | tf_op jit(solution)/shard_map/ppermute | solution.py:141
  77.3 1.3 collective-permute-start.19
  78.6 16.7 %collective-permute-done.22 = f32[8,128,128]{2,1,0:T(8,128)S(1)} collective-permute-done((f32[8,128,128]{2,1,0:T(8,128)S(1)}, f32[8,128,128]{2,1,0:T(8,128)S(1)}, u32[]{:S(2)}, u32[]{:S(2)}) %collective-permute-start.22) | collective-permute-done | bytes 524320 | tf_op jit(solution)/shard_map/ppermute | solution.py:141
  95.4 1.3 collective-permute-start.23
  96.9 1.3 collective-permute-start.9
  98.2 0.7 collective-permute-done.12
  99.1 3.4 %collective-permute-start.13 = (f32[8,128,128]{2,1,0:T(8,128)S(1)}, f32[8,128,128]{2,1,0:T(8,128)S(1)}, u32[]{:S(2)}, u32[]{:S(2)}) collective-permute-start(f32[8,128,128]{2,1,0:T(8,128)S(1)} %multiply_add_fusion.12), channel_id=1, source_target_pairs={{0,2},{1,3},{2,4},{3,5},{4,6},{5,7},{6,8},{7,9},{8,10},{9,11},{10,... | collective-permute-start | bytes 1572872 | tf_op jit(solution)/shard_map/ppermute | solution.py:141
  102.6 1.3 collective-permute-start.20
  103.9 6.4 %collective-permute-done.23 = f32[8,128,128]{2,1,0:T(8,128)S(1)} collective-permute-done((f32[8,128,128]{2,1,0:T(8,128)S(1)}, f32[8,128,128]{2,1,0:T(8,128)S(1)}, u32[]{:S(2)}, u32[]{:S(2)}) %collective-permute-start.23) | collective-permute-done | bytes 524320 | tf_op jit(solution)/shard_map/ppermute | solution.py:141
  110.5 1.5 collective-permute-start.24
  111.9 6.8 %collective-permute-done.9 = f32[8,128,128]{2,1,0:T(8,128)S(1)} collective-permute-done((f32[8,128,128]{2,1,0:T(8,128)S(1)}, f32[8,128,128]{2,1,0:T(8,128)S(1)}, u32[]{:S(2)}, u32[]{:S(2)}) %collective-permute-start.9) | collective-permute-done | bytes 524320 | tf_op jit(solution)/shard_map/ppermute | solution.py:141
  118.8 8.9 %collective-permute-start.10 = (f32[8,128,128]{2,1,0:T(8,128)S(1)}, f32[8,128,128]{2,1,0:T(8,128)S(1)}, u32[]{:S(2)}, u32[]{:S(2)}) collective-permute-start(f32[8,128,128]{2,1,0:T(8,128)S(1)} %multiply_add_fusion.15), channel_id=1, source_target_pairs={{0,16},{1,17},{2,18},{3,19},{4,20},{5,21},{6,22},{7,23},{8,24},{9,... | collective-permute-start | bytes 1572872 | tf_op jit(solution)/shard_map/ppermute | solution.py:141
  127.8 1.3 collective-permute-start.14
  129.2 19.6 %collective-permute-done.20 = f32[8,128,128]{2,1,0:T(8,128)S(1)} collective-permute-done((f32[8,128,128]{2,1,0:T(8,128)S(1)}, f32[8,128,128]{2,1,0:T(8,128)S(1)}, u32[]{:S(2)}, u32[]{:S(2)}) %collective-permute-start.20) | collective-permute-done | bytes 524320 | tf_op jit(solution)/shard_map/ppermute | solution.py:141
  149.3 1.1 copy-done.1
  150.4 1.3 fusion.13
  151.7 1.7 collective-permute-start.25
  153.9 0.8 copy-done.4
  154.7 1.6 fusion.11
  156.3 0.7 copy.10
  157.0 3.3 %maximum_select_fusion.1.gs_ref = f32[32,128,128]{2,1,0:T(8,128)} fusion(f32[16,128,128]{2,1,0:T(8,128)} %collective-permute-done.25, f32[16,128,128]{2,1,0:T(8,128)S(1)} %get-tuple-element.48, pred[]{:T(512)S(6)} %eq.7), kind=kLoop, calls=%fused_computation.2 | loop fusion | flops 1572864 | bytes 4194305 | tf_op jit(solution)/shard_map/jit(_where)/select_n | solution.py:218
  160.3 1.5 maximum_select_fusion.s_ref
  161.8 14.1 %shard_map.84 = (bf16[128,4096]{1,0:T(8,128)(2,1)}, bf16[128,4096]{1,0:T(8,128)(2,1)}, bf16[128,4096]{1,0:T(8,128)(2,1)}, bf16[128,4096]{1,0:T(8,128)(2,1)}) custom-call(bf16[128,4096]{1,0:T(8,128)(2,1)} %q_ref, bf16[128,4096]{1,0:T(8,128)(2,1)} %k_ref, bf16[128,4096]{1,0:T(8,128)(2,1)} %v_ref, bf16[128,4096]{1,0:T(8,128)(2,1)} %g_ref, f32[32,128]{1,0:T(8,128)} %bitcast.168, ...), custom_call_target="tpu_custom_call" | custom-call | tf_op jit(solution)/shard_map/pallas_call | solution.py:95
  (84 shorter events, 5.8 us)
Async XLA Ops:
  0.6 7.7 %copy-start.7 = (bf16[128,4096]{1,0:T(8,128)(2,1)S(1)}, bf16[128,4096]{1,0:T(8,128)(2,1)}, u32[]{:S(2)}) copy-start(bf16[128,4096]{1,0:T(8,128)(2,1)} %g_ref) | copy-start | bytes 3145732
  1.5 25.6 %collective-permute-start.1 = (f32[32]{0:T(128)S(1)}, f32[32]{0:T(128)S(1)}, u32[]{:S(2)}, u32[]{:S(2)}) collective-permute-start(f32[32]{0:T(128)S(1)} %convert_reduce_fusion), channel_id=1, source_target_pairs={{0,1},{1,0},{2,3},{3,2},{4,5},{5,4},{6,7},{7,6},{8,9},{9,8},{10,11... | collective-permute-start | bytes 392 | tf_op jit(solution)/shard_map/ppermute | solution.py:170
  4.9 1.2 collective-permute-start
  6.1 14.8 %collective-permute-start.4 = (f32[2,32]{1,0:T(2,128)S(1)}, f32[2,32]{1,0:T(2,128)S(1)}, u32[]{:S(2)}, u32[]{:S(2)}) collective-permute-start(f32[2,32]{1,0:T(2,128)S(1)} %pad_maximum_fusion.4), channel_id=1, source_target_pairs={{0,2},{1,3},{2,4},{3,5},{4,6},{5,7},{6,8},{7,9},{8,10},{9,11},{10,... | collective-permute-start | bytes 776 | tf_op jit(solution)/shard_map/ppermute | solution.py:113
  9.6 1.3 copy-start
  11.0 5.5 %copy-start.5 = (bf16[128,4096]{1,0:T(8,128)(2,1)S(1)}, bf16[128,4096]{1,0:T(8,128)(2,1)}, u32[]{:S(2)}) copy-start(bf16[128,4096]{1,0:T(8,128)(2,1)} %k_ref) | copy-start | bytes 3145732
  12.0 6.1 %copy-start.6 = (bf16[128,4096]{1,0:T(8,128)(2,1)S(1)}, bf16[128,4096]{1,0:T(8,128)(2,1)}, u32[]{:S(2)}) copy-start(bf16[128,4096]{1,0:T(8,128)(2,1)} %v_ref) | copy-start | bytes 3145732
  12.0 23.9 %collective-permute-start.16 = (f32[16,128,128]{2,1,0:T(8,128)}, f32[16,128,128]{2,1,0:T(8,128)}, u32[]{:S(2)}, u32[]{:S(2)}) collective-permute-start(f32[16,128,128]{2,1,0:T(8,128)} %constant_dynamic-slice_fusion.18), channel_id=1, source_target_pairs={{0,1},{1,0},{2,3},{3,2},{4,5},{5,4},{6,7},{7,6},{8,9},{9,8},{10,11... | collective-permute-start | bytes 3145736 | tf_op jit(solution)/shard_map/ppermute | solution.py:170
  20.9 6.1 %collective-permute-start.5 = (f32[4,32]{1,0:T(4,128)S(1)}, f32[4,32]{1,0:T(4,128)S(1)}, u32[]{:S(2)}, u32[]{:S(2)}) collective-permute-start(f32[4,32]{1,0:T(4,128)S(1)} %pad_maximum_fusion.3), channel_id=1, source_target_pairs={{0,4},{1,5},{2,6},{3,7},{4,8},{5,9},{6,10},{7,11},{8,12},{9,13},{1... | collective-permute-start | bytes 1544 | tf_op jit(solution)/shard_map/ppermute | solution.py:113
  22.1 18.3 %collective-permute-start.2 = (f32[16,128,128]{2,1,0:T(8,128)}, f32[16,128,128]{2,1,0:T(8,128)S(1)}, u32[]{:S(2)}, u32[]{:S(2)}) collective-permute-start(f32[16,128,128]{2,1,0:T(8,128)} %constant_dynamic-slice_fusion.19), channel_id=1, source_target_pairs={{0,1},{1,0},{2,3},{3,2},{4,5},{5,4},{6,7},{7,6},{8,9},{9,8},{10,11... | collective-permute-start | bytes 3145736 | tf_op jit(solution)/shard_map/ppermute | solution.py:170
  27.1 3.7 %collective-permute-start.6 = (f32[8,32]{1,0:T(8,128)S(1)}, f32[8,32]{1,0:T(8,128)S(1)}, u32[]{:S(2)}, u32[]{:S(2)}) collective-permute-start(f32[8,32]{1,0:T(8,128)S(1)} %pad_maximum_fusion.2), channel_id=1, source_target_pairs={{0,8},{1,9},{2,10},{3,11},{4,12},{5,13},{6,14},{7,15},{8,16},{9,17... | collective-permute-start | bytes 3080 | tf_op jit(solution)/shard_map/ppermute | solution.py:113
  30.8 4.1 %collective-permute-start.7 = (f32[16,32]{1,0:T(8,128)S(1)}, f32[16,32]{1,0:T(8,128)S(1)}, u32[]{:S(2)}, u32[]{:S(2)}) collective-permute-start(f32[16,32]{1,0:T(8,128)S(1)} %concatenate.40), channel_id=1, source_target_pairs={{0,16},{1,17},{2,18},{3,19},{4,20},{5,21},{6,22},{7,23},{8,24},{9,... | collective-permute-start | bytes 6152 | tf_op jit(solution)/shard_map/ppermute | solution.py:113
  37.8 11.6 %collective-permute-start.17 = (f32[8,128,128]{2,1,0:T(8,128)S(1)}, f32[8,128,128]{2,1,0:T(8,128)S(1)}, u32[]{:S(2)}, u32[]{:S(2)}) collective-permute-start(f32[8,128,128]{2,1,0:T(8,128)S(1)} %get-tuple-element.54), channel_id=1, source_target_pairs={{2,0},{3,1},{4,2},{5,3},{6,4},{7,5},{8,6},{9,7},{10,8},{11,9},{12,... | collective-permute-start | bytes 1572872 | tf_op jit(solution)/shard_map/ppermute | solution.py:141
  39.1 12.5 %collective-permute-start.21 = (f32[8,128,128]{2,1,0:T(8,128)S(1)}, f32[8,128,128]{2,1,0:T(8,128)S(1)}, u32[]{:S(2)}, u32[]{:S(2)}) collective-permute-start(f32[8,128,128]{2,1,0:T(8,128)S(1)} %get-tuple-element.55), channel_id=1, source_target_pairs={{8,0},{9,1},{10,2},{11,3},{12,4},{13,5},{14,6},{15,7},{16,8},{17,9... | collective-permute-start | bytes 1572872 | tf_op jit(solution)/shard_map/ppermute | solution.py:141
  40.4 1.0 copy-start.3
  41.4 13.1 %collective-permute-start.3 = (f32[8,128,128]{2,1,0:T(8,128)S(1)}, f32[8,128,128]{2,1,0:T(8,128)S(1)}, u32[]{:S(2)}, u32[]{:S(2)}) collective-permute-start(f32[8,128,128]{2,1,0:T(8,128)S(1)} %get-tuple-element.58), channel_id=1, source_target_pairs={{0,2},{1,3},{2,4},{3,5},{4,6},{5,7},{6,8},{7,9},{8,10},{9,11},{10,... | collective-permute-start | bytes 1572872 | tf_op jit(solution)/shard_map/ppermute | solution.py:141
  45.4 23.5 %collective-permute-start.11 = (f32[8,128,128]{2,1,0:T(8,128)S(1)}, f32[8,128,128]{2,1,0:T(8,128)S(1)}, u32[]{:S(2)}, u32[]{:S(2)}) collective-permute-start(f32[8,128,128]{2,1,0:T(8,128)S(1)} %get-tuple-element.59), channel_id=1, source_target_pairs={{0,8},{1,9},{2,10},{3,11},{4,12},{5,13},{6,14},{7,15},{8,16},{9,17... | collective-permute-start | bytes 1572872 | tf_op jit(solution)/shard_map/ppermute | solution.py:141
  51.8 25.4 %collective-permute-start.18 = (f32[8,128,128]{2,1,0:T(8,128)S(1)}, f32[8,128,128]{2,1,0:T(8,128)S(1)}, u32[]{:S(2)}, u32[]{:S(2)}) collective-permute-start(f32[8,128,128]{2,1,0:T(8,128)S(1)} %get-tuple-element.52), channel_id=1, source_target_pairs={{4,0},{5,1},{6,2},{7,3},{8,4},{9,5},{10,6},{11,7},{12,8},{13,9},{1... | collective-permute-start | bytes 1572872 | tf_op jit(solution)/shard_map/ppermute | solution.py:141
  53.2 42.1 %collective-permute-start.22 = (f32[8,128,128]{2,1,0:T(8,128)S(1)}, f32[8,128,128]{2,1,0:T(8,128)S(1)}, u32[]{:S(2)}, u32[]{:S(2)}) collective-permute-start(f32[8,128,128]{2,1,0:T(8,128)S(1)} %get-tuple-element.53), channel_id=1, source_target_pairs={{16,0},{17,1},{18,2},{19,3},{20,4},{21,5},{22,6},{23,7},{24,8},{25... | collective-permute-start | bytes 1572872 | tf_op jit(solution)/shard_map/ppermute | solution.py:141
  69.1 27.6 %collective-permute-start.8 = (f32[8,128,128]{2,1,0:T(8,128)S(1)}, f32[8,128,128]{2,1,0:T(8,128)S(1)}, u32[]{:S(2)}, u32[]{:S(2)}) collective-permute-start(f32[8,128,128]{2,1,0:T(8,128)S(1)} %get-tuple-element.56), channel_id=1, source_target_pairs={{0,4},{1,5},{2,6},{3,7},{4,8},{5,9},{6,10},{7,11},{8,12},{9,13},{1... | collective-permute-start | bytes 1572872 | tf_op jit(solution)/shard_map/ppermute | solution.py:141
  70.4 28.5 %collective-permute-start.12 = (f32[8,128,128]{2,1,0:T(8,128)S(1)}, f32[8,128,128]{2,1,0:T(8,128)S(1)}, u32[]{:S(2)}, u32[]{:S(2)}) collective-permute-start(f32[8,128,128]{2,1,0:T(8,128)S(1)} %get-tuple-element.57), channel_id=1, source_target_pairs={{0,16},{1,17},{2,18},{3,19},{4,20},{5,21},{6,22},{7,23},{8,24},{9,... | collective-permute-start | bytes 1572872 | tf_op jit(solution)/shard_map/ppermute | solution.py:141
  77.3 25.2 %collective-permute-start.19 = (f32[8,128,128]{2,1,0:T(8,128)S(1)}, f32[8,128,128]{2,1,0:T(8,128)S(1)}, u32[]{:S(2)}, u32[]{:S(2)}) collective-permute-start(f32[8,128,128]{2,1,0:T(8,128)S(1)} %multiply_add_fusion.8), channel_id=1, source_target_pairs={{8,0},{9,1},{10,2},{11,3},{12,4},{13,5},{14,6},{15,7},{16,8},{17,9... | collective-permute-start | bytes 1572872 | tf_op jit(solution)/shard_map/ppermute | solution.py:141
  95.4 14.9 %collective-permute-start.23 = (f32[8,128,128]{2,1,0:T(8,128)S(1)}, f32[8,128,128]{2,1,0:T(8,128)S(1)}, u32[]{:S(2)}, u32[]{:S(2)}) collective-permute-start(f32[8,128,128]{2,1,0:T(8,128)S(1)} %multiply_add_fusion.4), channel_id=1, source_target_pairs={{2,0},{3,1},{4,2},{5,3},{6,4},{7,5},{8,6},{9,7},{10,8},{11,9},{12,... | collective-permute-start | bytes 1572872 | tf_op jit(solution)/shard_map/ppermute | solution.py:141
  96.9 21.8 %collective-permute-start.9 = (f32[8,128,128]{2,1,0:T(8,128)S(1)}, f32[8,128,128]{2,1,0:T(8,128)S(1)}, u32[]{:S(2)}, u32[]{:S(2)}) collective-permute-start(f32[8,128,128]{2,1,0:T(8,128)S(1)} %multiply_add_fusion.16), channel_id=1, source_target_pairs={{0,8},{1,9},{2,10},{3,11},{4,12},{5,13},{6,14},{7,15},{8,16},{9,17... | collective-permute-start | bytes 1572872 | tf_op jit(solution)/shard_map/ppermute | solution.py:141
  99.1 28.6 %collective-permute-start.13 = (f32[8,128,128]{2,1,0:T(8,128)S(1)}, f32[8,128,128]{2,1,0:T(8,128)S(1)}, u32[]{:S(2)}, u32[]{:S(2)}) collective-permute-start(f32[8,128,128]{2,1,0:T(8,128)S(1)} %multiply_add_fusion.12), channel_id=1, source_target_pairs={{0,2},{1,3},{2,4},{3,5},{4,6},{5,7},{6,8},{7,9},{8,10},{9,11},{10,... | collective-permute-start | bytes 1572872 | tf_op jit(solution)/shard_map/ppermute | solution.py:141
  102.6 46.2 %collective-permute-start.20 = (f32[8,128,128]{2,1,0:T(8,128)S(1)}, f32[8,128,128]{2,1,0:T(8,128)S(1)}, u32[]{:S(2)}, u32[]{:S(2)}) collective-permute-start(f32[8,128,128]{2,1,0:T(8,128)S(1)} %multiply_add_fusion.7), channel_id=1, source_target_pairs={{16,0},{17,1},{18,2},{19,3},{20,4},{21,5},{22,6},{23,7},{24,8},{25... | collective-permute-start | bytes 1572872 | tf_op jit(solution)/shard_map/ppermute | solution.py:141
  110.5 38.6 %collective-permute-start.24 = (f32[8,128,128]{2,1,0:T(8,128)S(1)}, f32[8,128,128]{2,1,0:T(8,128)S(1)}, u32[]{:S(2)}, u32[]{:S(2)}) collective-permute-start(f32[8,128,128]{2,1,0:T(8,128)S(1)} %multiply_add_fusion.3), channel_id=1, source_target_pairs={{4,0},{5,1},{6,2},{7,3},{8,4},{9,5},{10,6},{11,7},{12,8},{13,9},{1... | collective-permute-start | bytes 1572872 | tf_op jit(solution)/shard_map/ppermute | solution.py:141
  118.8 34.6 %collective-permute-start.10 = (f32[8,128,128]{2,1,0:T(8,128)S(1)}, f32[8,128,128]{2,1,0:T(8,128)S(1)}, u32[]{:S(2)}, u32[]{:S(2)}) collective-permute-start(f32[8,128,128]{2,1,0:T(8,128)S(1)} %multiply_add_fusion.15), channel_id=1, source_target_pairs={{0,16},{1,17},{2,18},{3,19},{4,20},{5,21},{6,22},{7,23},{8,24},{9,... | collective-permute-start | bytes 1572872 | tf_op jit(solution)/shard_map/ppermute | solution.py:141
  127.8 25.8 %collective-permute-start.14 = (f32[8,128,128]{2,1,0:T(8,128)S(1)}, f32[8,128,128]{2,1,0:T(8,128)S(1)}, u32[]{:S(2)}, u32[]{:S(2)}) collective-permute-start(f32[8,128,128]{2,1,0:T(8,128)S(1)} %multiply_add_fusion.11), channel_id=1, source_target_pairs={{0,4},{1,5},{2,6},{3,7},{4,8},{5,9},{6,10},{7,11},{8,12},{9,13},{1... | collective-permute-start | bytes 1572872 | tf_op jit(solution)/shard_map/ppermute | solution.py:141
  148.8 1.6 copy-start.1
  151.7 5.3 %collective-permute-start.25 = (f32[16,128,128]{2,1,0:T(8,128)}, f32[16,128,128]{2,1,0:T(8,128)}, u32[]{:S(2)}, u32[]{:S(2)}) collective-permute-start(f32[16,128,128]{2,1,0:T(8,128)} %get-tuple-element.49), channel_id=1, source_target_pairs={{0,1},{1,0},{2,3},{3,2},{4,5},{5,4},{6,7},{7,6},{8,9},{9,8},{10,11... | collective-permute-start | bytes 3145736 | tf_op jit(solution)/shard_map/ppermute | solution.py:215
  153.4 1.2 copy-start.4
  156.3 4.0 %collective-permute-start.15 = (f32[16,128,128]{2,1,0:T(8,128)}, f32[16,128,128]{2,1,0:T(8,128)S(1)}, u32[]{:S(2)}, u32[]{:S(2)}) collective-permute-start(f32[16,128,128]{2,1,0:T(8,128)} %get-tuple-element.51), channel_id=1, source_target_pairs={{0,1},{1,0},{2,3},{3,2},{4,5},{5,4},{6,7},{7,6},{8,9},{9,8},{10,11... | collective-permute-start | bytes 3145736 | tf_op jit(solution)/shard_map/ppermute | solution.py:215
  157.0 3.3 %copy-start.2 = (f32[16,128,128]{2,1,0:T(8,128)S(1)}, f32[16,128,128]{2,1,0:T(8,128)}, u32[]{:S(2)}) copy-start(f32[16,128,128]{2,1,0:T(8,128)} %get-tuple-element.50) | copy-start | bytes 3145732

commit v8 on v4

--- a/solution.py
+++ b/solution.py
@@ -57,7 +57,7 @@
     block = cum_ref.shape[0]
     dk = q_ref.shape[1] // block
     later = lax.broadcasted_iota(jnp.int32, (size, size), 0) >= lax.broadcasted_iota(jnp.int32, (size, size), 1)
-    kept = pl.program_id(0) // (keep_ref.shape[0] * 2 // block) == core_ref[0]
+    kept = pl.program_id(0) // 2 == core_ref[0]
     for j in range(block):
         cols = slice(j * dk, (j + 1) * dk)
         q = q_ref[:, cols]
@@ -205,18 +205,20 @@
             )
         scans.append(jnp.concatenate(parts, 0))
     before, after = scans
-    zero = jnp.zeros_like(own_total_half)
-    own_decay = jnp.exp(own_total_half)
-    other_decay = jnp.exp(other_total_half)
-
-    def mix(a, x, b, y):
-        return a[:, None, None] * x + b[:, None, None] * y
-
-    keep_fwd = mix(jnp.where(first, one, other_decay), before, jnp.where(first, zero, one), other_state)
-    give_fwd = mix(jnp.where(first, own_decay, one), before, jnp.where(first, one, zero), mine_state)
-    keep_bwd = mix(jnp.where(first, other_decay, one), after, jnp.where(first, one, zero), other_grad)
-    give_bwd = mix(jnp.where(first, one, own_decay), after, jnp.where(first, zero, one), mine_grad)
+    total_c0 = jnp.where(first, own_total_half, other_total_half)
+    total_c1 = jnp.where(first, other_total_half, own_total_half)
+    state_c0 = jnp.where(first, mine_state, other_state)
+    grad_c1 = jnp.where(first, other_grad, mine_grad)
+    fwd_core0 = before
+    fwd_core1 = jnp.exp(total_c0)[:, None, None] * before + state_c0
+    bwd_core0 = jnp.exp(total_c1)[:, None, None] * after + grad_c1
+    bwd_core1 = after
+    keep_fwd = jnp.where(first, fwd_core0, fwd_core1)
+    keep_bwd = jnp.where(first, bwd_core0, bwd_core1)
+    give_fwd = jnp.where(first, fwd_core1, fwd_core0)
+    give_bwd = jnp.where(first, bwd_core1, bwd_core0)
     got_fwd, got_bwd = lax.ppermute((give_fwd, give_bwd), axis, partner)
+
     inputs = (queries, key_vectors, values, out_grad)
     return tuple(finish(inputs, pieces, core, (keep_fwd, got_fwd, keep_bwd, got_bwd)))
 

time: 279 us -> 175 us (0.63)
  the two profiles are of different devices: /device:TPU:15 before, /device:TPU:1 now
where the time goes in v8:
time: 175 us; the launch traced here: 174 us
  waiting for transfers between devices  79.5 us (45%)
  starting transfers between devices  54.7 us (31%)
  Pallas kernels  14.1 us (8%)
  local copies, waits for them, and re-layouts  11.2 us (6%)
  other arithmetic  9.15 us (5%)
  matrix products  4.02 us (2%)
    ppermute x16, waiting for transfers between devices, chip_scan(): received = lax.ppermute(sent, axis, pairs)  65.3 us
    ppermute x16, starting transfers between devices, chip_scan(): received = lax.ppermute(sent, axis, pairs)  43.7 us
    pallas_call x1, Pallas kernels, finish(): pl.pallas_call(head_kernel, grid_spec=pltpu.PrefetchScalarGridSpec(num_sc...  14.1 us
    ppermute x5, waiting for transfers between devices, gather_rows(): known = jnp.concatenate([known, lax.ppermute(known, axis, pairs)], 0)  12 us
    ppermute x3, starting transfers between devices, shards(): other_total, other_state, other_grad = lax.ppermute(sent, axis, partner)  8.34 us
  transfers between devices with their start and end apart: 26, of which 12 were waited for; matrix products, arithmetic and copies ran while one was open for 11% of the time, Pallas kernels for 0%

profile of v8, /device:TPU:1, one launch (start us, length us, event | category | flops | bytes accessed | tf_op | source)
XLA Modules:
  0.0 174.0 jit_solution(16321419717347638062)
XLA Ops:
  0.6 0.9 convert_reduce_fusion
  1.5 3.3 %collective-permute-start.1 = (f32[32]{0:T(128)S(1)}, f32[32]{0:T(128)S(1)}, u32[]{:S(2)}, u32[]{:S(2)}) collective-permute-start(f32[32]{0:T(128)S(1)} %convert_reduce_fusion), channel_id=1, source_target_pairs={{0,1},{1,0},{2,3},{3,2},{4,5},{5,4},{6,7},{7,6},{8,9},{9,8},{10,11... | collective-permute-start | bytes 392 | tf_op jit(solution)/shard_map/ppermute | solution.py:175
  4.9 0.8 copy.9
  6.1 0.7 collective-permute-start.4
  6.9 1.5 copy.18
  8.4 1.3 fusion
  9.6 1.3 copy-done
  11.0 1.0 constant_dynamic-slice_fusion.18
  12.0 4.5 %collective-permute-start.16 = (f32[16,128,128]{2,1,0:T(8,128)}, f32[16,128,128]{2,1,0:T(8,128)}, u32[]{:S(2)}, u32[]{:S(2)}) collective-permute-start(f32[16,128,128]{2,1,0:T(8,128)} %constant_dynamic-slice_fusion.18), channel_id=1, source_target_pairs={{0,1},{1,0},{2,3},{3,2},{4,5},{5,4},{6,7},{7,6},{8,9},{9,8},{10,11... | collective-permute-start | bytes 3145736 | tf_op jit(solution)/shard_map/ppermute | solution.py:175
  16.5 1.6 copy.17
  18.1 2.8 %fusion.2 = f32[32,128,128]{2,1,0:T(8,128)S(1)} fusion(f32[128,32,128]{0,2,1:T(8,128)} %bitcast.168, f32[128,32]{0,1:T(8,128)S(1)} %copy.11, bf16[128,4096]{1,0:T(8,128)(2,1)S(1)} %copy-done.3), kind=kOutput, calls=%fused_computation.3 | convolution fusion | flops 805830656 | bytes 5259264 | tf_op jit(solution)/shard_map/she,shf->hef/dot_general | solution.py:27
  21.0 1.0 constant_dynamic-slice_fusion.19
  22.6 4.4 %collective-permute-done.5 = f32[4,32]{1,0:T(4,128)S(1)} collective-permute-done((f32[4,32]{1,0:T(4,128)S(1)}, f32[4,32]{1,0:T(4,128)S(1)}, u32[]{:S(2)}, u32[]{:S(2)}) %collective-permute-start.5) | collective-permute-done | bytes 544 | tf_op jit(solution)/shard_map/ppermute | solution.py:118
  27.2 3.6 %collective-permute-done.6 = f32[8,32]{1,0:T(8,128)S(1)} collective-permute-done((f32[8,32]{1,0:T(8,128)S(1)}, f32[8,32]{1,0:T(8,128)S(1)}, u32[]{:S(2)}, u32[]{:S(2)}) %collective-permute-start.6) | collective-permute-done | bytes 1056 | tf_op jit(solution)/shard_map/ppermute | solution.py:118
  30.9 4.0 %collective-permute-done.7 = f32[16,32]{1,0:T(8,128)S(1)} collective-permute-done((f32[16,32]{1,0:T(8,128)S(1)}, f32[16,32]{1,0:T(8,128)S(1)}, u32[]{:S(2)}, u32[]{:S(2)}) %collective-permute-start.7) | collective-permute-done | bytes 2080 | tf_op jit(solution)/shard_map/ppermute | solution.py:118
  34.9 0.6 gather_fusion
  36.0 1.7 multiply_add_fusion
  37.8 1.3 collective-permute-start.17
  39.1 1.3 collective-permute-start.21
  40.7 4.0 %collective-permute-start.3 = (f32[8,128,128]{2,1,0:T(8,128)S(1)}, f32[8,128,128]{2,1,0:T(8,128)S(1)}, u32[]{:S(2)}, u32[]{:S(2)}) collective-permute-start(f32[8,128,128]{2,1,0:T(8,128)S(1)} %get-tuple-element.58), channel_id=1, source_target_pairs={{0,2},{1,3},{2,4},{3,5},{4,6},{5,7},{6,8},{7,9},{8,10},{9,11},{10,... | collective-permute-start | bytes 1572872 | tf_op jit(solution)/shard_map/ppermute | solution.py:146
  44.7 4.0 %collective-permute-start.11 = (f32[8,128,128]{2,1,0:T(8,128)S(1)}, f32[8,128,128]{2,1,0:T(8,128)S(1)}, u32[]{:S(2)}, u32[]{:S(2)}) collective-permute-start(f32[8,128,128]{2,1,0:T(8,128)S(1)} %get-tuple-element.59), channel_id=1, source_target_pairs={{0,8},{1,9},{2,10},{3,11},{4,12},{5,13},{6,14},{7,15},{8,16},{9,17... | collective-permute-start | bytes 1572872 | tf_op jit(solution)/shard_map/ppermute | solution.py:146
  49.1 2.5 %collective-permute-done.21 = f32[8,128,128]{2,1,0:T(8,128)S(1)} collective-permute-done((f32[8,128,128]{2,1,0:T(8,128)S(1)}, f32[8,128,128]{2,1,0:T(8,128)S(1)}, u32[]{:S(2)}, u32[]{:S(2)}) %collective-permute-start.21) | collective-permute-done | bytes 524320 | tf_op jit(solution)/shard_map/ppermute | solution.py:146
  51.8 1.3 collective-permute-start.18
  53.2 1.3 collective-permute-start.22
  54.5 13.7 %collective-permute-done.11 = f32[8,128,128]{2,1,0:T(8,128)S(1)} collective-permute-done((f32[8,128,128]{2,1,0:T(8,128)S(1)}, f32[8,128,128]{2,1,0:T(8,128)S(1)}, u32[]{:S(2)}, u32[]{:S(2)}) %collective-permute-start.11) | collective-permute-done | bytes 524320 | tf_op jit(solution)/shard_map/ppermute | solution.py:146
  68.4 1.3 collective-permute-start.8
  69.8 6.8 %collective-permute-start.12 = (f32[8,128,128]{2,1,0:T(8,128)S(1)}, f32[8,128,128]{2,1,0:T(8,128)S(1)}, u32[]{:S(2)}, u32[]{:S(2)}) collective-permute-start(f32[8,128,128]{2,1,0:T(8,128)S(1)} %get-tuple-element.57), channel_id=1, source_target_pairs={{0,16},{1,17},{2,18},{3,19},{4,20},{5,21},{6,22},{7,23},{8,24},{9,... | collective-permute-start | bytes 1572872 | tf_op jit(solution)/shard_map/ppermute | solution.py:146
  76.7 1.3 collective-permute-start.19
  78.0 16.7 %collective-permute-done.22 = f32[8,128,128]{2,1,0:T(8,128)S(1)} collective-permute-done((f32[8,128,128]{2,1,0:T(8,128)S(1)}, f32[8,128,128]{2,1,0:T(8,128)S(1)}, u32[]{:S(2)}, u32[]{:S(2)}) %collective-permute-start.22) | collective-permute-done | bytes 524320 | tf_op jit(solution)/shard_map/ppermute | solution.py:146
  94.8 1.3 collective-permute-start.23
  96.2 1.3 collective-permute-start.9
  97.6 0.7 collective-permute-done.12
  98.4 4.1 %collective-permute-start.13 = (f32[8,128,128]{2,1,0:T(8,128)S(1)}, f32[8,128,128]{2,1,0:T(8,128)S(1)}, u32[]{:S(2)}, u32[]{:S(2)}) collective-permute-start(f32[8,128,128]{2,1,0:T(8,128)S(1)} %multiply_add_fusion.12), channel_id=1, source_target_pairs={{0,2},{1,3},{2,4},{3,5},{4,6},{5,7},{6,8},{7,9},{8,10},{9,11},{10,... | collective-permute-start | bytes 1572872 | tf_op jit(solution)/shard_map/ppermute | solution.py:146
  102.7 1.3 collective-permute-start.20
  104.0 5.7 %collective-permute-done.23 = f32[8,128,128]{2,1,0:T(8,128)S(1)} collective-permute-done((f32[8,128,128]{2,1,0:T(8,128)S(1)}, f32[8,128,128]{2,1,0:T(8,128)S(1)}, u32[]{:S(2)}, u32[]{:S(2)}) %collective-permute-start.23) | collective-permute-done | bytes 524320 | tf_op jit(solution)/shard_map/ppermute | solution.py:146
  109.8 1.5 collective-permute-start.24
  111.3 6.0 %collective-permute-done.9 = f32[8,128,128]{2,1,0:T(8,128)S(1)} collective-permute-done((f32[8,128,128]{2,1,0:T(8,128)S(1)}, f32[8,128,128]{2,1,0:T(8,128)S(1)}, u32[]{:S(2)}, u32[]{:S(2)}) %collective-permute-start.9) | collective-permute-done | bytes 524320 | tf_op jit(solution)/shard_map/ppermute | solution.py:146
  117.4 10.3 %collective-permute-start.10 = (f32[8,128,128]{2,1,0:T(8,128)S(1)}, f32[8,128,128]{2,1,0:T(8,128)S(1)}, u32[]{:S(2)}, u32[]{:S(2)}) collective-permute-start(f32[8,128,128]{2,1,0:T(8,128)S(1)} %multiply_add_fusion.15), channel_id=1, source_target_pairs={{0,16},{1,17},{2,18},{3,19},{4,20},{5,21},{6,22},{7,23},{8,24},{9,... | collective-permute-start | bytes 1572872 | tf_op jit(solution)/shard_map/ppermute | solution.py:146
  127.8 1.3 collective-permute-start.14
  129.2 19.6 %collective-permute-done.20 = f32[8,128,128]{2,1,0:T(8,128)S(1)} collective-permute-done((f32[8,128,128]{2,1,0:T(8,128)S(1)}, f32[8,128,128]{2,1,0:T(8,128)S(1)}, u32[]{:S(2)}, u32[]{:S(2)}) %collective-permute-start.20) | collective-permute-done | bytes 524320 | tf_op jit(solution)/shard_map/ppermute | solution.py:146
  149.3 1.1 copy-done.1
  150.4 1.7 fusion.12
  152.1 1.7 collective-permute-start.25
  154.3 1.7 fusion.10
  155.9 0.7 copy.10
  156.6 2.2 %collective-permute-done.15.got_ref = f32[16,128,128]{2,1,0:T(8,128)S(1)} collective-permute-done((f32[16,128,128]{2,1,0:T(8,128)}, f32[16,128,128]{2,1,0:T(8,128)S(1)}, u32[]{:S(2)}, u32[]{:S(2)}) %collective-permute-start.15) | collective-permute-done | bytes 1048608 | tf_op jit(solution)/shard_map/ppermute | solution.py:220
  158.8 1.0 copy-done.5
  159.8 14.1 %shard_map.84 = (bf16[128,4096]{1,0:T(8,128)(2,1)}, bf16[128,4096]{1,0:T(8,128)(2,1)}, bf16[128,4096]{1,0:T(8,128)(2,1)}, bf16[128,4096]{1,0:T(8,128)(2,1)}) custom-call(s32[1]{0:T(128)} %bitcast.core_ref, bf16[128,4096]{1,0:T(8,128)(2,1)} %q_ref, bf16[128,4096]{1,0:T(8,128)(2,1)} %k_ref, bf16[128,4096]{1,0:T(8,128)(2,1)} %v_ref, bf16[128,4096]{1,0:T(8,128)(2,1)} %g_ref, ...), custom_call_target="tpu_custom_call" | custom-call | tf_op jit(solution)/shard_map/pallas_call | solution.py:97
  (78 shorter events, 4.9 us)
Async XLA Ops:
  0.6 7.7 %copy-start.4 = (bf16[128,4096]{1,0:T(8,128)(2,1)S(1)}, bf16[128,4096]{1,0:T(8,128)(2,1)}, u32[]{:S(2)}) copy-start(bf16[128,4096]{1,0:T(8,128)(2,1)} %g_ref) | copy-start | bytes 3145732
  1.5 25.6 %collective-permute-start.1 = (f32[32]{0:T(128)S(1)}, f32[32]{0:T(128)S(1)}, u32[]{:S(2)}, u32[]{:S(2)}) collective-permute-start(f32[32]{0:T(128)S(1)} %convert_reduce_fusion), channel_id=1, source_target_pairs={{0,1},{1,0},{2,3},{3,2},{4,5},{5,4},{6,7},{7,6},{8,9},{9,8},{10,11... | collective-permute-start | bytes 392 | tf_op jit(solution)/shard_map/ppermute | solution.py:175
  4.9 1.2 collective-permute-start
  6.1 14.8 %collective-permute-start.4 = (f32[2,32]{1,0:T(2,128)S(1)}, f32[2,32]{1,0:T(2,128)S(1)}, u32[]{:S(2)}, u32[]{:S(2)}) collective-permute-start(f32[2,32]{1,0:T(2,128)S(1)} %pad_maximum_fusion.4), channel_id=1, source_target_pairs={{0,2},{1,3},{2,4},{3,5},{4,6},{5,7},{6,8},{7,9},{8,10},{9,11},{10,... | collective-permute-start | bytes 776 | tf_op jit(solution)/shard_map/ppermute | solution.py:118
  9.6 1.4 copy-start
  11.0 5.5 %copy-start.2 = (bf16[128,4096]{1,0:T(8,128)(2,1)S(1)}, bf16[128,4096]{1,0:T(8,128)(2,1)}, u32[]{:S(2)}) copy-start(bf16[128,4096]{1,0:T(8,128)(2,1)} %k_ref) | copy-start | bytes 3145732
  12.0 6.1 %copy-start.3 = (bf16[128,4096]{1,0:T(8,128)(2,1)S(1)}, bf16[128,4096]{1,0:T(8,128)(2,1)}, u32[]{:S(2)}) copy-start(bf16[128,4096]{1,0:T(8,128)(2,1)} %v_ref) | copy-start | bytes 3145732
  12.0 23.9 %collective-permute-start.16 = (f32[16,128,128]{2,1,0:T(8,128)}, f32[16,128,128]{2,1,0:T(8,128)}, u32[]{:S(2)}, u32[]{:S(2)}) collective-permute-start(f32[16,128,128]{2,1,0:T(8,128)} %constant_dynamic-slice_fusion.18), channel_id=1, source_target_pairs={{0,1},{1,0},{2,3},{3,2},{4,5},{5,4},{6,7},{7,6},{8,9},{9,8},{10,11... | collective-permute-start | bytes 3145736 | tf_op jit(solution)/shard_map/ppermute | solution.py:175
  20.9 6.1 %collective-permute-start.5 = (f32[4,32]{1,0:T(4,128)S(1)}, f32[4,32]{1,0:T(4,128)S(1)}, u32[]{:S(2)}, u32[]{:S(2)}) collective-permute-start(f32[4,32]{1,0:T(4,128)S(1)} %pad_maximum_fusion.3), channel_id=1, source_target_pairs={{0,4},{1,5},{2,6},{3,7},{4,8},{5,9},{6,10},{7,11},{8,12},{9,13},{1... | collective-permute-start | bytes 1544 | tf_op jit(solution)/shard_map/ppermute | solution.py:118
  22.1 18.3 %collective-permute-start.2 = (f32[16,128,128]{2,1,0:T(8,128)}, f32[16,128,128]{2,1,0:T(8,128)S(1)}, u32[]{:S(2)}, u32[]{:S(2)}) collective-permute-start(f32[16,128,128]{2,1,0:T(8,128)} %constant_dynamic-slice_fusion.19), channel_id=1, source_target_pairs={{0,1},{1,0},{2,3},{3,2},{4,5},{5,4},{6,7},{7,6},{8,9},{9,8},{10,11... | collective-permute-start | bytes 3145736 | tf_op jit(solution)/shard_map/ppermute | solution.py:175
  27.1 3.7 %collective-permute-start.6 = (f32[8,32]{1,0:T(8,128)S(1)}, f32[8,32]{1,0:T(8,128)S(1)}, u32[]{:S(2)}, u32[]{:S(2)}) collective-permute-start(f32[8,32]{1,0:T(8,128)S(1)} %pad_maximum_fusion.2), channel_id=1, source_target_pairs={{0,8},{1,9},{2,10},{3,11},{4,12},{5,13},{6,14},{7,15},{8,16},{9,17... | collective-permute-start | bytes 3080 | tf_op jit(solution)/shard_map/ppermute | solution.py:118
  30.8 4.1 %collective-permute-start.7 = (f32[16,32]{1,0:T(8,128)S(1)}, f32[16,32]{1,0:T(8,128)S(1)}, u32[]{:S(2)}, u32[]{:S(2)}) collective-permute-start(f32[16,32]{1,0:T(8,128)S(1)} %concatenate.28), channel_id=1, source_target_pairs={{0,16},{1,17},{2,18},{3,19},{4,20},{5,21},{6,22},{7,23},{8,24},{9,... | collective-permute-start | bytes 6152 | tf_op jit(solution)/shard_map/ppermute | solution.py:118
  37.8 11.3 %collective-permute-start.17 = (f32[8,128,128]{2,1,0:T(8,128)S(1)}, f32[8,128,128]{2,1,0:T(8,128)S(1)}, u32[]{:S(2)}, u32[]{:S(2)}) collective-permute-start(f32[8,128,128]{2,1,0:T(8,128)S(1)} %get-tuple-element.54), channel_id=1, source_target_pairs={{2,0},{3,1},{4,2},{5,3},{6,4},{7,5},{8,6},{9,7},{10,8},{11,9},{12,... | collective-permute-start | bytes 1572872 | tf_op jit(solution)/shard_map/ppermute | solution.py:146
  39.1 12.5 %collective-permute-start.21 = (f32[8,128,128]{2,1,0:T(8,128)S(1)}, f32[8,128,128]{2,1,0:T(8,128)S(1)}, u32[]{:S(2)}, u32[]{:S(2)}) collective-permute-start(f32[8,128,128]{2,1,0:T(8,128)S(1)} %get-tuple-element.55), channel_id=1, source_target_pairs={{8,0},{9,1},{10,2},{11,3},{12,4},{13,5},{14,6},{15,7},{16,8},{17,9... | collective-permute-start | bytes 1572872 | tf_op jit(solution)/shard_map/ppermute | solution.py:146
  40.7 13.8 %collective-permute-start.3 = (f32[8,128,128]{2,1,0:T(8,128)S(1)}, f32[8,128,128]{2,1,0:T(8,128)S(1)}, u32[]{:S(2)}, u32[]{:S(2)}) collective-permute-start(f32[8,128,128]{2,1,0:T(8,128)S(1)} %get-tuple-element.58), channel_id=1, source_target_pairs={{0,2},{1,3},{2,4},{3,5},{4,6},{5,7},{6,8},{7,9},{8,10},{9,11},{10,... | collective-permute-start | bytes 1572872 | tf_op jit(solution)/shard_map/ppermute | solution.py:146
  44.7 23.5 %collective-permute-start.11 = (f32[8,128,128]{2,1,0:T(8,128)S(1)}, f32[8,128,128]{2,1,0:T(8,128)S(1)}, u32[]{:S(2)}, u32[]{:S(2)}) collective-permute-start(f32[8,128,128]{2,1,0:T(8,128)S(1)} %get-tuple-element.59), channel_id=1, source_target_pairs={{0,8},{1,9},{2,10},{3,11},{4,12},{5,13},{6,14},{7,15},{8,16},{9,17... | collective-permute-start | bytes 1572872 | tf_op jit(solution)/shard_map/ppermute | solution.py:146
  51.8 24.8 %collective-permute-start.18 = (f32[8,128,128]{2,1,0:T(8,128)S(1)}, f32[8,128,128]{2,1,0:T(8,128)S(1)}, u32[]{:S(2)}, u32[]{:S(2)}) collective-permute-start(f32[8,128,128]{2,1,0:T(8,128)S(1)} %get-tuple-element.52), channel_id=1, source_target_pairs={{4,0},{5,1},{6,2},{7,3},{8,4},{9,5},{10,6},{11,7},{12,8},{13,9},{1... | collective-permute-start | bytes 1572872 | tf_op jit(solution)/shard_map/ppermute | solution.py:146
  53.2 41.4 %collective-permute-start.22 = (f32[8,128,128]{2,1,0:T(8,128)S(1)}, f32[8,128,128]{2,1,0:T(8,128)S(1)}, u32[]{:S(2)}, u32[]{:S(2)}) collective-permute-start(f32[8,128,128]{2,1,0:T(8,128)S(1)} %get-tuple-element.53), channel_id=1, source_target_pairs={{16,0},{17,1},{18,2},{19,3},{20,4},{21,5},{22,6},{23,7},{24,8},{25... | collective-permute-start | bytes 1572872 | tf_op jit(solution)/shard_map/ppermute | solution.py:146
  68.4 27.6 %collective-permute-start.8 = (f32[8,128,128]{2,1,0:T(8,128)S(1)}, f32[8,128,128]{2,1,0:T(8,128)S(1)}, u32[]{:S(2)}, u32[]{:S(2)}) collective-permute-start(f32[8,128,128]{2,1,0:T(8,128)S(1)} %get-tuple-element.56), channel_id=1, source_target_pairs={{0,4},{1,5},{2,6},{3,7},{4,8},{5,9},{6,10},{7,11},{8,12},{9,13},{1... | collective-permute-start | bytes 1572872 | tf_op jit(solution)/shard_map/ppermute | solution.py:146
  69.8 28.5 %collective-permute-start.12 = (f32[8,128,128]{2,1,0:T(8,128)S(1)}, f32[8,128,128]{2,1,0:T(8,128)S(1)}, u32[]{:S(2)}, u32[]{:S(2)}) collective-permute-start(f32[8,128,128]{2,1,0:T(8,128)S(1)} %get-tuple-element.57), channel_id=1, source_target_pairs={{0,16},{1,17},{2,18},{3,19},{4,20},{5,21},{6,22},{7,23},{8,24},{9,... | collective-permute-start | bytes 1572872 | tf_op jit(solution)/shard_map/ppermute | solution.py:146
  76.7 25.9 %collective-permute-start.19 = (f32[8,128,128]{2,1,0:T(8,128)S(1)}, f32[8,128,128]{2,1,0:T(8,128)S(1)}, u32[]{:S(2)}, u32[]{:S(2)}) collective-permute-start(f32[8,128,128]{2,1,0:T(8,128)S(1)} %multiply_add_fusion.8), channel_id=1, source_target_pairs={{8,0},{9,1},{10,2},{11,3},{12,4},{13,5},{14,6},{15,7},{16,8},{17,9... | collective-permute-start | bytes 1572872 | tf_op jit(solution)/shard_map/ppermute | solution.py:146
  94.8 14.9 %collective-permute-start.23 = (f32[8,128,128]{2,1,0:T(8,128)S(1)}, f32[8,128,128]{2,1,0:T(8,128)S(1)}, u32[]{:S(2)}, u32[]{:S(2)}) collective-permute-start(f32[8,128,128]{2,1,0:T(8,128)S(1)} %multiply_add_fusion.4), channel_id=1, source_target_pairs={{2,0},{3,1},{4,2},{5,3},{6,4},{7,5},{8,6},{9,7},{10,8},{11,9},{12,... | collective-permute-start | bytes 1572872 | tf_op jit(solution)/shard_map/ppermute | solution.py:146
  96.2 21.0 %collective-permute-start.9 = (f32[8,128,128]{2,1,0:T(8,128)S(1)}, f32[8,128,128]{2,1,0:T(8,128)S(1)}, u32[]{:S(2)}, u32[]{:S(2)}) collective-permute-start(f32[8,128,128]{2,1,0:T(8,128)S(1)} %multiply_add_fusion.16), channel_id=1, source_target_pairs={{0,8},{1,9},{2,10},{3,11},{4,12},{5,13},{6,14},{7,15},{8,16},{9,17... | collective-permute-start | bytes 1572872 | tf_op jit(solution)/shard_map/ppermute | solution.py:146
  98.4 29.3 %collective-permute-start.13 = (f32[8,128,128]{2,1,0:T(8,128)S(1)}, f32[8,128,128]{2,1,0:T(8,128)S(1)}, u32[]{:S(2)}, u32[]{:S(2)}) collective-permute-start(f32[8,128,128]{2,1,0:T(8,128)S(1)} %multiply_add_fusion.12), channel_id=1, source_target_pairs={{0,2},{1,3},{2,4},{3,5},{4,6},{5,7},{6,8},{7,9},{8,10},{9,11},{10,... | collective-permute-start | bytes 1572872 | tf_op jit(solution)/shard_map/ppermute | solution.py:146
  102.7 46.1 %collective-permute-start.20 = (f32[8,128,128]{2,1,0:T(8,128)S(1)}, f32[8,128,128]{2,1,0:T(8,128)S(1)}, u32[]{:S(2)}, u32[]{:S(2)}) collective-permute-start(f32[8,128,128]{2,1,0:T(8,128)S(1)} %multiply_add_fusion.7), channel_id=1, source_target_pairs={{16,0},{17,1},{18,2},{19,3},{20,4},{21,5},{22,6},{23,7},{24,8},{25... | collective-permute-start | bytes 1572872 | tf_op jit(solution)/shard_map/ppermute | solution.py:146
  109.8 39.3 %collective-permute-start.24 = (f32[8,128,128]{2,1,0:T(8,128)S(1)}, f32[8,128,128]{2,1,0:T(8,128)S(1)}, u32[]{:S(2)}, u32[]{:S(2)}) collective-permute-start(f32[8,128,128]{2,1,0:T(8,128)S(1)} %multiply_add_fusion.3), channel_id=1, source_target_pairs={{4,0},{5,1},{6,2},{7,3},{8,4},{9,5},{10,6},{11,7},{12,8},{13,9},{1... | collective-permute-start | bytes 1572872 | tf_op jit(solution)/shard_map/ppermute | solution.py:146
  117.4 36.4 %collective-permute-start.10 = (f32[8,128,128]{2,1,0:T(8,128)S(1)}, f32[8,128,128]{2,1,0:T(8,128)S(1)}, u32[]{:S(2)}, u32[]{:S(2)}) collective-permute-start(f32[8,128,128]{2,1,0:T(8,128)S(1)} %multiply_add_fusion.15), channel_id=1, source_target_pairs={{0,16},{1,17},{2,18},{3,19},{4,20},{5,21},{6,22},{7,23},{8,24},{9,... | collective-permute-start | bytes 1572872 | tf_op jit(solution)/shard_map/ppermute | solution.py:146
  127.8 26.2 %collective-permute-start.14 = (f32[8,128,128]{2,1,0:T(8,128)S(1)}, f32[8,128,128]{2,1,0:T(8,128)S(1)}, u32[]{:S(2)}, u32[]{:S(2)}) collective-permute-start(f32[8,128,128]{2,1,0:T(8,128)S(1)} %multiply_add_fusion.11), channel_id=1, source_target_pairs={{0,4},{1,5},{2,6},{3,7},{4,8},{5,9},{6,10},{7,11},{8,12},{9,13},{1... | collective-permute-start | bytes 1572872 | tf_op jit(solution)/shard_map/ppermute | solution.py:146
  148.8 1.6 copy-start.1
  152.1 4.5 %collective-permute-start.25 = (f32[16,128,128]{2,1,0:T(8,128)}, f32[16,128,128]{2,1,0:T(8,128)}, u32[]{:S(2)}, u32[]{:S(2)}) collective-permute-start(f32[16,128,128]{2,1,0:T(8,128)} %get-tuple-element.48), channel_id=1, source_target_pairs={{0,1},{1,0},{2,3},{3,2},{4,5},{5,4},{6,7},{7,6},{8,9},{9,8},{10,11... | collective-permute-start | bytes 3145736 | tf_op jit(solution)/shard_map/ppermute | solution.py:220
  155.9 2.9 %collective-permute-start.15 = (f32[16,128,128]{2,1,0:T(8,128)}, f32[16,128,128]{2,1,0:T(8,128)S(1)}, u32[]{:S(2)}, u32[]{:S(2)}) collective-permute-start(f32[16,128,128]{2,1,0:T(8,128)} %get-tuple-element.50), channel_id=1, source_target_pairs={{0,1},{1,0},{2,3},{3,2},{4,5},{5,4},{6,7},{7,6},{8,9},{9,8},{10,11... | collective-permute-start | bytes 3145736 | tf_op jit(solution)/shard_map/ppermute | solution.py:220
  158.8 1.0 copy-start.5

commit v9 on v8

--- a/solution.py
+++ b/solution.py
@@ -57,7 +57,7 @@
     block = cum_ref.shape[0]
     dk = q_ref.shape[1] // block
     later = lax.broadcasted_iota(jnp.int32, (size, size), 0) >= lax.broadcasted_iota(jnp.int32, (size, size), 1)
-    kept = pl.program_id(0) // 2 == core_ref[0]
+    kept = pl.program_id(0) // (keep_ref.shape[0] // block) == core_ref[0]
     for j in range(block):
         cols = slice(j * dk, (j + 1) * dk)
         q = q_ref[:, cols]
@@ -89,7 +89,7 @@
     half = halves[0].shape[0]
     heads = 2 * half
     dk = width // heads
-    block = 8
+    block = 16
     steps = half // block
     tile = pl.BlockSpec((length, block * dk), lambda h, c: (0, h))
     states = pl.BlockSpec((block, dk, dk), lambda h, c: (h % steps, 0, 0))

time: 175 us -> 176 us (level)
  no operation moved by 1% of the time
where the time goes in v9:
time: 176 us; the launch traced here: 175 us
  waiting for transfers between devices  79.5 us (45%)
  starting transfers between devices  54.7 us (31%)
  Pallas kernels  15.3 us (9%)
  local copies, waits for them, and re-layouts  11.2 us (6%)
  other arithmetic  9.15 us (5%)
  matrix products  4.02 us (2%)
    ppermute x16, waiting for transfers between devices, chip_scan(): received = lax.ppermute(sent, axis, pairs)  65.3 us
    ppermute x16, starting transfers between devices, chip_scan(): received = lax.ppermute(sent, axis, pairs)  43.7 us
    pallas_call x1, Pallas kernels, finish(): pl.pallas_call(head_kernel, grid_spec=pltpu.PrefetchScalarGridSpec(num_sc...  15.3 us
    ppermute x5, waiting for transfers between devices, gather_rows(): known = jnp.concatenate([known, lax.ppermute(known, axis, pairs)], 0)  12 us
    ppermute x3, starting transfers between devices, shards(): other_total, other_state, other_grad = lax.ppermute(sent, axis, partner)  8.34 us
  transfers between devices with their start and end apart: 26, of which 12 were waited for; matrix products, arithmetic and copies ran while one was open for 11% of the time, Pallas kernels for 0%

profile of v9, /device:TPU:1, one launch (start us, length us, event | category | flops | bytes accessed | tf_op | source)
XLA Modules:
  0.0 175.1 jit_solution(1316525219684671276)
XLA Ops:
  0.6 0.9 convert_reduce_fusion
  1.5 3.3 %collective-permute-start.1 = (f32[32]{0:T(128)S(1)}, f32[32]{0:T(128)S(1)}, u32[]{:S(2)}, u32[]{:S(2)}) collective-permute-start(f32[32]{0:T(128)S(1)} %convert_reduce_fusion), channel_id=1, source_target_pairs={{0,1},{1,0},{2,3},{3,2},{4,5},{5,4},{6,7},{7,6},{8,9},{9,8},{10,11... | collective-permute-start | bytes 392 | tf_op jit(solution)/shard_map/ppermute | solution.py:175
  4.9 0.8 copy.9
  6.1 0.7 collective-permute-start.4
  6.9 1.5 copy.18
  8.4 1.3 fusion
  9.6 1.3 copy-done
  11.0 1.0 constant_dynamic-slice_fusion.18
  12.0 4.5 %collective-permute-start.16 = (f32[16,128,128]{2,1,0:T(8,128)}, f32[16,128,128]{2,1,0:T(8,128)}, u32[]{:S(2)}, u32[]{:S(2)}) collective-permute-start(f32[16,128,128]{2,1,0:T(8,128)} %constant_dynamic-slice_fusion.18), channel_id=1, source_target_pairs={{0,1},{1,0},{2,3},{3,2},{4,5},{5,4},{6,7},{7,6},{8,9},{9,8},{10,11... | collective-permute-start | bytes 3145736 | tf_op jit(solution)/shard_map/ppermute | solution.py:175
  16.5 1.6 copy.17
  18.1 2.8 %fusion.2 = f32[32,128,128]{2,1,0:T(8,128)S(1)} fusion(f32[128,32,128]{0,2,1:T(8,128)} %bitcast.168, f32[128,32]{0,1:T(8,128)S(1)} %copy.11, bf16[128,4096]{1,0:T(8,128)(2,1)S(1)} %copy-done.3), kind=kOutput, calls=%fused_computation.3 | convolution fusion | flops 805830656 | bytes 5259264 | tf_op jit(solution)/shard_map/she,shf->hef/dot_general | solution.py:27
  21.0 1.0 constant_dynamic-slice_fusion.19
  22.6 4.4 %collective-permute-done.5 = f32[4,32]{1,0:T(4,128)S(1)} collective-permute-done((f32[4,32]{1,0:T(4,128)S(1)}, f32[4,32]{1,0:T(4,128)S(1)}, u32[]{:S(2)}, u32[]{:S(2)}) %collective-permute-start.5) | collective-permute-done | bytes 544 | tf_op jit(solution)/shard_map/ppermute | solution.py:118
  27.2 3.6 %collective-permute-done.6 = f32[8,32]{1,0:T(8,128)S(1)} collective-permute-done((f32[8,32]{1,0:T(8,128)S(1)}, f32[8,32]{1,0:T(8,128)S(1)}, u32[]{:S(2)}, u32[]{:S(2)}) %collective-permute-start.6) | collective-permute-done | bytes 1056 | tf_op jit(solution)/shard_map/ppermute | solution.py:118
  30.9 4.0 %collective-permute-done.7 = f32[16,32]{1,0:T(8,128)S(1)} collective-permute-done((f32[16,32]{1,0:T(8,128)S(1)}, f32[16,32]{1,0:T(8,128)S(1)}, u32[]{:S(2)}, u32[]{:S(2)}) %collective-permute-start.7) | collective-permute-done | bytes 2080 | tf_op jit(solution)/shard_map/ppermute | solution.py:118
  34.9 0.6 gather_fusion
  36.0 1.7 multiply_add_fusion
  37.8 1.3 collective-permute-start.17
  39.1 1.3 collective-permute-start.21
  40.7 4.0 %collective-permute-start.3 = (f32[8,128,128]{2,1,0:T(8,128)S(1)}, f32[8,128,128]{2,1,0:T(8,128)S(1)}, u32[]{:S(2)}, u32[]{:S(2)}) collective-permute-start(f32[8,128,128]{2,1,0:T(8,128)S(1)} %get-tuple-element.58), channel_id=1, source_target_pairs={{0,2},{1,3},{2,4},{3,5},{4,6},{5,7},{6,8},{7,9},{8,10},{9,11},{10,... | collective-permute-start | bytes 1572872 | tf_op jit(solution)/shard_map/ppermute | solution.py:146
  44.7 4.0 %collective-permute-start.11 = (f32[8,128,128]{2,1,0:T(8,128)S(1)}, f32[8,128,128]{2,1,0:T(8,128)S(1)}, u32[]{:S(2)}, u32[]{:S(2)}) collective-permute-start(f32[8,128,128]{2,1,0:T(8,128)S(1)} %get-tuple-element.59), channel_id=1, source_target_pairs={{0,8},{1,9},{2,10},{3,11},{4,12},{5,13},{6,14},{7,15},{8,16},{9,17... | collective-permute-start | bytes 1572872 | tf_op jit(solution)/shard_map/ppermute | solution.py:146
  49.1 2.5 %collective-permute-done.21 = f32[8,128,128]{2,1,0:T(8,128)S(1)} collective-permute-done((f32[8,128,128]{2,1,0:T(8,128)S(1)}, f32[8,128,128]{2,1,0:T(8,128)S(1)}, u32[]{:S(2)}, u32[]{:S(2)}) %collective-permute-start.21) | collective-permute-done | bytes 524320 | tf_op jit(solution)/shard_map/ppermute | solution.py:146
  51.8 1.3 collective-permute-start.18
  53.2 1.3 collective-permute-start.22
  54.5 13.7 %collective-permute-done.11 = f32[8,128,128]{2,1,0:T(8,128)S(1)} collective-permute-done((f32[8,128,128]{2,1,0:T(8,128)S(1)}, f32[8,128,128]{2,1,0:T(8,128)S(1)}, u32[]{:S(2)}, u32[]{:S(2)}) %collective-permute-start.11) | collective-permute-done | bytes 524320 | tf_op jit(solution)/shard_map/ppermute | solution.py:146
  68.4 1.3 collective-permute-start.8
  69.8 6.8 %collective-permute-start.12 = (f32[8,128,128]{2,1,0:T(8,128)S(1)}, f32[8,128,128]{2,1,0:T(8,128)S(1)}, u32[]{:S(2)}, u32[]{:S(2)}) collective-permute-start(f32[8,128,128]{2,1,0:T(8,128)S(1)} %get-tuple-element.57), channel_id=1, source_target_pairs={{0,16},{1,17},{2,18},{3,19},{4,20},{5,21},{6,22},{7,23},{8,24},{9,... | collective-permute-start | bytes 1572872 | tf_op jit(solution)/shard_map/ppermute | solution.py:146
  76.7 1.3 collective-permute-start.19
  78.0 16.7 %collective-permute-done.22 = f32[8,128,128]{2,1,0:T(8,128)S(1)} collective-permute-done((f32[8,128,128]{2,1,0:T(8,128)S(1)}, f32[8,128,128]{2,1,0:T(8,128)S(1)}, u32[]{:S(2)}, u32[]{:S(2)}) %collective-permute-start.22) | collective-permute-done | bytes 524320 | tf_op jit(solution)/shard_map/ppermute | solution.py:146
  94.8 1.3 collective-permute-start.23
  96.2 1.3 collective-permute-start.9
  97.6 0.7 collective-permute-done.12
  98.4 4.1 %collective-permute-start.13 = (f32[8,128,128]{2,1,0:T(8,128)S(1)}, f32[8,128,128]{2,1,0:T(8,128)S(1)}, u32[]{:S(2)}, u32[]{:S(2)}) collective-permute-start(f32[8,128,128]{2,1,0:T(8,128)S(1)} %multiply_add_fusion.12), channel_id=1, source_target_pairs={{0,2},{1,3},{2,4},{3,5},{4,6},{5,7},{6,8},{7,9},{8,10},{9,11},{10,... | collective-permute-start | bytes 1572872 | tf_op jit(solution)/shard_map/ppermute | solution.py:146
  102.7 1.3 collective-permute-start.20
  104.0 5.7 %collective-permute-done.23 = f32[8,128,128]{2,1,0:T(8,128)S(1)} collective-permute-done((f32[8,128,128]{2,1,0:T(8,128)S(1)}, f32[8,128,128]{2,1,0:T(8,128)S(1)}, u32[]{:S(2)}, u32[]{:S(2)}) %collective-permute-start.23) | collective-permute-done | bytes 524320 | tf_op jit(solution)/shard_map/ppermute | solution.py:146
  109.8 1.5 collective-permute-start.24
  111.3 6.0 %collective-permute-done.9 = f32[8,128,128]{2,1,0:T(8,128)S(1)} collective-permute-done((f32[8,128,128]{2,1,0:T(8,128)S(1)}, f32[8,128,128]{2,1,0:T(8,128)S(1)}, u32[]{:S(2)}, u32[]{:S(2)}) %collective-permute-start.9) | collective-permute-done | bytes 524320 | tf_op jit(solution)/shard_map/ppermute | solution.py:146
  117.4 10.3 %collective-permute-start.10 = (f32[8,128,128]{2,1,0:T(8,128)S(1)}, f32[8,128,128]{2,1,0:T(8,128)S(1)}, u32[]{:S(2)}, u32[]{:S(2)}) collective-permute-start(f32[8,128,128]{2,1,0:T(8,128)S(1)} %multiply_add_fusion.15), channel_id=1, source_target_pairs={{0,16},{1,17},{2,18},{3,19},{4,20},{5,21},{6,22},{7,23},{8,24},{9,... | collective-permute-start | bytes 1572872 | tf_op jit(solution)/shard_map/ppermute | solution.py:146
  127.8 1.3 collective-permute-start.14
  129.2 19.6 %collective-permute-done.20 = f32[8,128,128]{2,1,0:T(8,128)S(1)} collective-permute-done((f32[8,128,128]{2,1,0:T(8,128)S(1)}, f32[8,128,128]{2,1,0:T(8,128)S(1)}, u32[]{:S(2)}, u32[]{:S(2)}) %collective-permute-start.20) | collective-permute-done | bytes 524320 | tf_op jit(solution)/shard_map/ppermute | solution.py:146
  149.3 1.1 copy-done.1
  150.4 1.7 fusion.12
  152.1 1.7 collective-permute-start.25
  154.3 1.7 fusion.10
  155.9 0.7 copy.10
  156.6 2.2 %collective-permute-done.15.got_ref = f32[16,128,128]{2,1,0:T(8,128)S(1)} collective-permute-done((f32[16,128,128]{2,1,0:T(8,128)}, f32[16,128,128]{2,1,0:T(8,128)S(1)}, u32[]{:S(2)}, u32[]{:S(2)}) %collective-permute-start.15) | collective-permute-done | bytes 1048608 | tf_op jit(solution)/shard_map/ppermute | solution.py:220
  158.8 1.0 copy-done.5
  159.8 15.3 %shard_map.84 = (bf16[128,4096]{1,0:T(8,128)(2,1)}, bf16[128,4096]{1,0:T(8,128)(2,1)}, bf16[128,4096]{1,0:T(8,128)(2,1)}, bf16[128,4096]{1,0:T(8,128)(2,1)}) custom-call(s32[1]{0:T(128)} %bitcast.core_ref, bf16[128,4096]{1,0:T(8,128)(2,1)} %q_ref, bf16[128,4096]{1,0:T(8,128)(2,1)} %k_ref, bf16[128,4096]{1,0:T(8,128)(2,1)} %v_ref, bf16[128,4096]{1,0:T(8,128)(2,1)} %g_ref, ...), custom_call_target="tpu_custom_call" | custom-call | tf_op jit(solution)/shard_map/pallas_call | solution.py:97
  (78 shorter events, 4.9 us)
Async XLA Ops:
  0.6 7.7 %copy-start.4 = (bf16[128,4096]{1,0:T(8,128)(2,1)S(1)}, bf16[128,4096]{1,0:T(8,128)(2,1)}, u32[]{:S(2)}) copy-start(bf16[128,4096]{1,0:T(8,128)(2,1)} %g_ref) | copy-start | bytes 3145732
  1.5 25.6 %collective-permute-start.1 = (f32[32]{0:T(128)S(1)}, f32[32]{0:T(128)S(1)}, u32[]{:S(2)}, u32[]{:S(2)}) collective-permute-start(f32[32]{0:T(128)S(1)} %convert_reduce_fusion), channel_id=1, source_target_pairs={{0,1},{1,0},{2,3},{3,2},{4,5},{5,4},{6,7},{7,6},{8,9},{9,8},{10,11... | collective-permute-start | bytes 392 | tf_op jit(solution)/shard_map/ppermute | solution.py:175
  4.9 1.2 collective-permute-start
  6.1 14.8 %collective-permute-start.4 = (f32[2,32]{1,0:T(2,128)S(1)}, f32[2,32]{1,0:T(2,128)S(1)}, u32[]{:S(2)}, u32[]{:S(2)}) collective-permute-start(f32[2,32]{1,0:T(2,128)S(1)} %pad_maximum_fusion.4), channel_id=1, source_target_pairs={{0,2},{1,3},{2,4},{3,5},{4,6},{5,7},{6,8},{7,9},{8,10},{9,11},{10,... | collective-permute-start | bytes 776 | tf_op jit(solution)/shard_map/ppermute | solution.py:118
  9.6 1.4 copy-start
  11.0 5.5 %copy-start.2 = (bf16[128,4096]{1,0:T(8,128)(2,1)S(1)}, bf16[128,4096]{1,0:T(8,128)(2,1)}, u32[]{:S(2)}) copy-start(bf16[128,4096]{1,0:T(8,128)(2,1)} %k_ref) | copy-start | bytes 3145732
  12.0 6.1 %copy-start.3 = (bf16[128,4096]{1,0:T(8,128)(2,1)S(1)}, bf16[128,4096]{1,0:T(8,128)(2,1)}, u32[]{:S(2)}) copy-start(bf16[128,4096]{1,0:T(8,128)(2,1)} %v_ref) | copy-start | bytes 3145732
  12.0 23.9 %collective-permute-start.16 = (f32[16,128,128]{2,1,0:T(8,128)}, f32[16,128,128]{2,1,0:T(8,128)}, u32[]{:S(2)}, u32[]{:S(2)}) collective-permute-start(f32[16,128,128]{2,1,0:T(8,128)} %constant_dynamic-slice_fusion.18), channel_id=1, source_target_pairs={{0,1},{1,0},{2,3},{3,2},{4,5},{5,4},{6,7},{7,6},{8,9},{9,8},{10,11... | collective-permute-start | bytes 3145736 | tf_op jit(solution)/shard_map/ppermute | solution.py:175
  20.9 6.1 %collective-permute-start.5 = (f32[4,32]{1,0:T(4,128)S(1)}, f32[4,32]{1,0:T(4,128)S(1)}, u32[]{:S(2)}, u32[]{:S(2)}) collective-permute-start(f32[4,32]{1,0:T(4,128)S(1)} %pad_maximum_fusion.3), channel_id=1, source_target_pairs={{0,4},{1,5},{2,6},{3,7},{4,8},{5,9},{6,10},{7,11},{8,12},{9,13},{1... | collective-permute-start | bytes 1544 | tf_op jit(solution)/shard_map/ppermute | solution.py:118
  22.1 18.3 %collective-permute-start.2 = (f32[16,128,128]{2,1,0:T(8,128)}, f32[16,128,128]{2,1,0:T(8,128)S(1)}, u32[]{:S(2)}, u32[]{:S(2)}) collective-permute-start(f32[16,128,128]{2,1,0:T(8,128)} %constant_dynamic-slice_fusion.19), channel_id=1, source_target_pairs={{0,1},{1,0},{2,3},{3,2},{4,5},{5,4},{6,7},{7,6},{8,9},{9,8},{10,11... | collective-permute-start | bytes 3145736 | tf_op jit(solution)/shard_map/ppermute | solution.py:175
  27.1 3.7 %collective-permute-start.6 = (f32[8,32]{1,0:T(8,128)S(1)}, f32[8,32]{1,0:T(8,128)S(1)}, u32[]{:S(2)}, u32[]{:S(2)}) collective-permute-start(f32[8,32]{1,0:T(8,128)S(1)} %pad_maximum_fusion.2), channel_id=1, source_target_pairs={{0,8},{1,9},{2,10},{3,11},{4,12},{5,13},{6,14},{7,15},{8,16},{9,17... | collective-permute-start | bytes 3080 | tf_op jit(solution)/shard_map/ppermute | solution.py:118
  30.8 4.1 %collective-permute-start.7 = (f32[16,32]{1,0:T(8,128)S(1)}, f32[16,32]{1,0:T(8,128)S(1)}, u32[]{:S(2)}, u32[]{:S(2)}) collective-permute-start(f32[16,32]{1,0:T(8,128)S(1)} %concatenate.28), channel_id=1, source_target_pairs={{0,16},{1,17},{2,18},{3,19},{4,20},{5,21},{6,22},{7,23},{8,24},{9,... | collective-permute-start | bytes 6152 | tf_op jit(solution)/shard_map/ppermute | solution.py:118
  37.8 11.3 %collective-permute-start.17 = (f32[8,128,128]{2,1,0:T(8,128)S(1)}, f32[8,128,128]{2,1,0:T(8,128)S(1)}, u32[]{:S(2)}, u32[]{:S(2)}) collective-permute-start(f32[8,128,128]{2,1,0:T(8,128)S(1)} %get-tuple-element.54), channel_id=1, source_target_pairs={{2,0},{3,1},{4,2},{5,3},{6,4},{7,5},{8,6},{9,7},{10,8},{11,9},{12,... | collective-permute-start | bytes 1572872 | tf_op jit(solution)/shard_map/ppermute | solution.py:146
  39.1 12.5 %collective-permute-start.21 = (f32[8,128,128]{2,1,0:T(8,128)S(1)}, f32[8,128,128]{2,1,0:T(8,128)S(1)}, u32[]{:S(2)}, u32[]{:S(2)}) collective-permute-start(f32[8,128,128]{2,1,0:T(8,128)S(1)} %get-tuple-element.55), channel_id=1, source_target_pairs={{8,0},{9,1},{10,2},{11,3},{12,4},{13,5},{14,6},{15,7},{16,8},{17,9... | collective-permute-start | bytes 1572872 | tf_op jit(solution)/shard_map/ppermute | solution.py:146
  40.7 13.8 %collective-permute-start.3 = (f32[8,128,128]{2,1,0:T(8,128)S(1)}, f32[8,128,128]{2,1,0:T(8,128)S(1)}, u32[]{:S(2)}, u32[]{:S(2)}) collective-permute-start(f32[8,128,128]{2,1,0:T(8,128)S(1)} %get-tuple-element.58), channel_id=1, source_target_pairs={{0,2},{1,3},{2,4},{3,5},{4,6},{5,7},{6,8},{7,9},{8,10},{9,11},{10,... | collective-permute-start | bytes 1572872 | tf_op jit(solution)/shard_map/ppermute | solution.py:146
  44.7 23.5 %collective-permute-start.11 = (f32[8,128,128]{2,1,0:T(8,128)S(1)}, f32[8,128,128]{2,1,0:T(8,128)S(1)}, u32[]{:S(2)}, u32[]{:S(2)}) collective-permute-start(f32[8,128,128]{2,1,0:T(8,128)S(1)} %get-tuple-element.59), channel_id=1, source_target_pairs={{0,8},{1,9},{2,10},{3,11},{4,12},{5,13},{6,14},{7,15},{8,16},{9,17... | collective-permute-start | bytes 1572872 | tf_op jit(solution)/shard_map/ppermute | solution.py:146
  51.8 24.8 %collective-permute-start.18 = (f32[8,128,128]{2,1,0:T(8,128)S(1)}, f32[8,128,128]{2,1,0:T(8,128)S(1)}, u32[]{:S(2)}, u32[]{:S(2)}) collective-permute-start(f32[8,128,128]{2,1,0:T(8,128)S(1)} %get-tuple-element.52), channel_id=1, source_target_pairs={{4,0},{5,1},{6,2},{7,3},{8,4},{9,5},{10,6},{11,7},{12,8},{13,9},{1... | collective-permute-start | bytes 1572872 | tf_op jit(solution)/shard_map/ppermute | solution.py:146
  53.2 41.4 %collective-permute-start.22 = (f32[8,128,128]{2,1,0:T(8,128)S(1)}, f32[8,128,128]{2,1,0:T(8,128)S(1)}, u32[]{:S(2)}, u32[]{:S(2)}) collective-permute-start(f32[8,128,128]{2,1,0:T(8,128)S(1)} %get-tuple-element.53), channel_id=1, source_target_pairs={{16,0},{17,1},{18,2},{19,3},{20,4},{21,5},{22,6},{23,7},{24,8},{25... | collective-permute-start | bytes 1572872 | tf_op jit(solution)/shard_map/ppermute | solution.py:146
  68.4 27.6 %collective-permute-start.8 = (f32[8,128,128]{2,1,0:T(8,128)S(1)}, f32[8,128,128]{2,1,0:T(8,128)S(1)}, u32[]{:S(2)}, u32[]{:S(2)}) collective-permute-start(f32[8,128,128]{2,1,0:T(8,128)S(1)} %get-tuple-element.56), channel_id=1, source_target_pairs={{0,4},{1,5},{2,6},{3,7},{4,8},{5,9},{6,10},{7,11},{8,12},{9,13},{1... | collective-permute-start | bytes 1572872 | tf_op jit(solution)/shard_map/ppermute | solution.py:146
  69.8 28.5 %collective-permute-start.12 = (f32[8,128,128]{2,1,0:T(8,128)S(1)}, f32[8,128,128]{2,1,0:T(8,128)S(1)}, u32[]{:S(2)}, u32[]{:S(2)}) collective-permute-start(f32[8,128,128]{2,1,0:T(8,128)S(1)} %get-tuple-element.57), channel_id=1, source_target_pairs={{0,16},{1,17},{2,18},{3,19},{4,20},{5,21},{6,22},{7,23},{8,24},{9,... | collective-permute-start | bytes 1572872 | tf_op jit(solution)/shard_map/ppermute | solution.py:146
  76.7 25.9 %collective-permute-start.19 = (f32[8,128,128]{2,1,0:T(8,128)S(1)}, f32[8,128,128]{2,1,0:T(8,128)S(1)}, u32[]{:S(2)}, u32[]{:S(2)}) collective-permute-start(f32[8,128,128]{2,1,0:T(8,128)S(1)} %multiply_add_fusion.8), channel_id=1, source_target_pairs={{8,0},{9,1},{10,2},{11,3},{12,4},{13,5},{14,6},{15,7},{16,8},{17,9... | collective-permute-start | bytes 1572872 | tf_op jit(solution)/shard_map/ppermute | solution.py:146
  94.8 14.9 %collective-permute-start.23 = (f32[8,128,128]{2,1,0:T(8,128)S(1)}, f32[8,128,128]{2,1,0:T(8,128)S(1)}, u32[]{:S(2)}, u32[]{:S(2)}) collective-permute-start(f32[8,128,128]{2,1,0:T(8,128)S(1)} %multiply_add_fusion.4), channel_id=1, source_target_pairs={{2,0},{3,1},{4,2},{5,3},{6,4},{7,5},{8,6},{9,7},{10,8},{11,9},{12,... | collective-permute-start | bytes 1572872 | tf_op jit(solution)/shard_map/ppermute | solution.py:146
  96.2 21.0 %collective-permute-start.9 = (f32[8,128,128]{2,1,0:T(8,128)S(1)}, f32[8,128,128]{2,1,0:T(8,128)S(1)}, u32[]{:S(2)}, u32[]{:S(2)}) collective-permute-start(f32[8,128,128]{2,1,0:T(8,128)S(1)} %multiply_add_fusion.16), channel_id=1, source_target_pairs={{0,8},{1,9},{2,10},{3,11},{4,12},{5,13},{6,14},{7,15},{8,16},{9,17... | collective-permute-start | bytes 1572872 | tf_op jit(solution)/shard_map/ppermute | solution.py:146
  98.4 29.3 %collective-permute-start.13 = (f32[8,128,128]{2,1,0:T(8,128)S(1)}, f32[8,128,128]{2,1,0:T(8,128)S(1)}, u32[]{:S(2)}, u32[]{:S(2)}) collective-permute-start(f32[8,128,128]{2,1,0:T(8,128)S(1)} %multiply_add_fusion.12), channel_id=1, source_target_pairs={{0,2},{1,3},{2,4},{3,5},{4,6},{5,7},{6,8},{7,9},{8,10},{9,11},{10,... | collective-permute-start | bytes 1572872 | tf_op jit(solution)/shard_map/ppermute | solution.py:146
  102.7 46.1 %collective-permute-start.20 = (f32[8,128,128]{2,1,0:T(8,128)S(1)}, f32[8,128,128]{2,1,0:T(8,128)S(1)}, u32[]{:S(2)}, u32[]{:S(2)}) collective-permute-start(f32[8,128,128]{2,1,0:T(8,128)S(1)} %multiply_add_fusion.7), channel_id=1, source_target_pairs={{16,0},{17,1},{18,2},{19,3},{20,4},{21,5},{22,6},{23,7},{24,8},{25... | collective-permute-start | bytes 1572872 | tf_op jit(solution)/shard_map/ppermute | solution.py:146
  109.8 39.3 %collective-permute-start.24 = (f32[8,128,128]{2,1,0:T(8,128)S(1)}, f32[8,128,128]{2,1,0:T(8,128)S(1)}, u32[]{:S(2)}, u32[]{:S(2)}) collective-permute-start(f32[8,128,128]{2,1,0:T(8,128)S(1)} %multiply_add_fusion.3), channel_id=1, source_target_pairs={{4,0},{5,1},{6,2},{7,3},{8,4},{9,5},{10,6},{11,7},{12,8},{13,9},{1... | collective-permute-start | bytes 1572872 | tf_op jit(solution)/shard_map/ppermute | solution.py:146
  117.4 36.4 %collective-permute-start.10 = (f32[8,128,128]{2,1,0:T(8,128)S(1)}, f32[8,128,128]{2,1,0:T(8,128)S(1)}, u32[]{:S(2)}, u32[]{:S(2)}) collective-permute-start(f32[8,128,128]{2,1,0:T(8,128)S(1)} %multiply_add_fusion.15), channel_id=1, source_target_pairs={{0,16},{1,17},{2,18},{3,19},{4,20},{5,21},{6,22},{7,23},{8,24},{9,... | collective-permute-start | bytes 1572872 | tf_op jit(solution)/shard_map/ppermute | solution.py:146
  127.8 26.2 %collective-permute-start.14 = (f32[8,128,128]{2,1,0:T(8,128)S(1)}, f32[8,128,128]{2,1,0:T(8,128)S(1)}, u32[]{:S(2)}, u32[]{:S(2)}) collective-permute-start(f32[8,128,128]{2,1,0:T(8,128)S(1)} %multiply_add_fusion.11), channel_id=1, source_target_pairs={{0,4},{1,5},{2,6},{3,7},{4,8},{5,9},{6,10},{7,11},{8,12},{9,13},{1... | collective-permute-start | bytes 1572872 | tf_op jit(solution)/shard_map/ppermute | solution.py:146
  148.8 1.6 copy-start.1
  152.1 4.5 %collective-permute-start.25 = (f32[16,128,128]{2,1,0:T(8,128)}, f32[16,128,128]{2,1,0:T(8,128)}, u32[]{:S(2)}, u32[]{:S(2)}) collective-permute-start(f32[16,128,128]{2,1,0:T(8,128)} %get-tuple-element.48), channel_id=1, source_target_pairs={{0,1},{1,0},{2,3},{3,2},{4,5},{5,4},{6,7},{7,6},{8,9},{9,8},{10,11... | collective-permute-start | bytes 3145736 | tf_op jit(solution)/shard_map/ppermute | solution.py:220
  155.9 2.9 %collective-permute-start.15 = (f32[16,128,128]{2,1,0:T(8,128)}, f32[16,128,128]{2,1,0:T(8,128)S(1)}, u32[]{:S(2)}, u32[]{:S(2)}) collective-permute-start(f32[16,128,128]{2,1,0:T(8,128)} %get-tuple-element.50), channel_id=1, source_target_pairs={{0,1},{1,0},{2,3},{3,2},{4,5},{5,4},{6,7},{7,6},{8,9},{9,8},{10,11... | collective-permute-start | bytes 3145736 | tf_op jit(solution)/shard_map/ppermute | solution.py:220
  158.8 1.0 copy-start.5
